TPU v7x, 256 devices: a whole 4x4x8 slice. The times are simulated.
256 devices in a mesh: cells: 64 (over y, z, core), freq: 4 (over x).
Axes of the slice: x: 4, y: 4, z: 8, core: 2. Of those that a mesh axis runs over, the one named last changes fastest.
Arguments:
- adj_source: float32 [4, 2, 262144], P('freq', None, 'cells'), may hold values from -6 to 6
- contrast: float32 [4, 262144], P('freq', 'cells'), may hold values from 0.2 to 0.8
- background: float32 [4, 2, 262144], P('freq', None, 'cells'), may hold values from -6 to 6
- near_blocks: float32 [4, 2, 192, 262144], P('freq', None, None, 'cells'), may hold values from -0.3125 to 0.3125
- near_list: int32 [4096, 3], P('cells'), may hold values from 0 to 4095, as said below
- proj_basis: float32 [4, 2, 16, 262144], P('freq', None, None, 'cells'), may hold values from -0.5 to 0.5
- expand_basis: float32 [4, 2, 16, 262144], P('freq', None, None, 'cells'), may hold values from -1 to 1
- coupling: float32 [4, 2, 16, 16, 65536], P('freq', None, None, None, 'cells'), may hold values from -0.25 to 0.25
- far_owner: int32 [65536, 1], P('cells'), may hold values from 0 to 63; in each aligned block of 1024 rows (0 to 1023, 1024 to 2047, ...) at most 32 rows name the same one
- far_slot: int32 [65536], P('cells'), may hold values from 0 to 63
Outputs:
- adjoint: float32 [4, 2, 262144], P('freq', None, 'cells')
- gradient: float32 [262144], P('cells')
Inputs may be any that keep to these rules, and one draw needn't show every extreme that they name: near_list[c, 0] = c, and every partner of c lies on the same device: near_list[c, k] // 64 == c // 64. `far_owner`: among the far pairs of one device's targets (aligned blocks of 1024 rows) at most 32 have sources on any one device.
All inputs are finite; a program needn't handle non-finite values.
Results may differ from a plain program's by a relative error of at most 0.0001.
Values sent between devices are 32-bit elements; how exact they have to be, the bound alone decides.
No kernel may reach another device: no remote copies, remote signals or barrier semaphores. Data moves between devices by JAX's collectives and lax.ppermute only.
A program may use at most 64 MiB of HBM per device.

v0:
```python
import jax
import jax.numpy as jnp
from jax import lax
from jax.experimental import pallas as pl
from jax.experimental.pallas import tpu as pltpu
from jax.sharding import PartitionSpec as P

ITERS = 2
F32 = jnp.float32
BF16 = jnp.bfloat16
CHUNK = 512
PAIR_CHUNK = 128
VMEM_LIMIT = 56 * 1024 * 1024


def _split3(a):
    hi = a.astype(BF16)
    r = a - hi.astype(F32)
    mid = r.astype(BF16)
    lo = (r - mid.astype(F32)).astype(BF16)
    return jnp.concatenate([hi, mid, lo], axis=0)


def _sdot(split, onehot):
    m = split.shape[0] // 3
    r = jnp.dot(split, onehot, preferred_element_type=F32)
    return r[:m] + r[m : 2 * m] + r[2 * m :]


def _xdot(a, onehot):
    return _sdot(_split3(a), onehot)


def _iota(shape, dim):
    return lax.broadcasted_iota(jnp.int32, shape, dim)


def _weighted_proj(u, c, pre, pim):
    wre = u[0:1] * c
    wim = u[1:2] * c
    return jnp.concatenate([pre * wre - pim * wim, pre * wim + pim * wre], axis=0)


def _proj_chunk(pw, off, clusters, width):
    n = pw.shape[1]
    seg = ((_iota((n, clusters), 0) + off) // width) == _iota((n, clusters), 1)
    return _xdot(pw, seg.astype(BF16))


def _send_of(q, rr_ref, clusters):
    nsend = rr_ref.shape[1]
    oh = (_iota((clusters, nsend), 0) == rr_ref[...]).astype(BF16)
    return _xdot(q, oh)


def _proj_kernel(u_ref, c_ref, p_ref, rr_ref, send_ref):
    cells = u_ref.shape[1]
    clusters = cells // 64
    rank2 = 2 * p_ref.shape[1]

    def body(ci, q):
        off = pl.multiple_of(ci * CHUNK, CHUNK)
        sl = pl.ds(off, CHUNK)
        pw = _weighted_proj(u_ref[:, sl], c_ref[:, sl], p_ref[0, :, sl], p_ref[1, :, sl])
        return q + _proj_chunk(pw, off, clusters, 64)

    q = lax.fori_loop(0, cells // CHUNK, body, jnp.zeros((rank2, clusters), F32))
    send_ref[...] = _send_of(q, rr_ref, clusters)


def _near_kernel(u_ref, c_ref, nb_ref, nlc_ref, base_ref, out_ref):
    cells = u_ref.shape[1]
    width = 64
    clusters = cells // width
    near = nlc_ref.shape[0]

    def wt_body(ci, acc):
        off = pl.multiple_of(ci * CHUNK, CHUNK)
        sl = pl.ds(off, CHUNK)
        w = u_ref[:, sl] * c_ref[:, sl]
        sel = _iota((width, CHUNK), 0) == ((_iota((width, CHUNK), 1) + off) % width)
        wm = jnp.concatenate(
            [jnp.where(sel, w[0:1], 0.0), jnp.where(sel, w[1:2], 0.0)], axis=0
        )
        seg = ((_iota((CHUNK, clusters), 0) + off) // width) == _iota((CHUNK, clusters), 1)
        return acc + _xdot(wm, seg.astype(BF16))

    wt = lax.fori_loop(0, cells // CHUNK, wt_body, jnp.zeros((2 * width, clusters), F32))
    wt_split = _split3(wt)

    def near_body(ci, carry):
        off = pl.multiple_of(ci * CHUNK, CHUNK)
        sl = pl.ds(off, CHUNK)
        crow = _iota((clusters, CHUNK), 0)
        acc_re = jnp.zeros((1, CHUNK), F32)
        acc_im = jnp.zeros((1, CHUNK), F32)
        for k in range(near):
            m = (crow == nlc_ref[k : k + 1, sl]).astype(BF16)
            wk = _sdot(wt_split, m)
            wre = wk[:width]
            wim = wk[width:]
            nre = nb_ref[0, pl.ds(k * width, width), sl]
            nim = nb_ref[1, pl.ds(k * width, width), sl]
            acc_re = acc_re + jnp.sum(nre * wre - nim * wim, axis=0, keepdims=True)
            acc_im = acc_im + jnp.sum(nre * wim + nim * wre, axis=0, keepdims=True)
        out_ref[:, sl] = base_ref[:, sl] + jnp.concatenate([acc_re, acc_im], axis=0)
        return carry

    lax.fori_loop(0, cells // CHUNK, near_body, 0)


def _far_common(part_ref, recv_ref, idx_ref, cpl_ref, e_ref, u_ref, chunk_tail):
    cells = part_ref.shape[1]
    width = 64
    clusters = cells // width
    rank = cpl_ref.shape[1]
    npairs = idx_ref.shape[1]
    far = npairs // clusters
    nrecv = recv_ref.shape[1]
    rsplit = _split3(recv_ref[...])

    def pair_body(pj, z):
        off = pl.multiple_of(pj * PAIR_CHUNK, PAIR_CHUNK)
        sl = pl.ds(off, PAIR_CHUNK)
        g = (_iota((nrecv, PAIR_CHUNK), 0) == idx_ref[:, sl]).astype(BF16)
        qs = _sdot(rsplit, g)
        qre = qs[:rank][None]
        qim = qs[rank:][None]
        cre = cpl_ref[0, :, :, sl]
        cim = cpl_ref[1, :, :, sl]
        zre = jnp.sum(cre * qre - cim * qim, axis=1)
        zim = jnp.sum(cre * qim + cim * qre, axis=1)
        seg = ((_iota((PAIR_CHUNK, clusters), 0) + off) // far) == _iota((PAIR_CHUNK, clusters), 1)
        return z + _xdot(jnp.concatenate([zre, zim], axis=0), seg.astype(BF16))

    z = lax.fori_loop(0, npairs // PAIR_CHUNK, pair_body, jnp.zeros((2 * rank, clusters), F32))
    z_split = _split3(z)

    def cell_body(ci, acc):
        off = pl.multiple_of(ci * CHUNK, CHUNK)
        sl = pl.ds(off, CHUNK)
        spread = _iota((clusters, CHUNK), 0) == ((_iota((clusters, CHUNK), 1) + off) // width)
        zz = _sdot(z_split, spread.astype(BF16))
        zre = zz[:rank]
        zim = zz[rank:]
        ere = e_ref[0, :, sl]
        eim = e_ref[1, :, sl]
        far_re = jnp.sum(ere * zre - eim * zim, axis=0, keepdims=True)
        far_im = jnp.sum(ere * zim + eim * zre, axis=0, keepdims=True)
        u = part_ref[:, sl] + jnp.concatenate([far_re, far_im], axis=0)
        u_ref[:, sl] = u
        return chunk_tail(u, off, sl, acc)

    return cell_body


def _far_proj_kernel(part_ref, recv_ref, idx_ref, cpl_ref, e_ref, c_ref, p_ref, rr_ref, u_ref, send_ref):
    cells = part_ref.shape[1]
    clusters = cells // 64
    rank2 = 2 * p_ref.shape[1]

    def tail(u, off, sl, q):
        pw = _weighted_proj(u, c_ref[:, sl], p_ref[0, :, sl], p_ref[1, :, sl])
        return q + _proj_chunk(pw, off, clusters, 64)

    body = _far_common(part_ref, recv_ref, idx_ref, cpl_ref, e_ref, u_ref, tail)
    q = lax.fori_loop(0, cells // CHUNK, body, jnp.zeros((rank2, clusters), F32))
    send_ref[...] = _send_of(q, rr_ref, clusters)


def _far_grad_kernel(part_ref, recv_ref, idx_ref, cpl_ref, e_ref, bg_ref, u_ref, t_ref):
    cells = part_ref.shape[1]

    def tail(u, off, sl, acc):
        bg = bg_ref[:, sl]
        t_ref[:, sl] = bg[0:1] * u[0:1] + bg[1:2] * u[1:2]
        return acc

    body = _far_common(part_ref, recv_ref, idx_ref, cpl_ref, e_ref, u_ref, tail)
    lax.fori_loop(0, cells // CHUNK, body, 0)


def _call(kernel, outs, args, flops, name):
    leaves = outs if isinstance(outs, tuple) else (outs,)
    nbytes = sum(a.size * a.dtype.itemsize for a in args) + sum(
        o.size * jnp.dtype(o.dtype).itemsize for o in leaves
    )
    return pl.pallas_call(
        kernel,
        out_shape=outs,
        compiler_params=pltpu.CompilerParams(vmem_limit_bytes=VMEM_LIMIT),
        cost_estimate=pl.CostEstimate(flops=flops, bytes_accessed=nbytes, transcendentals=0),
        name=name,
    )(*args)


def _exchange(send, devices):
    rows, total = send.shape
    slots = total // devices
    got = lax.all_to_all(send.reshape(rows, devices, slots), "cells", 1, 1, tiled=True)
    return got.reshape(rows, total)


def per_device(
    adj_source,
    contrast,
    background,
    near_blocks,
    near_list,
    proj_basis,
    expand_basis,
    coupling,
    far_owner,
    far_slot,
):
    devices = lax.axis_size("cells")
    clusters = near_list.shape[0]
    cells = contrast.shape[1]
    width = cells // clusters
    npairs = far_slot.shape[0]
    cap = 32

    src = adj_source[0]
    cst = contrast
    nb = near_blocks[0]
    pb = proj_basis[0]
    eb = expand_basis[0]
    cp = coupling[0]
    bg = background[0]

    me = lax.axis_index("cells")
    local_list = near_list - me * clusters
    nlc = jnp.repeat(local_list.T, width, axis=1)

    owner = far_owner[:, 0]
    slot = far_slot
    onehot = (owner[:, None] == jnp.arange(devices, dtype=jnp.int32)[None, :]).astype(jnp.int32)
    before = jnp.cumsum(onehot, axis=0) - onehot
    pos = jnp.sum(before * onehot, axis=1)
    idx = (owner * cap + pos)[None, :].astype(jnp.int32)
    req = jnp.zeros((devices, cap), jnp.int32).at[owner, pos].set(slot)
    rr = lax.all_to_all(req, "cells", 0, 0, tiled=True).reshape(1, devices * cap)

    nsend = devices * cap
    rank2 = 2 * pb.shape[1]
    send_shape = jax.ShapeDtypeStruct((rank2, nsend), F32)
    field_shape = jax.ShapeDtypeStruct((2, cells), F32)

    send = _call(_proj_kernel, send_shape, (src, cst, pb, rr), 4 * rank2 * cells, "proj")
    field = src
    for step in range(ITERS):
        recv = _exchange(send, devices)
        part = _call(
            _near_kernel, field_shape, (field, cst, nb, nlc, src), 8 * nb.shape[1] * cells, "near"
        )
        if step < ITERS - 1:
            field, send = _call(
                _far_proj_kernel,
                (field_shape, send_shape),
                (part, recv, idx, cp, eb, cst, pb, rr),
                8 * cp.size,
                "far_proj",
            )
        else:
            field, terms = _call(
                _far_grad_kernel,
                (field_shape, jax.ShapeDtypeStruct((1, cells), F32)),
                (part, recv, idx, cp, eb, bg),
                8 * cp.size,
                "far_grad",
            )
    freqs = lax.axis_size("freq")
    total = terms[0]
    hop = 1
    while hop < freqs:
        total = total + lax.ppermute(total, "freq", [(i, i ^ hop) for i in range(freqs)])
        hop *= 2
    return (field[None], total)


def solution(mesh):
    return jax.shard_map(
        per_device,
        mesh=mesh,
        in_specs=(
            P("freq", None, "cells"),
            P("freq", "cells"),
            P("freq", None, "cells"),
            P("freq", None, None, "cells"),
            P("cells", None),
            P("freq", None, None, "cells"),
            P("freq", None, None, "cells"),
            P("freq", None, None, None, "cells"),
            P("cells", None),
            P("cells"),
        ),
        out_specs=(P("freq", None, "cells"), P("cells")),
        check_vma=False,
    )
```

profile of v0, /device:TPU:8, one launch (start us, length us, event | category | flops | bytes accessed | tf_op | source)
XLA Modules:
  0.0 136.3 jit_solution(3989010937347783463)
XLA Ops:
  0.6 0.0 copy-start.1
  0.6 0.7 fusion.3
  1.4 18.0 %reduce-window.6 = s32[64,8,128]{2,1,0:T(8,128)S(1)} reduce-window(s32[64,8,128]{2,1,0:T(8,128)S(1)} %fusion.3, s32[]{:T(128)} %constant.8.clone.1), window={size=1x1x128 pad=0_0x0_0x127_0}, to_apply=%region_0.0 | reduce-window | flops 8323072 | bytes 524292 | tf_op jit(solution)/shard_map/reduce-window
  19.4 0.1 slice.8
  19.5 0.1 copy.15
  19.7 0.1 copy.16
  19.8 0.1 broadcast_add_fusion
  19.9 0.8 fusion.2
  20.7 0.7 compare_select_fusion
  21.4 0.7 multiply_reduce_fusion
  22.1 0.8 and_reduce_fusion
  22.9 4.5 %scatter_custom_fusion = s32[2048]{0:T(1024)S(1)} fusion(s32[1024]{0:T(1024)S(1)} %broadcast_select_fusion, s32[1024]{0:T(1024)} %param.19, s32[]{:T(128)} %constant.8.clone.1), kind=kCustom, calls=%fused_computation.15 | custom fusion | bytes 8704
  27.4 0.1 reshape.82
  27.4 0.1 copy.17
  27.5 20.5 %all_to_all.19 = s32[64,1,32]{2,1,0:T(1,128)S(1)} all-to-all(s32[64,1,32]{2,1,0:T(1,128)S(1)} %copy.17), channel_id=1, replica_groups=mesh['cells'=64,'freq'=4] {'cells'}, dimensions={0} | all-to-all | bytes 16384 | tf_op jit(solution)/shard_map/all_to_all | solution.py:242
  48.0 0.5 broadcast.73
  48.6 0.7 reduce.7
  49.3 0.7 reshape.75.rr_ref
  50.0 0.0 copy-start
  50.0 4.8 %proj.1 = f32[32,2048]{1,0:T(8,128)} custom-call(f32[2,4096]{1,0:T(2,128)} %bitcast.58, f32[1,4096]{1,0:T(1,128)} %c_ref.7, f32[2,16,4096]{2,1,0:T(8,128)} %bitcast.53, s32[1,2048]{1,0:T(1,128)} %reshape.75.rr_ref), custom_call_target="tpu_custom_call" | custom-call | flops 524288 | bytes 843776 | tf_op jit(solution)/shard_map/proj/pallas_call | solution.py:188
  54.8 1.3 reshape.76
  56.0 0.6 copy.27
  56.7 1.1 reshape.101
  57.8 5.5 %all-to-all-start.1 = ((f32[64,1,1024]{2,1,0:T(1,128)}), f32[64,1,1024]{2,1,0:T(1,128)S(1)}, u32[]{:S(2)}, u32[]{:S(2)}) async-start(f32[64,1,1024]{2,1,0:T(1,128)} %reshape.101), calls=%async_computation.1 | async-start | bytes 524288 | tf_op jit(solution)/shard_map/all_to_all | solution.py:200
  63.3 0.0 copy-done.1
  63.4 0.1 broadcast_in_dim.6
  63.4 0.7 reshape.73.nlc_ref
  64.2 10.8 %near.2.part_ref = f32[2,4096]{1,0:T(2,128)} custom-call(f32[2,4096]{1,0:T(2,128)} %bitcast.59, f32[1,4096]{1,0:T(1,128)} %c_ref.7, f32[2,192,4096]{2,1,0:T(8,128)} %bitcast.45, s32[3,4096]{1,0:T(4,128)} %reshape.73.nlc_ref, f32[2,4096]{1,0:T(2,128)} %bitcast.60), custom_call_target="tpu_custom_call" | custom-call | flops 6291456 | bytes 6455296 | tf_op jit(solution)/shard_map/near/pallas_call | solution.py:188
  75.0 0.0 copy-done
  75.0 0.6 bitcast_add_fusion.idx_ref
  75.6 0.0 all-to-all-done.1
  75.6 0.5 broadcast.74
  76.1 1.2 reduce.8
  77.3 0.3 reshape.102
  77.6 0.6 copy.19
  78.3 1.2 reshape.77.recv_ref
  79.4 10.3 %far_proj.1 = (f32[2,4096]{1,0:T(2,128)}, f32[32,2048]{1,0:T(8,128)}) custom-call(f32[2,4096]{1,0:T(2,128)} %near.2.part_ref, f32[32,2048]{1,0:T(8,128)} %reshape.77.recv_ref, s32[1,1024]{1,0:T(1,128)} %bitcast_add_fusion.idx_ref, f32[2,16,16,1024]{3,2,1,0:T(8,128)} %bitcast.47, f32[2,16,4096]{2,1,0:T(8,128)} %bitcast.55, f32[1,4096]{1,0:T(1,128)} %c_ref.7, ...), custom_call_target="tpu_custom_call" | custom-call | flops 4194304 | bytes 3764224 | tf_op jit(solution)/shard_map/far_proj/pallas_call | solution.py:188
  89.8 1.3 reshape.78
  91.1 0.6 copy.26
  91.7 1.1 reshape.103
  92.8 10.3 %all-to-all-start.2 = ((f32[64,1,1024]{2,1,0:T(1,128)}), f32[64,1,1024]{2,1,0:T(1,128)S(1)}, u32[]{:S(2)}, u32[]{:S(2)}) async-start(f32[64,1,1024]{2,1,0:T(1,128)} %reshape.103), calls=%async_computation.2 | async-start | bytes 524288 | tf_op jit(solution)/shard_map/all_to_all | solution.py:200
  103.2 10.8 %near.3.part_ref = f32[2,4096]{1,0:T(2,128)} custom-call(f32[2,4096]{1,0:T(2,128)} %get-tuple-element.6.u_ref, f32[1,4096]{1,0:T(1,128)} %c_ref.7, f32[2,192,4096]{2,1,0:T(8,128)} %bitcast.46, s32[3,4096]{1,0:T(4,128)} %reshape.73.nlc_ref, f32[2,4096]{1,0:T(2,128)} %bitcast.61), custom_call_target="tpu_custom_call" | custom-call | flops 6291456 | bytes 6455296 | tf_op jit(solution)/shard_map/near/pallas_call | solution.py:188
  114.0 0.7 all-to-all-done.2
  114.7 1.2 reduce.9
  115.9 0.3 reshape.104
  116.2 0.6 copy.21
  116.8 1.2 reshape.79.recv_ref
  118.0 7.7 %far_grad.1 = (f32[2,4096]{1,0:T(2,128)}, f32[1,4096]{1,0:T(1,128)}) custom-call(f32[2,4096]{1,0:T(2,128)} %near.3.part_ref, f32[32,2048]{1,0:T(8,128)} %reshape.79.recv_ref, s32[1,1024]{1,0:T(1,128)} %bitcast_add_fusion.idx_ref, f32[2,16,16,1024]{3,2,1,0:T(8,128)} %bitcast.48, f32[2,16,4096]{2,1,0:T(8,128)} %bitcast.56, f32[2,4096]{1,0:T(2,128)} %bitcast.67), custom_call_target="tpu_custom_call" | custom-call | flops 4194304 | bytes 3002368 | tf_op jit(solution)/shard_map/far_grad/pallas_call | solution.py:188
  125.7 1.5 %collective-permute-start = (f32[4096]{0:T(1024)}, f32[4096]{0:T(1024)S(1)}, u32[]{:S(2)}, u32[]{:S(2)}) collective-permute-start(f32[4096]{0:T(1024)} %bitcast.69), channel_id=1, source_target_pairs={{0,1},{1,0},{2,3},{3,2},{4,5},{5,4},{6,7},{7,6},{8,9},{9,8},{10,11... | collective-permute-start | bytes 49160 | tf_op jit(solution)/shard_map/ppermute | solution.py:276
  127.3 2.4 %collective-permute-done = f32[4096]{0:T(1024)S(1)} collective-permute-done((f32[4096]{0:T(1024)}, f32[4096]{0:T(1024)S(1)}, u32[]{:S(2)}, u32[]{:S(2)}) %collective-permute-start) | collective-permute-done | bytes 16416 | tf_op jit(solution)/shard_map/ppermute | solution.py:276
  129.7 0.7 add.37
  130.4 3.0 %collective-permute-start.1 = (f32[4096]{0:T(1024)S(1)}, f32[4096]{0:T(1024)S(1)}, u32[]{:S(2)}, u32[]{:S(2)}) collective-permute-start(f32[4096]{0:T(1024)S(1)} %add.37), channel_id=1, source_target_pairs={{0,2},{1,3},{2,0},{3,1},{4,6},{5,7},{6,4},{7,5},{8,10},{9,11},{10,... | collective-permute-start | bytes 49160 | tf_op jit(solution)/shard_map/ppermute | solution.py:276
  133.5 2.2 %collective-permute-done.1 = f32[4096]{0:T(1024)S(1)} collective-permute-done((f32[4096]{0:T(1024)S(1)}, f32[4096]{0:T(1024)S(1)}, u32[]{:S(2)}, u32[]{:S(2)}) %collective-permute-start.1) | collective-permute-done | bytes 16416 | tf_op jit(solution)/shard_map/ppermute | solution.py:276
  135.7 0.6 add.38
  (4 shorter events, 0.0 us)
Async XLA Ops:
  0.6 62.7 %copy-start.1 = (s32[64,3]{0,1:T(4,128)S(1)}, s32[64,3]{0,1:T(4,128)}, u32[]{:S(2)}) copy-start(s32[64,3]{0,1:T(4,128)} %param.14) | copy-start | bytes 2308
  50.0 25.0 %copy-start = (s32[1024,1]{0,1:T(1,128)S(1)}, s32[1024,1]{0,1:T(1,128)}, u32[]{:S(2)}) copy-start(s32[1024,1]{0,1:T(1,128)} %param.18) | copy-start | bytes 12292
  57.8 17.8 %all-to-all-start.1 = ((f32[64,1,1024]{2,1,0:T(1,128)}), f32[64,1,1024]{2,1,0:T(1,128)S(1)}, u32[]{:S(2)}, u32[]{:S(2)}) async-start(f32[64,1,1024]{2,1,0:T(1,128)} %reshape.101), calls=%async_computation.1 | async-start | bytes 524288 | tf_op jit(solution)/shard_map/all_to_all | solution.py:200
  92.8 21.9 %all-to-all-start.2 = ((f32[64,1,1024]{2,1,0:T(1,128)}), f32[64,1,1024]{2,1,0:T(1,128)S(1)}, u32[]{:S(2)}, u32[]{:S(2)}) async-start(f32[64,1,1024]{2,1,0:T(1,128)} %reshape.103), calls=%async_computation.2 | async-start | bytes 524288 | tf_op jit(solution)/shard_map/all_to_all | solution.py:200
  125.7 3.9 %collective-permute-start = (f32[4096]{0:T(1024)}, f32[4096]{0:T(1024)S(1)}, u32[]{:S(2)}, u32[]{:S(2)}) collective-permute-start(f32[4096]{0:T(1024)} %bitcast.69), channel_id=1, source_target_pairs={{0,1},{1,0},{2,3},{3,2},{4,5},{5,4},{6,7},{7,6},{8,9},{9,8},{10,11... | collective-permute-start | bytes 49160 | tf_op jit(solution)/shard_map/ppermute | solution.py:276
  130.4 5.2 %collective-permute-start.1 = (f32[4096]{0:T(1024)S(1)}, f32[4096]{0:T(1024)S(1)}, u32[]{:S(2)}, u32[]{:S(2)}) collective-permute-start(f32[4096]{0:T(1024)S(1)} %add.37), channel_id=1, source_target_pairs={{0,2},{1,3},{2,0},{3,1},{4,6},{5,7},{6,4},{7,5},{8,10},{9,11},{10,... | collective-permute-start | bytes 49160 | tf_op jit(solution)/shard_map/ppermute | solution.py:276
where the time goes:
time: 137 us; the launch traced here: 136 us
  Pallas kernels  44.5 us (32%)
  other arithmetic  26.8 us (20%)
  blocking collectives  20.5 us (15%)
  starting transfers between devices  20.4 us (15%)
  local copies, waits for them, and re-layouts  17.9 us (13%)
  waiting for transfers between devices  5.32 us (4%)
    pallas_call x5, Pallas kernels, _call(): pl.pallas_call(kernel, out_shape=outs, compiler_params=pltpu.CompilerPara...  44.5 us
    all_to_all x1, blocking collectives, per_device(): lax.all_to_all(req, 'cells', 0, 0, tiled=True).reshape(1, devices * cap)  20.5 us
    another operation x3, other arithmetic  18.2 us
    all_to_all x2, starting transfers between devices, _exchange(): lax.all_to_all(send.reshape(rows, devices, slots), 'cells', 1, 1, tiled=T...  15.8 us
    unnamed x10, local copies, waits for them, and re-layouts  7.52 us
    ppermute x2, waiting for transfers between devices, per_device(): lax.ppermute(total, 'freq', [(i, i ^ hop) for i in range(freqs)])  4.63 us
    ppermute x2, starting transfers between devices, per_device(): lax.ppermute(total, 'freq', [(i, i ^ hop) for i in range(freqs)])  4.56 us
    reshape x4, local copies, waits for them, and re-layouts, _exchange(): send.reshape(rows, devices, slots)  3.8 us
  transfers between devices with their start and end apart: 4, of which 3 were waited for; matrix products, arithmetic and copies ran while one was open for 1% of the time, Pallas kernels for 16%

commit v1 on v0

--- a/solution.py
+++ b/solution.py
@@ -49,7 +49,7 @@
 
 def _send_of(q, rr_ref, clusters):
     nsend = rr_ref.shape[1]
-    oh = (_iota((clusters, nsend), 0) == rr_ref[...]).astype(BF16)
+    oh = (_iota((clusters, nsend), 0).astype(F32) == rr_ref[...]).astype(BF16)
     return _xdot(q, oh)
 
 
@@ -178,6 +178,21 @@
 
     body = _far_common(part_ref, recv_ref, idx_ref, cpl_ref, e_ref, u_ref, tail)
     lax.fori_loop(0, cells // CHUNK, body, 0)
+
+
+def _prep_kernel(or_ref, sr_ref, idx_ref, req_ref):
+    n = or_ref.shape[1]
+    devices, cap = req_ref.shape
+    oht = _iota((devices, n), 0) == or_ref[...]
+    upper = (_iota((n, n), 0) < _iota((n, n), 1)).astype(BF16)
+    counts = jnp.dot(oht.astype(BF16), upper, preferred_element_type=F32)
+    pos = jnp.sum(jnp.where(oht, counts, 0.0), axis=0, keepdims=True).astype(jnp.int32)
+    idx_ref[...] = or_ref[...] * cap + pos
+    pkt = (_iota((cap, n), 0) == pos).astype(BF16)
+    ohs = jnp.where(oht, sr_ref[...].astype(F32), 0.0).astype(BF16)
+    req_ref[...] = lax.dot_general(
+        ohs, pkt, (((1,), (1,)), ((), ())), preferred_element_type=F32
+    )
 
 
 def _call(kernel, outs, args, flops, name):
@@ -232,13 +247,16 @@
     local_list = near_list - me * clusters
     nlc = jnp.repeat(local_list.T, width, axis=1)
 
-    owner = far_owner[:, 0]
-    slot = far_slot
-    onehot = (owner[:, None] == jnp.arange(devices, dtype=jnp.int32)[None, :]).astype(jnp.int32)
-    before = jnp.cumsum(onehot, axis=0) - onehot
-    pos = jnp.sum(before * onehot, axis=1)
-    idx = (owner * cap + pos)[None, :].astype(jnp.int32)
-    req = jnp.zeros((devices, cap), jnp.int32).at[owner, pos].set(slot)
+    idx, req = _call(
+        _prep_kernel,
+        (
+            jax.ShapeDtypeStruct((1, npairs), jnp.int32),
+            jax.ShapeDtypeStruct((devices, cap), F32),
+        ),
+        (far_owner.reshape(1, npairs), far_slot.reshape(1, npairs)),
+        2 * devices * npairs * npairs,
+        "prep",
+    )
     rr = lax.all_to_all(req, "cells", 0, 0, tiled=True).reshape(1, devices * cap)
 
     nsend = devices * cap

time: 137 us -> 112 us (0.82)
  other arithmetic: 26.8 us -> 4.52 us
  local copies, waits for them, and re-layouts: 17.9 us -> 12.9 us
  Pallas kernels: 44.5 us -> 46.4 us
    another operation x3 -> x0, other arithmetic: 18.2 us -> none
    unnamed x10 -> x6, local copies, waits for them, and re-layouts: 7.52 us -> 2.96 us
    pallas_call x5 -> x6, Pallas kernels: 44.5 us -> 46.4 us  [_call(): pl.pallas_call(kernel, out_shape=outs, compiler_params=pltpu.CompilerPara...]
    unnamed x3 -> x0, other arithmetic: 1.5 us -> none
  transfers between devices with their start and end apart: 4 -> 4, of which waited for: 3 -> 3; matrix products, arithmetic and copies ran while one was open for 1% -> 1% of each run, Pallas kernels for 16% -> 20%
where the time goes in v1:
time: 112 us; the launch traced here: 111 us
  Pallas kernels  46.4 us (41%)
  blocking collectives  20.7 us (18%)
  starting transfers between devices  20.4 us (18%)
  local copies, waits for them, and re-layouts  12.9 us (12%)
  waiting for transfers between devices  5.32 us (5%)
  other arithmetic  4.52 us (4%)
    pallas_call x6, Pallas kernels, _call(): pl.pallas_call(kernel, out_shape=outs, compiler_params=pltpu.CompilerPara...  46.4 us
    all_to_all x1, blocking collectives, per_device(): lax.all_to_all(req, 'cells', 0, 0, tiled=True).reshape(1, devices * cap)  20.7 us
    all_to_all x2, starting transfers between devices, _exchange(): lax.all_to_all(send.reshape(rows, devices, slots), 'cells', 1, 1, tiled=T...  15.8 us
    ppermute x2, waiting for transfers between devices, per_device(): lax.ppermute(total, 'freq', [(i, i ^ hop) for i in range(freqs)])  4.64 us
    ppermute x2, starting transfers between devices, per_device(): lax.ppermute(total, 'freq', [(i, i ^ hop) for i in range(freqs)])  4.55 us
    reshape x4, local copies, waits for them, and re-layouts, _exchange(): send.reshape(rows, devices, slots)  3.8 us
    unnamed x6, local copies, waits for them, and re-layouts  2.96 us
    all_to_all x2, other arithmetic, _exchange(): lax.all_to_all(send.reshape(rows, devices, slots), 'cells', 1, 1, tiled=T...  2.46 us
  transfers between devices with their start and end apart: 4, of which 3 were waited for; matrix products, arithmetic and copies ran while one was open for 1% of the time, Pallas kernels for 20%

profile of v1, /device:TPU:8, one launch (start us, length us, event | category | flops | bytes accessed | tf_op | source)
XLA Modules:
  0.0 110.9 jit_solution(5925621232263463201)
XLA Ops:
  0.6 0.0 copy-start
  0.6 1.9 %prep.1 = (s32[1,1024]{1,0:T(1,128)}, f32[64,32]{1,0:T(8,128)}) custom-call(s32[1,1024]{1,0:T(1,128)} %bitcast.44, s32[1,1024]{1,0:T(1,128)} %bitcast.45), custom_call_target="tpu_custom_call" | custom-call | flops 134217728 | bytes 20480 | tf_op jit(solution)/shard_map/prep/pallas_call | solution.py:203
  2.5 20.7 %all_to_all.19 = f32[64,1,32]{2,1,0:T(1,128)S(1)} all-to-all(f32[64,1,32]{2,1,0:T(1,128)} %bitcast.40), channel_id=1, replica_groups=mesh['cells'=64,'freq'=4] {'cells'}, dimensions={0} | all-to-all | bytes 16384 | tf_op jit(solution)/shard_map/all_to_all | solution.py:260
  23.2 0.5 broadcast.3
  23.7 0.7 reduce.3
  24.4 0.7 reshape.34.rr_ref
  25.1 4.8 %proj.1 = f32[32,2048]{1,0:T(8,128)} custom-call(f32[2,4096]{1,0:T(2,128)} %bitcast.35, f32[1,4096]{1,0:T(1,128)} %c_ref.7, f32[2,16,4096]{2,1,0:T(8,128)} %bitcast.31, f32[1,2048]{1,0:T(1,128)} %reshape.34.rr_ref), custom_call_target="tpu_custom_call" | custom-call | flops 524288 | bytes 843776 | tf_op jit(solution)/shard_map/proj/pallas_call | solution.py:203
  29.9 1.3 %reshape.35 = f32[32,64,32]{2,1,0:T(8,128)S(1)} reshape(f32[32,2048]{1,0:T(8,128)} %proj.1) | data formatting | bytes 524288 | tf_op jit(solution)/shard_map/reshape | solution.py:215
  31.2 0.6 copy.20
  31.8 1.1 %reshape.48 = f32[64,1,1024]{2,1,0:T(1,128)} reshape(f32[64,32,32]{2,1,0:T(8,128)S(1)} %bitcast.27) | data formatting | bytes 524288
  32.9 5.5 %all-to-all-start.1 = ((f32[64,1,1024]{2,1,0:T(1,128)}), f32[64,1,1024]{2,1,0:T(1,128)S(1)}, u32[]{:S(2)}, u32[]{:S(2)}) async-start(f32[64,1,1024]{2,1,0:T(1,128)} %reshape.48), calls=%async_computation.1 | async-start | bytes 524288 | tf_op jit(solution)/shard_map/all_to_all | solution.py:215
  38.4 0.0 copy-done
  38.5 0.1 broadcast_in_dim.6
  38.5 0.7 reshape.31.nlc_ref
  39.3 10.8 %near.2.part_ref = f32[2,4096]{1,0:T(2,128)} custom-call(f32[2,4096]{1,0:T(2,128)} %bitcast.36, f32[1,4096]{1,0:T(1,128)} %c_ref.7, f32[2,192,4096]{2,1,0:T(8,128)} %bitcast.23, s32[3,4096]{1,0:T(4,128)} %reshape.31.nlc_ref, f32[2,4096]{1,0:T(2,128)} %bitcast.37), custom_call_target="tpu_custom_call" | custom-call | flops 6291456 | bytes 6455296 | tf_op jit(solution)/shard_map/near/pallas_call | solution.py:203
  50.1 0.0 all-to-all-done.1
  50.1 0.6 broadcast.4
  50.7 1.2 %reduce.4 = f32[64,1024]{1,0:T(8,128)S(1)} reduce(f32[64,1,1024]{2,1,0:T(1,128)S(1)} %all-to-all-done.1, f32[]{:T(128)} %broadcast.4), dimensions={1}, to_apply=%all_to_all.14.reduce_sub_computation | reduce | bytes 524292 | tf_op jit(solution)/shard_map/all_to_all | solution.py:215
  51.9 0.3 reshape.49
  52.3 0.6 copy.14
  52.9 1.2 %reshape.36.recv_ref = f32[32,2048]{1,0:T(8,128)} reshape(f32[32,64,32]{2,1,0:T(8,128)S(1)} %copy.14) | data formatting | bytes 524288 | tf_op jit(solution)/shard_map/reshape | solution.py:216
  54.1 10.3 %far_proj.1 = (f32[2,4096]{1,0:T(2,128)}, f32[32,2048]{1,0:T(8,128)}) custom-call(f32[2,4096]{1,0:T(2,128)} %near.2.part_ref, f32[32,2048]{1,0:T(8,128)} %reshape.36.recv_ref, s32[1,1024]{1,0:T(1,128)} %get-tuple-element.9.idx_ref, f32[2,16,16,1024]{3,2,1,0:T(8,128)} %bitcast.25, f32[2,16,4096]{2,1,0:T(8,128)} %bitcast.33, f32[1,4096]{1,0:T(1,128)} %c_ref.7, ...), custom_call_target="tpu_custom_call" | custom-call | flops 4194304 | bytes 3764224 | tf_op jit(solution)/shard_map/far_proj/pallas_call | solution.py:203
  64.4 1.3 %reshape.37 = f32[32,64,32]{2,1,0:T(8,128)S(1)} reshape(f32[32,2048]{1,0:T(8,128)} %get-tuple-element.11) | data formatting | bytes 524288 | tf_op jit(solution)/shard_map/reshape | solution.py:215
  65.7 0.6 copy.19
  66.3 1.1 %reshape.50 = f32[64,1,1024]{2,1,0:T(1,128)} reshape(f32[64,32,32]{2,1,0:T(8,128)S(1)} %bitcast.29) | data formatting | bytes 524288
  67.4 10.3 %all-to-all-start.2 = ((f32[64,1,1024]{2,1,0:T(1,128)}), f32[64,1,1024]{2,1,0:T(1,128)S(1)}, u32[]{:S(2)}, u32[]{:S(2)}) async-start(f32[64,1,1024]{2,1,0:T(1,128)} %reshape.50), calls=%async_computation.2 | async-start | bytes 524288 | tf_op jit(solution)/shard_map/all_to_all | solution.py:215
  77.8 10.8 %near.3.part_ref = f32[2,4096]{1,0:T(2,128)} custom-call(f32[2,4096]{1,0:T(2,128)} %get-tuple-element.10.u_ref, f32[1,4096]{1,0:T(1,128)} %c_ref.7, f32[2,192,4096]{2,1,0:T(8,128)} %bitcast.24, s32[3,4096]{1,0:T(4,128)} %reshape.31.nlc_ref, f32[2,4096]{1,0:T(2,128)} %bitcast.38), custom_call_target="tpu_custom_call" | custom-call | flops 6291456 | bytes 6455296 | tf_op jit(solution)/shard_map/near/pallas_call | solution.py:203
  88.6 0.7 all-to-all-done.2
  89.3 1.2 %reduce.5 = f32[64,1024]{1,0:T(8,128)S(1)} reduce(f32[64,1,1024]{2,1,0:T(1,128)S(1)} %all-to-all-done.2, f32[]{:T(128)} %broadcast.4), dimensions={1}, to_apply=%all_to_all.15.reduce_sub_computation | reduce | bytes 524292 | tf_op jit(solution)/shard_map/all_to_all | solution.py:215
  90.5 0.3 reshape.51
  90.9 0.6 copy.16
  91.5 1.2 %reshape.38.recv_ref = f32[32,2048]{1,0:T(8,128)} reshape(f32[32,64,32]{2,1,0:T(8,128)S(1)} %copy.16) | data formatting | bytes 524288 | tf_op jit(solution)/shard_map/reshape | solution.py:216
  92.7 7.7 %far_grad.1 = (f32[2,4096]{1,0:T(2,128)}, f32[1,4096]{1,0:T(1,128)}) custom-call(f32[2,4096]{1,0:T(2,128)} %near.3.part_ref, f32[32,2048]{1,0:T(8,128)} %reshape.38.recv_ref, s32[1,1024]{1,0:T(1,128)} %get-tuple-element.9.idx_ref, f32[2,16,16,1024]{3,2,1,0:T(8,128)} %bitcast.26, f32[2,16,4096]{2,1,0:T(8,128)} %bitcast.34, f32[2,4096]{1,0:T(2,128)} %bitcast.39), custom_call_target="tpu_custom_call" | custom-call | flops 4194304 | bytes 3002368 | tf_op jit(solution)/shard_map/far_grad/pallas_call | solution.py:203
  100.4 1.5 %collective-permute-start = (f32[4096]{0:T(1024)}, f32[4096]{0:T(1024)S(1)}, u32[]{:S(2)}, u32[]{:S(2)}) collective-permute-start(f32[4096]{0:T(1024)} %bitcast.41), channel_id=1, source_target_pairs={{0,1},{1,0},{2,3},{3,2},{4,5},{5,4},{6,7},{7,6},{8,9},{9,8},{10,11... | collective-permute-start | bytes 49160 | tf_op jit(solution)/shard_map/ppermute | solution.py:294
  101.9 2.4 %collective-permute-done = f32[4096]{0:T(1024)S(1)} collective-permute-done((f32[4096]{0:T(1024)}, f32[4096]{0:T(1024)S(1)}, u32[]{:S(2)}, u32[]{:S(2)}) %collective-permute-start) | collective-permute-done | bytes 16416 | tf_op jit(solution)/shard_map/ppermute | solution.py:294
  104.4 0.7 add.6
  105.1 3.0 %collective-permute-start.1 = (f32[4096]{0:T(1024)S(1)}, f32[4096]{0:T(1024)S(1)}, u32[]{:S(2)}, u32[]{:S(2)}) collective-permute-start(f32[4096]{0:T(1024)S(1)} %add.6), channel_id=1, source_target_pairs={{0,2},{1,3},{2,0},{3,1},{4,6},{5,7},{6,4},{7,5},{8,10},{9,11},{10,... | collective-permute-start | bytes 49160 | tf_op jit(solution)/shard_map/ppermute | solution.py:294
  108.1 2.2 %collective-permute-done.1 = f32[4096]{0:T(1024)S(1)} collective-permute-done((f32[4096]{0:T(1024)S(1)}, f32[4096]{0:T(1024)S(1)}, u32[]{:S(2)}, u32[]{:S(2)}) %collective-permute-start.1) | collective-permute-done | bytes 16416 | tf_op jit(solution)/shard_map/ppermute | solution.py:294
  110.3 0.6 add.7
  (1 shorter events, 0.0 us)
Async XLA Ops:
  0.6 37.8 %copy-start = (s32[64,3]{0,1:T(4,128)S(1)}, s32[64,3]{0,1:T(4,128)}, u32[]{:S(2)}) copy-start(s32[64,3]{0,1:T(4,128)} %param.14) | copy-start | bytes 2308
  32.9 17.2 %all-to-all-start.1 = ((f32[64,1,1024]{2,1,0:T(1,128)}), f32[64,1,1024]{2,1,0:T(1,128)S(1)}, u32[]{:S(2)}, u32[]{:S(2)}) async-start(f32[64,1,1024]{2,1,0:T(1,128)} %reshape.48), calls=%async_computation.1 | async-start | bytes 524288 | tf_op jit(solution)/shard_map/all_to_all | solution.py:215
  67.4 21.9 %all-to-all-start.2 = ((f32[64,1,1024]{2,1,0:T(1,128)}), f32[64,1,1024]{2,1,0:T(1,128)S(1)}, u32[]{:S(2)}, u32[]{:S(2)}) async-start(f32[64,1,1024]{2,1,0:T(1,128)} %reshape.50), calls=%async_computation.2 | async-start | bytes 524288 | tf_op jit(solution)/shard_map/all_to_all | solution.py:215
  100.4 3.9 %collective-permute-start = (f32[4096]{0:T(1024)}, f32[4096]{0:T(1024)S(1)}, u32[]{:S(2)}, u32[]{:S(2)}) collective-permute-start(f32[4096]{0:T(1024)} %bitcast.41), channel_id=1, source_target_pairs={{0,1},{1,0},{2,3},{3,2},{4,5},{5,4},{6,7},{7,6},{8,9},{9,8},{10,11... | collective-permute-start | bytes 49160 | tf_op jit(solution)/shard_map/ppermute | solution.py:294
  105.1 5.2 %collective-permute-start.1 = (f32[4096]{0:T(1024)S(1)}, f32[4096]{0:T(1024)S(1)}, u32[]{:S(2)}, u32[]{:S(2)}) collective-permute-start(f32[4096]{0:T(1024)S(1)} %add.6), channel_id=1, source_target_pairs={{0,2},{1,3},{2,0},{3,1},{4,6},{5,7},{6,4},{7,5},{8,10},{9,11},{10,... | collective-permute-start | bytes 49160 | tf_op jit(solution)/shard_map/ppermute | solution.py:294

commit v2 on v1

--- a/solution.py
+++ b/solution.py
@@ -53,7 +53,7 @@
     return _xdot(q, oh)
 
 
-def _proj_kernel(u_ref, c_ref, p_ref, rr_ref, send_ref):
+def _proj_kernel(u_ref, c_ref, p_ref, q_ref):
     cells = u_ref.shape[1]
     clusters = cells // 64
     rank2 = 2 * p_ref.shape[1]
@@ -64,8 +64,7 @@
         pw = _weighted_proj(u_ref[:, sl], c_ref[:, sl], p_ref[0, :, sl], p_ref[1, :, sl])
         return q + _proj_chunk(pw, off, clusters, 64)
 
-    q = lax.fori_loop(0, cells // CHUNK, body, jnp.zeros((rank2, clusters), F32))
-    send_ref[...] = _send_of(q, rr_ref, clusters)
+    q_ref[...] = lax.fori_loop(0, cells // CHUNK, body, jnp.zeros((rank2, clusters), F32))
 
 
 def _near_kernel(u_ref, c_ref, nb_ref, nlc_ref, base_ref, out_ref):
@@ -109,21 +108,18 @@
     lax.fori_loop(0, cells // CHUNK, near_body, 0)
 
 
-def _far_common(part_ref, recv_ref, idx_ref, cpl_ref, e_ref, u_ref, chunk_tail):
+def _far_common(part_ref, qs_ref, cpl_ref, e_ref, u_ref, chunk_tail):
     cells = part_ref.shape[1]
     width = 64
     clusters = cells // width
     rank = cpl_ref.shape[1]
-    npairs = idx_ref.shape[1]
+    npairs = qs_ref.shape[1]
     far = npairs // clusters
-    nrecv = recv_ref.shape[1]
-    rsplit = _split3(recv_ref[...])
 
     def pair_body(pj, z):
         off = pl.multiple_of(pj * PAIR_CHUNK, PAIR_CHUNK)
         sl = pl.ds(off, PAIR_CHUNK)
-        g = (_iota((nrecv, PAIR_CHUNK), 0) == idx_ref[:, sl]).astype(BF16)
-        qs = _sdot(rsplit, g)
+        qs = qs_ref[:, sl]
         qre = qs[:rank][None]
         qim = qs[rank:][None]
         cre = cpl_ref[0, :, :, sl]
@@ -154,7 +150,7 @@
     return cell_body
 
 
-def _far_proj_kernel(part_ref, recv_ref, idx_ref, cpl_ref, e_ref, c_ref, p_ref, rr_ref, u_ref, send_ref):
+def _far_proj_kernel(part_ref, qs_ref, cpl_ref, e_ref, c_ref, p_ref, u_ref, q_ref):
     cells = part_ref.shape[1]
     clusters = cells // 64
     rank2 = 2 * p_ref.shape[1]
@@ -163,12 +159,11 @@
         pw = _weighted_proj(u, c_ref[:, sl], p_ref[0, :, sl], p_ref[1, :, sl])
         return q + _proj_chunk(pw, off, clusters, 64)
 
-    body = _far_common(part_ref, recv_ref, idx_ref, cpl_ref, e_ref, u_ref, tail)
-    q = lax.fori_loop(0, cells // CHUNK, body, jnp.zeros((rank2, clusters), F32))
-    send_ref[...] = _send_of(q, rr_ref, clusters)
-
-
-def _far_grad_kernel(part_ref, recv_ref, idx_ref, cpl_ref, e_ref, bg_ref, u_ref, t_ref):
+    body = _far_common(part_ref, qs_ref, cpl_ref, e_ref, u_ref, tail)
+    q_ref[...] = lax.fori_loop(0, cells // CHUNK, body, jnp.zeros((rank2, clusters), F32))
+
+
+def _far_grad_kernel(part_ref, qs_ref, cpl_ref, e_ref, bg_ref, u_ref, t_ref):
     cells = part_ref.shape[1]
 
     def tail(u, off, sl, acc):
@@ -176,7 +171,7 @@
         t_ref[:, sl] = bg[0:1] * u[0:1] + bg[1:2] * u[1:2]
         return acc
 
-    body = _far_common(part_ref, recv_ref, idx_ref, cpl_ref, e_ref, u_ref, tail)
+    body = _far_common(part_ref, qs_ref, cpl_ref, e_ref, u_ref, tail)
     lax.fori_loop(0, cells // CHUNK, body, 0)
 
 
@@ -209,11 +204,12 @@
     )(*args)
 
 
-def _exchange(send, devices):
+def _exchange(q, rr, idx, devices):
+    send = q[:, rr]
     rows, total = send.shape
     slots = total // devices
     got = lax.all_to_all(send.reshape(rows, devices, slots), "cells", 1, 1, tiled=True)
-    return got.reshape(rows, total)
+    return got.reshape(rows, total)[:, idx]
 
 
 def per_device(
@@ -257,25 +253,26 @@
         2 * devices * npairs * npairs,
         "prep",
     )
-    rr = lax.all_to_all(req, "cells", 0, 0, tiled=True).reshape(1, devices * cap)
+    rr = lax.all_to_all(req, "cells", 0, 0, tiled=True).reshape(devices * cap).astype(jnp.int32)
+    idx = idx.reshape(npairs)
 
     nsend = devices * cap
     rank2 = 2 * pb.shape[1]
-    send_shape = jax.ShapeDtypeStruct((rank2, nsend), F32)
+    q_shape = jax.ShapeDtypeStruct((rank2, clusters), F32)
     field_shape = jax.ShapeDtypeStruct((2, cells), F32)
 
-    send = _call(_proj_kernel, send_shape, (src, cst, pb, rr), 4 * rank2 * cells, "proj")
+    q = _call(_proj_kernel, q_shape, (src, cst, pb), 4 * rank2 * cells, "proj")
     field = src
     for step in range(ITERS):
-        recv = _exchange(send, devices)
+        qs = _exchange(q, rr, idx, devices)
         part = _call(
             _near_kernel, field_shape, (field, cst, nb, nlc, src), 8 * nb.shape[1] * cells, "near"
         )
         if step < ITERS - 1:
-            field, send = _call(
+            field, q = _call(
                 _far_proj_kernel,
-                (field_shape, send_shape),
-                (part, recv, idx, cp, eb, cst, pb, rr),
+                (field_shape, q_shape),
+                (part, qs, cp, eb, cst, pb),
                 8 * cp.size,
                 "far_proj",
             )
@@ -283,7 +280,7 @@
             field, terms = _call(
                 _far_grad_kernel,
                 (field_shape, jax.ShapeDtypeStruct((1, cells), F32)),
-                (part, recv, idx, cp, eb, bg),
+                (part, qs, cp, eb, bg),
                 8 * cp.size,
                 "far_grad",
             )

time: 112 us -> 116 us (1.036)
  blocking collectives: 20.7 us -> 0 us
  starting transfers between devices: 20.4 us -> 34.1 us
  local copies, waits for them, and re-layouts: 12.9 us -> 24.2 us
  Pallas kernels: 46.4 us -> 42.2 us
  waiting for transfers between devices: 5.32 us -> 8.72 us
    all_to_all x1 -> x0, blocking collectives: 20.7 us -> none  [per_device(): lax.all_to_all(req, 'cells', 0, 0, tiled=True).reshape(1, devices * cap)]
    gather x0 -> x6, local copies, waits for them, and re-layouts: none -> 18.2 us  [the longest x2 10.9 us: _exchange(): send = q[:, rr]]
    all_to_all x0 -> x1, starting transfers between devices: none -> 12.2 us  [per_device(): lax.all_to_all(req, 'cells', 0, 0, tiled=True).reshape(devices * cap)]
    reshape x7 -> x0, local copies, waits for them, and re-layouts: 6.84 us -> none  [the longest x4 3.8 us: _exchange(): send.reshape(rows, devices, slots)]
    pallas_call x6, Pallas kernels: 46.4 us -> 42.2 us  [_call(): pl.pallas_call(kernel, out_shape=outs, compiler_params=pltpu.CompilerPara...]
    all_to_all x0 -> x1, waiting for transfers between devices: none -> 3.32 us  [per_device(): lax.all_to_all(req, 'cells', 0, 0, tiled=True).reshape(devices * cap)]
    pallas_call x0 -> x2, local copies, waits for them, and re-layouts: none -> 1.59 us  [_call(): pl.pallas_call(kernel, out_shape=outs, compiler_params=pltpu.CompilerPara...]
    all_to_all x2, starting transfers between devices: 15.8 us -> 17.4 us  [_exchange(): lax.all_to_all(send.reshape(rows, devices, slots), 'cells', 1, 1, tiled=T...]
  transfers between devices with their start and end apart: 4 -> 5, of which waited for: 3 -> 4; matrix products, arithmetic and copies ran while one was open for 1% -> 2% of each run, Pallas kernels for 20% -> 23%
where the time goes in v2:
time: 116 us; the launch traced here: 115 us
  Pallas kernels  42.2 us (36%)
  starting transfers between devices  34.1 us (29%)
  local copies, waits for them, and re-layouts  24.2 us (21%)
  waiting for transfers between devices  8.72 us (8%)
  other arithmetic  4.73 us (4%)
    pallas_call x6, Pallas kernels, _call(): pl.pallas_call(kernel, out_shape=outs, compiler_params=pltpu.CompilerPara...  42.2 us
    all_to_all x2, starting transfers between devices, _exchange(): lax.all_to_all(send.reshape(rows, devices, slots), 'cells', 1, 1, tiled=T...  17.4 us
    all_to_all x1, starting transfers between devices, per_device(): lax.all_to_all(req, 'cells', 0, 0, tiled=True).reshape(devices * cap)  12.2 us
    gather x2, local copies, waits for them, and re-layouts, _exchange(): send = q[:, rr]  10.9 us
    gather x4, local copies, waits for them, and re-layouts, _exchange(): return got.reshape(rows, total)[:, idx]  7.27 us
    ppermute x2, waiting for transfers between devices, per_device(): lax.ppermute(total, 'freq', [(i, i ^ hop) for i in range(freqs)])  4.71 us
    ppermute x2, starting transfers between devices, per_device(): lax.ppermute(total, 'freq', [(i, i ^ hop) for i in range(freqs)])  4.48 us
    all_to_all x1, waiting for transfers between devices, per_device(): lax.all_to_all(req, 'cells', 0, 0, tiled=True).reshape(devices * cap)  3.32 us
  transfers between devices with their start and end apart: 5, of which 4 were waited for; matrix products, arithmetic and copies ran while one was open for 2% of the time, Pallas kernels for 23%

profile of v2, /device:TPU:8, one launch (start us, length us, event | category | flops | bytes accessed | tf_op | source)
XLA Modules:
  0.0 114.8 jit_solution(5443995192800418993)
XLA Ops:
  0.6 1.9 %prep.1 = (s32[1,1024]{1,0:T(1,128)}, f32[64,32]{1,0:T(8,128)}) custom-call(s32[1,1024]{1,0:T(1,128)} %bitcast.58, s32[1,1024]{1,0:T(1,128)} %bitcast.59), custom_call_target="tpu_custom_call" | custom-call | flops 134217728 | bytes 20480 | tf_op jit(solution)/shard_map/prep/pallas_call | solution.py:198
  2.5 0.0 copy-start
  2.5 12.2 %all-to-all-start = ((f32[64,1,32]{2,1,0:T(1,128)}), f32[64,1,32]{2,1,0:T(1,128)S(1)}, u32[]{:S(2)}, u32[]{:S(2)}) async-start(f32[64,1,32]{2,1,0:T(1,128)} %bitcast.52), calls=%async_computation | async-start | bytes 65536 | tf_op jit(solution)/shard_map/all_to_all | solution.py:256
  14.8 4.4 %proj.1 = f32[32,64]{1,0:T(8,128)} custom-call(f32[2,4096]{1,0:T(2,128)} %bitcast.45, f32[1,4096]{1,0:T(1,128)} %c_ref.7, f32[2,16,4096]{2,1,0:T(8,128)} %bitcast.39), custom_call_target="tpu_custom_call" | custom-call | flops 524288 | bytes 581632 | tf_op jit(solution)/shard_map/proj/pallas_call | solution.py:198
  19.2 0.8 copy.21
  20.0 3.3 %all-to-all-done = f32[64,1,32]{2,1,0:T(1,128)S(1)} async-done(((f32[64,1,32]{2,1,0:T(1,128)}), f32[64,1,32]{2,1,0:T(1,128)S(1)}, u32[]{:S(2)}, u32[]{:S(2)}) %all-to-all-start) | async-done | bytes 8224 | tf_op jit(solution)/shard_map/all_to_all | solution.py:256
  23.3 0.1 convert_reduce_fusion
  23.4 0.1 convert_element_type.14
  23.5 5.5 %gather_fusion = f32[2048,32]{1,0:T(8,128)S(1)} fusion(f32[32,64]{0,1:T(8,128)S(1)} %copy.21, s32[2048]{0:T(1024)S(1)} %broadcast_clamp_fusion), kind=kCustom, calls=%fused_computation | custom fusion | bytes 532480 | tf_op jit(solution)/shard_map/gather | solution.py:208
  29.0 1.1 reshape.127
  30.1 7.0 %all-to-all-start.1 = ((f32[64,1,1024]{2,1,0:T(1,128)}), f32[64,1,1024]{2,1,0:T(1,128)S(1)}, u32[]{:S(2)}, u32[]{:S(2)}) async-start(f32[64,1,1024]{2,1,0:T(1,128)} %reshape.127), calls=%async_computation.1 | async-start | bytes 524288 | tf_op jit(solution)/shard_map/all_to_all | solution.py:211
  37.2 0.7 subtract_bitcast_fusion
  37.9 0.1 broadcast_in_dim.4
  37.9 0.7 reshape.80.nlc_ref
  38.7 10.8 %near.2.part_ref = f32[2,4096]{1,0:T(2,128)} custom-call(f32[2,4096]{1,0:T(2,128)} %bitcast.46, f32[1,4096]{1,0:T(1,128)} %c_ref.7, f32[2,192,4096]{2,1,0:T(8,128)} %bitcast.33, s32[3,4096]{1,0:T(4,128)} %reshape.80.nlc_ref, f32[2,4096]{1,0:T(2,128)} %bitcast.47), custom_call_target="tpu_custom_call" | custom-call | flops 6291456 | bytes 6455296 | tf_op jit(solution)/shard_map/near/pallas_call | solution.py:198
  49.5 0.0 copy-done
  49.5 0.0 all-to-all-done.1
  49.6 0.6 broadcast.63
  50.1 1.3 %reduce.4 = f32[64,1024]{1,0:T(8,128)S(1)} reduce(f32[64,1,1024]{2,1,0:T(1,128)S(1)} %all-to-all-done.1, f32[]{:T(128)} %broadcast.63), dimensions={1}, to_apply=%all_to_all.14.reduce_sub_computation | reduce | bytes 524292 | tf_op jit(solution)/shard_map/all_to_all | solution.py:211
  51.4 0.3 reshape.128
  51.8 2.8 %gather_fusion.1 = f32[1024,32]{1,0:T(8,128)S(1)} fusion(f32[32,2048]{0,1:T(8,128)S(1)} %bitcast.38, s32[1024]{0:T(1024)S(1)} %broadcast_clamp_fusion.1), kind=kCustom, calls=%fused_computation.1 | custom fusion | bytes 266240 | tf_op jit(solution)/shard_map/gather | solution.py:212
  54.6 0.8 copy.22
  55.4 8.2 %far_proj.1 = (f32[2,4096]{1,0:T(2,128)}, f32[32,64]{1,0:T(8,128)}) custom-call(f32[2,4096]{1,0:T(2,128)} %near.2.part_ref, f32[32,1024]{1,0:T(8,128)} %bitcast.49, f32[2,16,16,1024]{3,2,1,0:T(8,128)} %bitcast.35, f32[2,16,4096]{2,1,0:T(8,128)} %bitcast.41, f32[1,4096]{1,0:T(1,128)} %c_ref.7, f32[2,16,4096]{2,1,0:T(8,128)} %bitcast.40), custom_call_target="tpu_custom_call" | custom-call | flops 4194304 | bytes 3366912 | tf_op jit(solution)/shard_map/far_proj/pallas_call | solution.py:198
  63.6 0.8 copy.23
  64.4 5.5 %gather_fusion.2 = f32[2048,32]{1,0:T(8,128)S(1)} fusion(f32[32,64]{0,1:T(8,128)S(1)} %copy.23, s32[2048]{0:T(1024)S(1)} %broadcast_clamp_fusion), kind=kCustom, calls=%fused_computation.2 | custom fusion | bytes 532480 | tf_op jit(solution)/shard_map/gather | solution.py:208
  69.9 1.1 reshape.129
  71.0 10.3 %all-to-all-start.2 = ((f32[64,1,1024]{2,1,0:T(1,128)}), f32[64,1,1024]{2,1,0:T(1,128)S(1)}, u32[]{:S(2)}, u32[]{:S(2)}) async-start(f32[64,1,1024]{2,1,0:T(1,128)} %reshape.129), calls=%async_computation.2 | async-start | bytes 524288 | tf_op jit(solution)/shard_map/all_to_all | solution.py:211
  81.4 10.8 %near.3.part_ref = f32[2,4096]{1,0:T(2,128)} custom-call(f32[2,4096]{1,0:T(2,128)} %get-tuple-element.10.u_ref, f32[1,4096]{1,0:T(1,128)} %c_ref.7, f32[2,192,4096]{2,1,0:T(8,128)} %bitcast.34, s32[3,4096]{1,0:T(4,128)} %reshape.80.nlc_ref, f32[2,4096]{1,0:T(2,128)} %bitcast.48), custom_call_target="tpu_custom_call" | custom-call | flops 6291456 | bytes 6455296 | tf_op jit(solution)/shard_map/near/pallas_call | solution.py:198
  92.2 0.7 all-to-all-done.2
  92.9 1.3 %reduce.5 = f32[64,1024]{1,0:T(8,128)S(1)} reduce(f32[64,1,1024]{2,1,0:T(1,128)S(1)} %all-to-all-done.2, f32[]{:T(128)} %broadcast.63), dimensions={1}, to_apply=%all_to_all.15.reduce_sub_computation | reduce | bytes 524292 | tf_op jit(solution)/shard_map/all_to_all | solution.py:211
  94.2 0.3 reshape.130
  94.6 2.8 %gather_fusion.3 = f32[1024,32]{1,0:T(8,128)S(1)} fusion(f32[32,2048]{0,1:T(8,128)S(1)} %bitcast.37, s32[1024]{0:T(1024)S(1)} %broadcast_clamp_fusion.1), kind=kCustom, calls=%fused_computation.3 | custom fusion | bytes 266240 | tf_op jit(solution)/shard_map/gather | solution.py:212
  97.4 0.8 copy.24
  98.2 6.0 %far_grad.1 = (f32[2,4096]{1,0:T(2,128)}, f32[1,4096]{1,0:T(1,128)}) custom-call(f32[2,4096]{1,0:T(2,128)} %near.3.part_ref, f32[32,1024]{1,0:T(8,128)} %bitcast.50, f32[2,16,16,1024]{3,2,1,0:T(8,128)} %bitcast.36, f32[2,16,4096]{2,1,0:T(8,128)} %bitcast.42, f32[2,4096]{1,0:T(2,128)} %bitcast.51), custom_call_target="tpu_custom_call" | custom-call | flops 4194304 | bytes 2867200 | tf_op jit(solution)/shard_map/far_grad/pallas_call | solution.py:198
  104.2 1.5 %collective-permute-start = (f32[4096]{0:T(1024)}, f32[4096]{0:T(1024)S(1)}, u32[]{:S(2)}, u32[]{:S(2)}) collective-permute-start(f32[4096]{0:T(1024)} %bitcast.54), channel_id=1, source_target_pairs={{0,1},{1,0},{2,3},{3,2},{4,5},{5,4},{6,7},{7,6},{8,9},{9,8},{10,11... | collective-permute-start | bytes 49160 | tf_op jit(solution)/shard_map/ppermute | solution.py:291
  105.7 2.5 %collective-permute-done = f32[4096]{0:T(1024)S(1)} collective-permute-done((f32[4096]{0:T(1024)}, f32[4096]{0:T(1024)S(1)}, u32[]{:S(2)}, u32[]{:S(2)}) %collective-permute-start) | collective-permute-done | bytes 16416 | tf_op jit(solution)/shard_map/ppermute | solution.py:291
  108.2 0.7 add.30
  108.9 3.0 %collective-permute-start.1 = (f32[4096]{0:T(1024)S(1)}, f32[4096]{0:T(1024)S(1)}, u32[]{:S(2)}, u32[]{:S(2)}) collective-permute-start(f32[4096]{0:T(1024)S(1)} %add.30), channel_id=1, source_target_pairs={{0,2},{1,3},{2,0},{3,1},{4,6},{5,7},{6,4},{7,5},{8,10},{9,11},{10,... | collective-permute-start | bytes 49160 | tf_op jit(solution)/shard_map/ppermute | solution.py:291
  111.9 2.2 %collective-permute-done.1 = f32[4096]{0:T(1024)S(1)} collective-permute-done((f32[4096]{0:T(1024)S(1)}, f32[4096]{0:T(1024)S(1)}, u32[]{:S(2)}, u32[]{:S(2)}) %collective-permute-start.1) | collective-permute-done | bytes 16416 | tf_op jit(solution)/shard_map/ppermute | solution.py:291
  114.1 0.6 add.31
  (4 shorter events, 0.0 us)
Async XLA Ops:
  2.5 47.0 %copy-start = (s32[1,1024]{1,0:T(1,128)S(1)}, s32[1,1024]{1,0:T(1,128)}, u32[]{:S(2)}) copy-start(s32[1,1024]{1,0:T(1,128)} %get-tuple-element.9) | copy-start | bytes 12292
  2.5 20.8 %all-to-all-start = ((f32[64,1,32]{2,1,0:T(1,128)}), f32[64,1,32]{2,1,0:T(1,128)S(1)}, u32[]{:S(2)}, u32[]{:S(2)}) async-start(f32[64,1,32]{2,1,0:T(1,128)} %bitcast.52), calls=%async_computation | async-start | bytes 65536 | tf_op jit(solution)/shard_map/all_to_all | solution.py:256
  30.1 19.4 %all-to-all-start.1 = ((f32[64,1,1024]{2,1,0:T(1,128)}), f32[64,1,1024]{2,1,0:T(1,128)S(1)}, u32[]{:S(2)}, u32[]{:S(2)}) async-start(f32[64,1,1024]{2,1,0:T(1,128)} %reshape.127), calls=%async_computation.1 | async-start | bytes 524288 | tf_op jit(solution)/shard_map/all_to_all | solution.py:211
  71.0 21.9 %all-to-all-start.2 = ((f32[64,1,1024]{2,1,0:T(1,128)}), f32[64,1,1024]{2,1,0:T(1,128)S(1)}, u32[]{:S(2)}, u32[]{:S(2)}) async-start(f32[64,1,1024]{2,1,0:T(1,128)} %reshape.129), calls=%async_computation.2 | async-start | bytes 524288 | tf_op jit(solution)/shard_map/all_to_all | solution.py:211
  104.2 3.9 %collective-permute-start = (f32[4096]{0:T(1024)}, f32[4096]{0:T(1024)S(1)}, u32[]{:S(2)}, u32[]{:S(2)}) collective-permute-start(f32[4096]{0:T(1024)} %bitcast.54), channel_id=1, source_target_pairs={{0,1},{1,0},{2,3},{3,2},{4,5},{5,4},{6,7},{7,6},{8,9},{9,8},{10,11... | collective-permute-start | bytes 49160 | tf_op jit(solution)/shard_map/ppermute | solution.py:291
  108.9 5.2 %collective-permute-start.1 = (f32[4096]{0:T(1024)S(1)}, f32[4096]{0:T(1024)S(1)}, u32[]{:S(2)}, u32[]{:S(2)}) collective-permute-start(f32[4096]{0:T(1024)S(1)} %add.30), channel_id=1, source_target_pairs={{0,2},{1,3},{2,0},{3,1},{4,6},{5,7},{6,4},{7,5},{8,10},{9,11},{10,... | collective-permute-start | bytes 49160 | tf_op jit(solution)/shard_map/ppermute | solution.py:291

commit v3 on v2

--- a/solution.py
+++ b/solution.py
@@ -47,10 +47,29 @@
     return _xdot(pw, seg.astype(BF16))
 
 
-def _send_of(q, rr_ref, clusters):
-    nsend = rr_ref.shape[1]
-    oh = (_iota((clusters, nsend), 0).astype(F32) == rr_ref[...]).astype(BF16)
-    return _xdot(q, oh)
+def _pack(q, rr_ref):
+    rank2, clusters = q.shape
+    rows, groups = rr_ref.shape
+    wide = groups * clusters
+    lane = _iota((rows, wide), 1)
+    grp = lane // clusters
+    rr = rr_ref[...]
+    want = rr[:, 0:1]
+    for g in range(1, groups):
+        want = jnp.where(grp == g, rr[:, g : g + 1], want)
+    oh = ((lane % clusters).astype(F32) == want).astype(BF16)
+    tile = (_iota((clusters, wide), 0) == _iota((clusters, wide), 1) % clusters).astype(BF16)
+    qw = _xdot(q, tile)
+    qw = jnp.concatenate([qw] * groups, axis=0)
+    keep = (_iota((groups * rank2, wide), 0) // rank2) == (_iota((groups * rank2, wide), 1) // clusters)
+    qw = jnp.where(keep, qw, 0.0)
+    r = lax.dot_general(oh, _split3(qw), (((1,), (1,)), ((), ())), preferred_element_type=F32)
+    n = groups * rank2
+    return r[:, :n] + r[:, n : 2 * n] + r[:, 2 * n :]
+
+
+def _pack_kernel(q_ref, rr_ref, send_ref):
+    send_ref[...] = _pack(q_ref[...], rr_ref)
 
 
 def _proj_kernel(u_ref, c_ref, p_ref, q_ref):
@@ -150,7 +169,7 @@
     return cell_body
 
 
-def _far_proj_kernel(part_ref, qs_ref, cpl_ref, e_ref, c_ref, p_ref, u_ref, q_ref):
+def _far_proj_kernel(part_ref, qs_ref, cpl_ref, e_ref, c_ref, p_ref, rr_ref, u_ref, send_ref):
     cells = part_ref.shape[1]
     clusters = cells // 64
     rank2 = 2 * p_ref.shape[1]
@@ -160,7 +179,8 @@
         return q + _proj_chunk(pw, off, clusters, 64)
 
     body = _far_common(part_ref, qs_ref, cpl_ref, e_ref, u_ref, tail)
-    q_ref[...] = lax.fori_loop(0, cells // CHUNK, body, jnp.zeros((rank2, clusters), F32))
+    q = lax.fori_loop(0, cells // CHUNK, body, jnp.zeros((rank2, clusters), F32))
+    send_ref[...] = _pack(q, rr_ref)
 
 
 def _far_grad_kernel(part_ref, qs_ref, cpl_ref, e_ref, bg_ref, u_ref, t_ref):
@@ -204,12 +224,11 @@
     )(*args)
 
 
-def _exchange(q, rr, idx, devices):
-    send = q[:, rr]
-    rows, total = send.shape
-    slots = total // devices
-    got = lax.all_to_all(send.reshape(rows, devices, slots), "cells", 1, 1, tiled=True)
-    return got.reshape(rows, total)[:, idx]
+def _exchange(send, idx, devices, cap):
+    total = send.size
+    got = lax.all_to_all(send.reshape(devices, total // devices), "cells", 0, 0)
+    got = got.reshape(devices * cap, total // (devices * cap))
+    return got[idx].T
 
 
 def per_device(
@@ -253,7 +272,8 @@
         2 * devices * npairs * npairs,
         "prep",
     )
-    rr = lax.all_to_all(req, "cells", 0, 0, tiled=True).reshape(devices * cap).astype(jnp.int32)
+    groups = 4
+    rr = lax.all_to_all(req, "cells", 0, 0, tiled=True).reshape(devices * cap // groups, groups)
     idx = idx.reshape(npairs)
 
     nsend = devices * cap
@@ -262,17 +282,19 @@
     field_shape = jax.ShapeDtypeStruct((2, cells), F32)
 
     q = _call(_proj_kernel, q_shape, (src, cst, pb), 4 * rank2 * cells, "proj")
+    send_shape = jax.ShapeDtypeStruct((devices * cap // groups, groups * rank2), F32)
+    send = _call(_pack_kernel, send_shape, (q, rr), 2 * send_shape.size * clusters, "pack")
     field = src
     for step in range(ITERS):
-        qs = _exchange(q, rr, idx, devices)
+        qs = _exchange(send, idx, devices, cap)
         part = _call(
             _near_kernel, field_shape, (field, cst, nb, nlc, src), 8 * nb.shape[1] * cells, "near"
         )
         if step < ITERS - 1:
-            field, q = _call(
+            field, send = _call(
                 _far_proj_kernel,
-                (field_shape, q_shape),
-                (part, qs, cp, eb, cst, pb),
+                (field_shape, send_shape),
+                (part, qs, cp, eb, cst, pb, rr),
                 8 * cp.size,
                 "far_proj",
             )

time: 116 us -> 104 us (0.90)
  local copies, waits for them, and re-layouts: 24.2 us -> 10.1 us
  Pallas kernels: 42.2 us -> 45.1 us
    gather x6 -> x4, local copies, waits for them, and re-layouts: 18.2 us -> 7.26 us  [_exchange(): return got[idx].T]
    unnamed x6 -> x2, local copies, waits for them, and re-layouts: 2.97 us -> 0.01 us
    pallas_call x6 -> x7, Pallas kernels: 42.2 us -> 45.1 us  [_call(): pl.pallas_call(kernel, out_shape=outs, compiler_params=pltpu.CompilerPara...]
    pallas_call x2 -> x0, local copies, waits for them, and re-layouts: 1.59 us -> none  [_call(): pl.pallas_call(kernel, out_shape=outs, compiler_params=pltpu.CompilerPara...]
    reshape x0 -> x3, local copies, waits for them, and re-layouts: none -> 1.5 us  [the longest x1 0.82 us: per_device(): lax.all_to_all(req, 'cells', 0, 0, tiled=True)]
    all_to_all x2 -> x3, other arithmetic: 2.59 us -> 1.97 us  [the longest x2 1.25 us: _exchange(): got = lax.all_to_all(send.reshape(devices, total // devices), 'cells', 0, 0)]
  transfers between devices with their start and end apart: 5 -> 5, of which waited for: 4 -> 4; matrix products, arithmetic and copies ran while one was open for 2% -> 1% of each run, Pallas kernels for 23% -> 25%
where the time goes in v3:
time: 104 us; the launch traced here: 103 us
  Pallas kernels  45.1 us (43%)
  starting transfers between devices  33.3 us (32%)
  local copies, waits for them, and re-layouts  10.1 us (10%)
  waiting for transfers between devices  9.47 us (9%)
  other arithmetic  4 us (4%)
    pallas_call x7, Pallas kernels, _call(): pl.pallas_call(kernel, out_shape=outs, compiler_params=pltpu.CompilerPara...  45.1 us
    all_to_all x2, starting transfers between devices, _exchange(): got = lax.all_to_all(send.reshape(devices, total // devices), 'cells', 0, 0)  16.5 us
    all_to_all x1, starting transfers between devices, per_device(): lax.all_to_all(req, 'cells', 0, 0, tiled=True)  12.2 us
    gather x4, local copies, waits for them, and re-layouts, _exchange(): return got[idx].T  7.26 us
    ppermute x2, waiting for transfers between devices, per_device(): lax.ppermute(total, 'freq', [(i, i ^ hop) for i in range(freqs)])  4.65 us
    ppermute x2, starting transfers between devices, per_device(): lax.ppermute(total, 'freq', [(i, i ^ hop) for i in range(freqs)])  4.54 us
    all_to_all x1, waiting for transfers between devices, per_device(): lax.all_to_all(req, 'cells', 0, 0, tiled=True)  4.11 us
  transfers between devices with their start and end apart: 5, of which 4 were waited for; matrix products, arithmetic and copies ran while one was open for 1% of the time, Pallas kernels for 25%

profile of v3, /device:TPU:8, one launch (start us, length us, event | category | flops | bytes accessed | tf_op | source)
XLA Modules:
  0.0 102.7 jit_solution(14260368739195845210)
XLA Ops:
  0.6 1.9 %prep.1 = (s32[1,1024]{1,0:T(1,128)}, f32[64,32]{1,0:T(8,128)}) custom-call(s32[1,1024]{1,0:T(1,128)} %bitcast.44, s32[1,1024]{1,0:T(1,128)} %bitcast.45), custom_call_target="tpu_custom_call" | custom-call | flops 134217728 | bytes 20480 | tf_op jit(solution)/shard_map/prep/pallas_call | solution.py:218
  2.5 0.0 copy-start
  2.5 12.2 %all-to-all-start = ((f32[64,1,32]{2,1,0:T(1,128)}), f32[64,1,32]{2,1,0:T(1,128)S(1)}, u32[]{:S(2)}, u32[]{:S(2)}) async-start(f32[64,1,32]{2,1,0:T(1,128)} %bitcast.39), calls=%async_computation | async-start | bytes 65536 | tf_op jit(solution)/shard_map/all_to_all | solution.py:276
  14.8 4.4 %proj.1.q_ref = f32[32,64]{1,0:T(8,128)} custom-call(f32[2,4096]{1,0:T(2,128)} %bitcast.31, f32[1,4096]{1,0:T(1,128)} %c_ref.7, f32[2,16,4096]{2,1,0:T(8,128)} %bitcast.26), custom_call_target="tpu_custom_call" | custom-call | flops 524288 | bytes 581632 | tf_op jit(solution)/shard_map/proj/pallas_call | solution.py:218
  19.2 4.1 %all-to-all-done = f32[64,1,32]{2,1,0:T(1,128)S(1)} async-done(((f32[64,1,32]{2,1,0:T(1,128)}), f32[64,1,32]{2,1,0:T(1,128)S(1)}, u32[]{:S(2)}, u32[]{:S(2)}) %all-to-all-start) | async-done | bytes 8224 | tf_op jit(solution)/shard_map/all_to_all | solution.py:276
  23.3 0.5 broadcast.35
  23.8 0.7 reduce.5
  24.6 0.8 reshape.69.rr_ref
  25.4 2.2 %pack.1 = f32[512,128]{1,0:T(8,128)} custom-call(f32[32,64]{1,0:T(8,128)} %proj.1.q_ref, f32[512,4]{1,0:T(8,128)} %reshape.69.rr_ref), custom_call_target="tpu_custom_call" | custom-call | flops 8388608 | bytes 278528 | tf_op jit(solution)/shard_map/pack/pallas_call | solution.py:218
  27.6 6.2 %all-to-all-start.1 = ((f32[64,1,1024]{2,1,0:T(1,128)}), f32[64,1,1024]{2,1,0:T(1,128)S(1)}, u32[]{:S(2)}, u32[]{:S(2)}) async-start(f32[64,1,1024]{2,1,0:T(1,128)} %bitcast.30), calls=%async_computation.1 | async-start | bytes 524288 | tf_op jit(solution)/shard_map/all_to_all | solution.py:229
  33.8 0.7 subtract_bitcast_fusion
  34.5 0.1 broadcast_in_dim.8
  34.6 0.7 reshape.66.nlc_ref
  35.3 10.8 %near.2.part_ref = f32[2,4096]{1,0:T(2,128)} custom-call(f32[2,4096]{1,0:T(2,128)} %bitcast.32, f32[1,4096]{1,0:T(1,128)} %c_ref.7, f32[2,192,4096]{2,1,0:T(8,128)} %bitcast.22, s32[3,4096]{1,0:T(4,128)} %reshape.66.nlc_ref, f32[2,4096]{1,0:T(2,128)} %bitcast.33), custom_call_target="tpu_custom_call" | custom-call | flops 6291456 | bytes 6455296 | tf_op jit(solution)/shard_map/near/pallas_call | solution.py:218
  46.1 0.0 copy-done
  46.2 0.0 all-to-all-done.1
  46.2 0.6 reduce.1
  46.8 0.3 reshape.70
  47.1 2.8 %gather_fusion = f32[1024,32]{1,0:T(8,128)S(1)} fusion(f32[2048,32]{1,0:T(8,128)S(1)} %reshape.70, s32[1024]{0:T(1024)S(1)} %broadcast_clamp_fusion), kind=kCustom, calls=%fused_computation | custom fusion | bytes 266240 | tf_op jit(solution)/shard_map/gather | solution.py:231
  50.0 0.8 copy.18
  50.8 8.9 %far_proj.1 = (f32[2,4096]{1,0:T(2,128)}, f32[512,128]{1,0:T(8,128)}) custom-call(f32[2,4096]{1,0:T(2,128)} %near.2.part_ref, f32[32,1024]{1,0:T(8,128)} %bitcast.35, f32[2,16,16,1024]{3,2,1,0:T(8,128)} %bitcast.24, f32[2,16,4096]{2,1,0:T(8,128)} %bitcast.28, f32[1,4096]{1,0:T(1,128)} %c_ref.7, f32[2,16,4096]{2,1,0:T(8,128)} %bitcast.27, ...), custom_call_target="tpu_custom_call" | custom-call | flops 4194304 | bytes 3629056 | tf_op jit(solution)/shard_map/far_proj/pallas_call | solution.py:218
  59.7 10.3 %all-to-all-start.2 = ((f32[64,1,1024]{2,1,0:T(1,128)}), f32[64,1,1024]{2,1,0:T(1,128)S(1)}, u32[]{:S(2)}, u32[]{:S(2)}) async-start(f32[64,1,1024]{2,1,0:T(1,128)} %bitcast.37), calls=%async_computation.2 | async-start | bytes 524288 | tf_op jit(solution)/shard_map/all_to_all | solution.py:229
  70.0 10.8 %near.3.part_ref = f32[2,4096]{1,0:T(2,128)} custom-call(f32[2,4096]{1,0:T(2,128)} %get-tuple-element.10.u_ref, f32[1,4096]{1,0:T(1,128)} %c_ref.7, f32[2,192,4096]{2,1,0:T(8,128)} %bitcast.23, s32[3,4096]{1,0:T(4,128)} %reshape.66.nlc_ref, f32[2,4096]{1,0:T(2,128)} %bitcast.34), custom_call_target="tpu_custom_call" | custom-call | flops 6291456 | bytes 6455296 | tf_op jit(solution)/shard_map/near/pallas_call | solution.py:218
  80.8 0.7 all-to-all-done.2
  81.6 0.6 reduce.2
  82.2 0.3 reshape.72
  82.5 2.8 %gather_fusion.1 = f32[1024,32]{1,0:T(8,128)S(1)} fusion(f32[2048,32]{1,0:T(8,128)S(1)} %reshape.72, s32[1024]{0:T(1024)S(1)} %broadcast_clamp_fusion), kind=kCustom, calls=%fused_computation.1 | custom fusion | bytes 266240 | tf_op jit(solution)/shard_map/gather | solution.py:231
  85.3 0.8 copy.20
  86.2 6.0 %far_grad.1 = (f32[2,4096]{1,0:T(2,128)}, f32[1,4096]{1,0:T(1,128)}) custom-call(f32[2,4096]{1,0:T(2,128)} %near.3.part_ref, f32[32,1024]{1,0:T(8,128)} %bitcast.36, f32[2,16,16,1024]{3,2,1,0:T(8,128)} %bitcast.25, f32[2,16,4096]{2,1,0:T(8,128)} %bitcast.29, f32[2,4096]{1,0:T(2,128)} %bitcast.38), custom_call_target="tpu_custom_call" | custom-call | flops 4194304 | bytes 2867200 | tf_op jit(solution)/shard_map/far_grad/pallas_call | solution.py:218
  92.2 1.5 %collective-permute-start = (f32[4096]{0:T(1024)}, f32[4096]{0:T(1024)S(1)}, u32[]{:S(2)}, u32[]{:S(2)}) collective-permute-start(f32[4096]{0:T(1024)} %bitcast.40), channel_id=1, source_target_pairs={{0,1},{1,0},{2,3},{3,2},{4,5},{5,4},{6,7},{7,6},{8,9},{9,8},{10,11... | collective-permute-start | bytes 49160 | tf_op jit(solution)/shard_map/ppermute | solution.py:313
  93.7 2.4 %collective-permute-done = f32[4096]{0:T(1024)S(1)} collective-permute-done((f32[4096]{0:T(1024)}, f32[4096]{0:T(1024)S(1)}, u32[]{:S(2)}, u32[]{:S(2)}) %collective-permute-start) | collective-permute-done | bytes 16416 | tf_op jit(solution)/shard_map/ppermute | solution.py:313
  96.1 0.7 add.18
  96.9 3.0 %collective-permute-start.1 = (f32[4096]{0:T(1024)S(1)}, f32[4096]{0:T(1024)S(1)}, u32[]{:S(2)}, u32[]{:S(2)}) collective-permute-start(f32[4096]{0:T(1024)S(1)} %add.18), channel_id=1, source_target_pairs={{0,2},{1,3},{2,0},{3,1},{4,6},{5,7},{6,4},{7,5},{8,10},{9,11},{10,... | collective-permute-start | bytes 49160 | tf_op jit(solution)/shard_map/ppermute | solution.py:313
  99.9 2.2 %collective-permute-done.1 = f32[4096]{0:T(1024)S(1)} collective-permute-done((f32[4096]{0:T(1024)S(1)}, f32[4096]{0:T(1024)S(1)}, u32[]{:S(2)}, u32[]{:S(2)}) %collective-permute-start.1) | collective-permute-done | bytes 16416 | tf_op jit(solution)/shard_map/ppermute | solution.py:313
  102.1 0.6 add.19
  (2 shorter events, 0.0 us)
Async XLA Ops:
  2.5 43.6 %copy-start = (s32[1,1024]{1,0:T(1,128)S(1)}, s32[1,1024]{1,0:T(1,128)}, u32[]{:S(2)}) copy-start(s32[1,1024]{1,0:T(1,128)} %get-tuple-element.9) | copy-start | bytes 12292
  2.5 20.8 %all-to-all-start = ((f32[64,1,32]{2,1,0:T(1,128)}), f32[64,1,32]{2,1,0:T(1,128)S(1)}, u32[]{:S(2)}, u32[]{:S(2)}) async-start(f32[64,1,32]{2,1,0:T(1,128)} %bitcast.39), calls=%async_computation | async-start | bytes 65536 | tf_op jit(solution)/shard_map/all_to_all | solution.py:276
  27.6 18.6 %all-to-all-start.1 = ((f32[64,1,1024]{2,1,0:T(1,128)}), f32[64,1,1024]{2,1,0:T(1,128)S(1)}, u32[]{:S(2)}, u32[]{:S(2)}) async-start(f32[64,1,1024]{2,1,0:T(1,128)} %bitcast.30), calls=%async_computation.1 | async-start | bytes 524288 | tf_op jit(solution)/shard_map/all_to_all | solution.py:229
  59.7 21.9 %all-to-all-start.2 = ((f32[64,1,1024]{2,1,0:T(1,128)}), f32[64,1,1024]{2,1,0:T(1,128)S(1)}, u32[]{:S(2)}, u32[]{:S(2)}) async-start(f32[64,1,1024]{2,1,0:T(1,128)} %bitcast.37), calls=%async_computation.2 | async-start | bytes 524288 | tf_op jit(solution)/shard_map/all_to_all | solution.py:229
  92.2 3.9 %collective-permute-start = (f32[4096]{0:T(1024)}, f32[4096]{0:T(1024)S(1)}, u32[]{:S(2)}, u32[]{:S(2)}) collective-permute-start(f32[4096]{0:T(1024)} %bitcast.40), channel_id=1, source_target_pairs={{0,1},{1,0},{2,3},{3,2},{4,5},{5,4},{6,7},{7,6},{8,9},{9,8},{10,11... | collective-permute-start | bytes 49160 | tf_op jit(solution)/shard_map/ppermute | solution.py:313
  96.9 5.2 %collective-permute-start.1 = (f32[4096]{0:T(1024)S(1)}, f32[4096]{0:T(1024)S(1)}, u32[]{:S(2)}, u32[]{:S(2)}) collective-permute-start(f32[4096]{0:T(1024)S(1)} %add.18), channel_id=1, source_target_pairs={{0,2},{1,3},{2,0},{3,1},{4,6},{5,7},{6,4},{7,5},{8,10},{9,11},{10,... | collective-permute-start | bytes 49160 | tf_op jit(solution)/shard_map/ppermute | solution.py:313

commit v4 on v3

--- a/solution.py
+++ b/solution.py
@@ -47,13 +47,12 @@
     return _xdot(pw, seg.astype(BF16))
 
 
-def _pack(q, rr_ref):
+def _pack(q, rr):
     rank2, clusters = q.shape
-    rows, groups = rr_ref.shape
+    rows, groups = rr.shape
     wide = groups * clusters
     lane = _iota((rows, wide), 1)
     grp = lane // clusters
-    rr = rr_ref[...]
     want = rr[:, 0:1]
     for g in range(1, groups):
         want = jnp.where(grp == g, rr[:, g : g + 1], want)
@@ -68,8 +67,30 @@
     return r[:, :n] + r[:, n : 2 * n] + r[:, 2 * n :]
 
 
-def _pack_kernel(q_ref, rr_ref, send_ref):
-    send_ref[...] = _pack(q_ref[...], rr_ref)
+def _proj_pack_kernel(u_ref, c_ref, p_ref, req_ref, send_ref):
+    cells = u_ref.shape[1]
+    clusters = cells // 64
+    rank2 = 2 * p_ref.shape[1]
+    devices, cap = req_ref.shape
+    groups = 4
+    lanes = groups * rank2
+
+    def body(ci, q):
+        off = pl.multiple_of(ci * CHUNK, CHUNK)
+        sl = pl.ds(off, CHUNK)
+        pw = _weighted_proj(u_ref[:, sl], c_ref[:, sl], p_ref[0, :, sl], p_ref[1, :, sl])
+        return q + _proj_chunk(pw, off, clusters, 64)
+
+    q = lax.fori_loop(0, cells // CHUNK, body, jnp.zeros((rank2, clusters), F32))
+    nrow = clusters // groups
+    order = (_iota((nrow, groups), 0) * groups + _iota((nrow, groups), 1)).astype(F32)
+    flat = _pack(q, order)
+    place = (_iota((cap, lanes), 0) == _iota((cap, lanes), 1)).astype(BF16)
+    reqrow = jnp.dot(req_ref[...].astype(BF16), place, preferred_element_type=F32)
+    block = nrow + 1
+    for e in range(devices):
+        send_ref[pl.ds(e * block, nrow), :] = flat
+        send_ref[pl.ds(e * block + nrow, 1), :] = reqrow[e : e + 1]
 
 
 def _proj_kernel(u_ref, c_ref, p_ref, q_ref):
@@ -180,7 +201,7 @@
 
     body = _far_common(part_ref, qs_ref, cpl_ref, e_ref, u_ref, tail)
     q = lax.fori_loop(0, cells // CHUNK, body, jnp.zeros((rank2, clusters), F32))
-    send_ref[...] = _pack(q, rr_ref)
+    send_ref[...] = _pack(q, rr_ref[...])
 
 
 def _far_grad_kernel(part_ref, qs_ref, cpl_ref, e_ref, bg_ref, u_ref, t_ref):
@@ -229,6 +250,16 @@
     got = lax.all_to_all(send.reshape(devices, total // devices), "cells", 0, 0)
     got = got.reshape(devices * cap, total // (devices * cap))
     return got[idx].T
+
+
+def _exchange_all(send, devices, clusters, rank2, cap, groups, src_index):
+    total = send.size
+    got = lax.all_to_all(send.reshape(devices, total // devices), "cells", 0, 0)
+    lanes = send.shape[1]
+    got = got.reshape(devices, total // (devices * lanes), lanes)
+    rr = got[:, -1, :cap].reshape(devices * cap // groups, groups)
+    table = got[:, :-1, :].reshape(devices * clusters, rank2)
+    return table[src_index].T, rr
 
 
 def per_device(
@@ -273,20 +304,23 @@
         "prep",
     )
     groups = 4
-    rr = lax.all_to_all(req, "cells", 0, 0, tiled=True).reshape(devices * cap // groups, groups)
     idx = idx.reshape(npairs)
+    src_index = far_owner[:, 0] * clusters + far_slot
 
     nsend = devices * cap
     rank2 = 2 * pb.shape[1]
     q_shape = jax.ShapeDtypeStruct((rank2, clusters), F32)
     field_shape = jax.ShapeDtypeStruct((2, cells), F32)
 
-    q = _call(_proj_kernel, q_shape, (src, cst, pb), 4 * rank2 * cells, "proj")
+    first_shape = jax.ShapeDtypeStruct((devices * (clusters // groups + 1), groups * rank2), F32)
+    send = _call(_proj_pack_kernel, first_shape, (src, cst, pb, req), 4 * rank2 * cells, "proj_pack")
     send_shape = jax.ShapeDtypeStruct((devices * cap // groups, groups * rank2), F32)
-    send = _call(_pack_kernel, send_shape, (q, rr), 2 * send_shape.size * clusters, "pack")
     field = src
     for step in range(ITERS):
-        qs = _exchange(send, idx, devices, cap)
+        if step == 0:
+            qs, rr = _exchange_all(send, devices, clusters, rank2, cap, groups, src_index)
+        else:
+            qs = _exchange(send, idx, devices, cap)
         part = _call(
             _near_kernel, field_shape, (field, cst, nb, nlc, src), 8 * nb.shape[1] * cells, "near"
         )

time: 104 us -> 92.9 us (0.89)
  starting transfers between devices: 33.3 us -> 23.6 us
  Pallas kernels: 45.1 us -> 43.6 us
  waiting for transfers between devices: 9.47 us -> 10.9 us
    all_to_all x2 -> x1, starting transfers between devices: 16.5 us -> 6.96 us  [_exchange(): got = lax.all_to_all(send.reshape(devices, total // devices), 'cells', 0, 0)]
    gather x0 -> x2, local copies, waits for them, and re-layouts: none -> 3.64 us  [_exchange_all(): return (table[src_index].T, rr)]
    gather x4 -> x2, local copies, waits for them, and re-layouts: 7.26 us -> 3.64 us  [_exchange(): return got[idx].T]
    pallas_call x7 -> x6, Pallas kernels: 45.1 us -> 43.6 us  [_call(): pl.pallas_call(kernel, out_shape=outs, compiler_params=pltpu.CompilerPara...]
    all_to_all x1, waiting for transfers between devices: 4.11 us -> 5.56 us  [_exchange_all(): got = lax.all_to_all(send.reshape(devices, total // devices), 'cells', 0, 0)]
  transfers between devices with their start and end apart: 5 -> 4, of which waited for: 4 -> 4; matrix products, arithmetic and copies ran while one was open for 1% -> 1% of each run, Pallas kernels for 25% -> 24%
where the time goes in v4:
time: 92.9 us; the launch traced here: 92 us
  Pallas kernels  43.6 us (47%)
  starting transfers between devices  23.6 us (25%)
  waiting for transfers between devices  10.9 us (12%)
  local copies, waits for them, and re-layouts  9.94 us (11%)
  other arithmetic  3.29 us (4%)
    pallas_call x6, Pallas kernels, _call(): pl.pallas_call(kernel, out_shape=outs, compiler_params=pltpu.CompilerPara...  43.6 us
    all_to_all x1, starting transfers between devices, _exchange_all(): got = lax.all_to_all(send.reshape(devices, total // devices), 'cells', 0, 0)  12.1 us
    all_to_all x1, starting transfers between devices, _exchange(): got = lax.all_to_all(send.reshape(devices, total // devices), 'cells', 0, 0)  6.96 us
    all_to_all x1, waiting for transfers between devices, _exchange_all(): got = lax.all_to_all(send.reshape(devices, total // devices), 'cells', 0, 0)  5.56 us
    ppermute x2, waiting for transfers between devices, per_device(): lax.ppermute(total, 'freq', [(i, i ^ hop) for i in range(freqs)])  4.68 us
    ppermute x2, starting transfers between devices, per_device(): lax.ppermute(total, 'freq', [(i, i ^ hop) for i in range(freqs)])  4.51 us
    gather x2, local copies, waits for them, and re-layouts, _exchange(): return got[idx].T  3.64 us
    gather x2, local copies, waits for them, and re-layouts, _exchange_all(): return (table[src_index].T, rr)  3.64 us
  transfers between devices with their start and end apart: 4, of which 4 were waited for; matrix products, arithmetic and copies ran while one was open for 1% of the time, Pallas kernels for 24%

profile of v4, /device:TPU:8, one launch (start us, length us, event | category | flops | bytes accessed | tf_op | source)
XLA Modules:
  0.0 92.0 jit_solution(2723999311294490716)
XLA Ops:
  0.6 0.0 copy-start.3
  0.6 1.9 %prep.1 = (s32[1,1024]{1,0:T(1,128)}, f32[64,32]{1,0:T(8,128)}) custom-call(s32[1,1024]{1,0:T(1,128)} %bitcast.42, s32[1,1024]{1,0:T(1,128)} %bitcast.41), custom_call_target="tpu_custom_call" | custom-call | flops 134217728 | bytes 20480 | tf_op jit(solution)/shard_map/prep/pallas_call | solution.py:239
  2.5 5.0 %proj_pack.1 = f32[1088,128]{1,0:T(8,128)} custom-call(f32[2,4096]{1,0:T(2,128)} %bitcast.29, f32[1,4096]{1,0:T(1,128)} %c_ref.7, f32[2,16,4096]{2,1,0:T(8,128)} %bitcast.25, f32[64,32]{1,0:T(8,128)} %get-tuple-element.8.req_ref), custom_call_target="tpu_custom_call" | custom-call | flops 524288 | bytes 1138688 | tf_op jit(solution)/shard_map/proj_pack/pallas_call | solution.py:239
  7.5 12.1 %all-to-all-start = ((f32[64,1,2176]{2,1,0:T(1,128)}), f32[64,1,2176]{2,1,0:T(1,128)S(1)}, u32[]{:S(2)}, u32[]{:S(2)}) async-start(f32[64,1,2176]{2,1,0:T(1,128)} %bitcast.24), calls=%async_computation | async-start | bytes 1114112 | tf_op jit(solution)/shard_map/all_to_all | solution.py:257
  19.6 0.0 copy-done.3
  19.7 0.1 broadcast_in_dim.10
  19.7 0.7 reshape.65.nlc_ref
  20.5 0.0 copy-start.1
  20.5 0.0 copy-start
  20.5 10.9 %near.2.part_ref = f32[2,4096]{1,0:T(2,128)} custom-call(f32[2,4096]{1,0:T(2,128)} %bitcast.30, f32[1,4096]{1,0:T(1,128)} %c_ref.7, f32[2,192,4096]{2,1,0:T(8,128)} %bitcast.20, s32[3,4096]{1,0:T(4,128)} %reshape.65.nlc_ref, f32[2,4096]{1,0:T(2,128)} %bitcast.31), custom_call_target="tpu_custom_call" | custom-call | flops 6291456 | bytes 6455296 | tf_op jit(solution)/shard_map/near/pallas_call | solution.py:239
  31.4 0.0 copy-done.1
  31.4 0.0 copy-done
  31.4 5.6 %all-to-all-done = f32[64,1,2176]{2,1,0:T(1,128)S(1)} async-done(((f32[64,1,2176]{2,1,0:T(1,128)}), f32[64,1,2176]{2,1,0:T(1,128)S(1)}, u32[]{:S(2)}, u32[]{:S(2)}) %all-to-all-start) | async-done | bytes 557088 | tf_op jit(solution)/shard_map/all_to_all | solution.py:257
  37.0 1.3 %reduce = f32[64,2176]{1,0:T(8,128)S(1)} reduce(f32[64,1,2176]{2,1,0:T(1,128)S(1)} %all-to-all-done, f32[]{:T(128)} %constant.22), dimensions={1}, to_apply=%all_to_all.13.reduce_sub_computation | reduce | bytes 1114116 | tf_op jit(solution)/shard_map/all_to_all | solution.py:257
  38.3 0.1 reshape.68
  38.4 0.1 slice_reduce_fusion
  38.5 0.8 reshape_squeeze.3.rr_ref
  39.3 0.5 reshape.69
  39.8 2.8 %gather_fusion = f32[1024,32]{1,0:T(8,128)S(1)} fusion(f32[4096,32]{1,0:T(8,128)S(1)} %reshape.69, s32[1024]{0:T(1024)S(1)} %fusion), kind=kCustom, calls=%fused_computation | custom fusion | bytes 266240 | tf_op jit(solution)/shard_map/gather | solution.py:262
  42.6 0.8 copy.18
  43.4 0.0 copy-start.2
  43.4 8.9 %far_proj.1 = (f32[2,4096]{1,0:T(2,128)}, f32[512,128]{1,0:T(8,128)}) custom-call(f32[2,4096]{1,0:T(2,128)} %near.2.part_ref, f32[32,1024]{1,0:T(8,128)} %bitcast.33, f32[2,16,16,1024]{3,2,1,0:T(8,128)} %bitcast.22, f32[2,16,4096]{2,1,0:T(8,128)} %bitcast.27, f32[1,4096]{1,0:T(1,128)} %c_ref.7, f32[2,16,4096]{2,1,0:T(8,128)} %bitcast.26, ...), custom_call_target="tpu_custom_call" | custom-call | flops 4194304 | bytes 3629056 | tf_op jit(solution)/shard_map/far_proj/pallas_call | solution.py:239
  52.4 7.0 %all-to-all-start.1 = ((f32[64,1,1024]{2,1,0:T(1,128)}), f32[64,1,1024]{2,1,0:T(1,128)S(1)}, u32[]{:S(2)}, u32[]{:S(2)}) async-start(f32[64,1,1024]{2,1,0:T(1,128)} %bitcast.35), calls=%async_computation.1 | async-start | bytes 524288 | tf_op jit(solution)/shard_map/all_to_all | solution.py:250
  59.3 0.0 copy-done.2
  59.4 10.9 %near.3.part_ref = f32[2,4096]{1,0:T(2,128)} custom-call(f32[2,4096]{1,0:T(2,128)} %get-tuple-element.9.u_ref, f32[1,4096]{1,0:T(1,128)} %c_ref.7, f32[2,192,4096]{2,1,0:T(8,128)} %bitcast.21, s32[3,4096]{1,0:T(4,128)} %reshape.65.nlc_ref, f32[2,4096]{1,0:T(2,128)} %bitcast.32), custom_call_target="tpu_custom_call" | custom-call | flops 6291456 | bytes 6455296 | tf_op jit(solution)/shard_map/near/pallas_call | solution.py:239
  70.2 0.6 all-to-all-done.1
  70.9 0.6 reduce.2
  71.5 0.3 reshape.70
  71.8 2.8 %gather_fusion.1 = f32[1024,32]{1,0:T(8,128)S(1)} fusion(f32[2048,32]{1,0:T(8,128)S(1)} %reshape.70, s32[1024]{0:T(1024)S(1)} %broadcast_clamp_fusion), kind=kCustom, calls=%fused_computation.1 | custom fusion | bytes 266240 | tf_op jit(solution)/shard_map/gather | solution.py:252
  74.6 0.8 copy.20
  75.5 6.0 %far_grad.1 = (f32[2,4096]{1,0:T(2,128)}, f32[1,4096]{1,0:T(1,128)}) custom-call(f32[2,4096]{1,0:T(2,128)} %near.3.part_ref, f32[32,1024]{1,0:T(8,128)} %bitcast.34, f32[2,16,16,1024]{3,2,1,0:T(8,128)} %bitcast.23, f32[2,16,4096]{2,1,0:T(8,128)} %bitcast.28, f32[2,4096]{1,0:T(2,128)} %bitcast.36), custom_call_target="tpu_custom_call" | custom-call | flops 4194304 | bytes 2867200 | tf_op jit(solution)/shard_map/far_grad/pallas_call | solution.py:239
  81.5 1.5 %collective-permute-start = (f32[4096]{0:T(1024)}, f32[4096]{0:T(1024)S(1)}, u32[]{:S(2)}, u32[]{:S(2)}) collective-permute-start(f32[4096]{0:T(1024)} %bitcast.37), channel_id=1, source_target_pairs={{0,1},{1,0},{2,3},{3,2},{4,5},{5,4},{6,7},{7,6},{8,9},{9,8},{10,11... | collective-permute-start | bytes 49160 | tf_op jit(solution)/shard_map/ppermute | solution.py:347
  83.0 2.5 %collective-permute-done = f32[4096]{0:T(1024)S(1)} collective-permute-done((f32[4096]{0:T(1024)}, f32[4096]{0:T(1024)S(1)}, u32[]{:S(2)}, u32[]{:S(2)}) %collective-permute-start) | collective-permute-done | bytes 16416 | tf_op jit(solution)/shard_map/ppermute | solution.py:347
  85.5 0.7 add.33
  86.2 3.0 %collective-permute-start.1 = (f32[4096]{0:T(1024)S(1)}, f32[4096]{0:T(1024)S(1)}, u32[]{:S(2)}, u32[]{:S(2)}) collective-permute-start(f32[4096]{0:T(1024)S(1)} %add.33), channel_id=1, source_target_pairs={{0,2},{1,3},{2,0},{3,1},{4,6},{5,7},{6,4},{7,5},{8,10},{9,11},{10,... | collective-permute-start | bytes 49160 | tf_op jit(solution)/shard_map/ppermute | solution.py:347
  89.2 2.2 %collective-permute-done.1 = f32[4096]{0:T(1024)S(1)} collective-permute-done((f32[4096]{0:T(1024)S(1)}, f32[4096]{0:T(1024)S(1)}, u32[]{:S(2)}, u32[]{:S(2)}) %collective-permute-start.1) | collective-permute-done | bytes 16416 | tf_op jit(solution)/shard_map/ppermute | solution.py:347
  91.4 0.6 add.34
  (6 shorter events, 0.1 us)
Async XLA Ops:
  0.6 19.0 %copy-start.3 = (s32[64,3]{0,1:T(4,128)S(1)}, s32[64,3]{0,1:T(4,128)}, u32[]{:S(2)}) copy-start(s32[64,3]{0,1:T(4,128)} %param.14) | copy-start | bytes 2308
  7.5 29.4 %all-to-all-start = ((f32[64,1,2176]{2,1,0:T(1,128)}), f32[64,1,2176]{2,1,0:T(1,128)S(1)}, u32[]{:S(2)}, u32[]{:S(2)}) async-start(f32[64,1,2176]{2,1,0:T(1,128)} %bitcast.24), calls=%async_computation | async-start | bytes 1114112 | tf_op jit(solution)/shard_map/all_to_all | solution.py:257
  20.5 10.9 %copy-start.1 = (s32[1024,1]{0,1:T(1,128)S(1)}, s32[1024,1]{0,1:T(1,128)}, u32[]{:S(2)}) copy-start(s32[1024,1]{0,1:T(1,128)} %param.18) | copy-start | bytes 12292
  20.5 10.9 %copy-start = (s32[1024]{0:T(1024)S(1)}, s32[1024]{0:T(1024)}, u32[]{:S(2)}) copy-start(s32[1024]{0:T(1024)} %param.19) | copy-start | bytes 12292
  43.4 15.9 %copy-start.2 = (s32[1,1024]{1,0:T(1,128)S(1)}, s32[1,1024]{1,0:T(1,128)}, u32[]{:S(2)}) copy-start(s32[1,1024]{1,0:T(1,128)} %get-tuple-element.11) | copy-start | bytes 12292
  52.4 18.5 %all-to-all-start.1 = ((f32[64,1,1024]{2,1,0:T(1,128)}), f32[64,1,1024]{2,1,0:T(1,128)S(1)}, u32[]{:S(2)}, u32[]{:S(2)}) async-start(f32[64,1,1024]{2,1,0:T(1,128)} %bitcast.35), calls=%async_computation.1 | async-start | bytes 524288 | tf_op jit(solution)/shard_map/all_to_all | solution.py:250
  81.5 3.9 %collective-permute-start = (f32[4096]{0:T(1024)}, f32[4096]{0:T(1024)S(1)}, u32[]{:S(2)}, u32[]{:S(2)}) collective-permute-start(f32[4096]{0:T(1024)} %bitcast.37), channel_id=1, source_target_pairs={{0,1},{1,0},{2,3},{3,2},{4,5},{5,4},{6,7},{7,6},{8,9},{9,8},{10,11... | collective-permute-start | bytes 49160 | tf_op jit(solution)/shard_map/ppermute | solution.py:347
  86.2 5.2 %collective-permute-start.1 = (f32[4096]{0:T(1024)S(1)}, f32[4096]{0:T(1024)S(1)}, u32[]{:S(2)}, u32[]{:S(2)}) collective-permute-start(f32[4096]{0:T(1024)S(1)} %add.33), channel_id=1, source_target_pairs={{0,2},{1,3},{2,0},{3,1},{4,6},{5,7},{6,4},{7,5},{8,10},{9,11},{10,... | collective-permute-start | bytes 49160 | tf_op jit(solution)/shard_map/ppermute | solution.py:347

commit v5 on v4

--- a/solution.py
+++ b/solution.py
@@ -341,11 +341,16 @@
                 "far_grad",
             )
     freqs = lax.axis_size("freq")
-    total = terms[0]
-    hop = 1
-    while hop < freqs:
-        total = total + lax.ppermute(total, "freq", [(i, i ^ hop) for i in range(freqs)])
-        hop *= 2
+    mine = terms[0]
+    got = [mine] + [
+        lax.ppermute(mine, "freq", [(i, (i + k) % freqs) for i in range(freqs)])
+        for k in range(1, freqs)
+    ]
+    stacked = jnp.stack(got)
+    f = lax.axis_index("freq")
+    total = stacked[(f - 0) % freqs]
+    for src in range(1, freqs):
+        total = total + stacked[(f - src) % freqs]
     return (field[None], total)
 
 

time: 92.9 us -> 92.1 us (level)
    ppermute x2 -> x3, waiting for transfers between devices: 4.68 us -> 4.27 us  [per_device(): lax.ppermute(mine, 'freq', [(i, (i + k) % freqs) for i in range(freqs)])]
    ppermute x2 -> x3, starting transfers between devices: 4.51 us -> 4.45 us  [per_device(): lax.ppermute(mine, 'freq', [(i, (i + k) % freqs) for i in range(freqs)])]
  transfers between devices with their start and end apart: 4 -> 5, of which waited for: 4 -> 4; matrix products, arithmetic and copies ran while one was open for 1% -> 1% of each run, Pallas kernels for 24% -> 24%
where the time goes in v5:
time: 92.1 us; the launch traced here: 91.7 us
  Pallas kernels  43.6 us (47%)
  starting transfers between devices  23.5 us (26%)
  waiting for transfers between devices  10.5 us (11%)
  local copies, waits for them, and re-layouts  9.91 us (11%)
  other arithmetic  3.41 us (4%)
    pallas_call x6, Pallas kernels, _call(): pl.pallas_call(kernel, out_shape=outs, compiler_params=pltpu.CompilerPara...  43.6 us
    all_to_all x1, starting transfers between devices, _exchange_all(): got = lax.all_to_all(send.reshape(devices, total // devices), 'cells', 0, 0)  12.1 us
    all_to_all x1, starting transfers between devices, _exchange(): got = lax.all_to_all(send.reshape(devices, total // devices), 'cells', 0, 0)  6.95 us
    all_to_all x1, waiting for transfers between devices, _exchange_all(): got = lax.all_to_all(send.reshape(devices, total // devices), 'cells', 0, 0)  5.57 us
    ppermute x3, starting transfers between devices, per_device(): lax.ppermute(mine, 'freq', [(i, (i + k) % freqs) for i in range(freqs)])  4.45 us
    ppermute x3, waiting for transfers between devices, per_device(): lax.ppermute(mine, 'freq', [(i, (i + k) % freqs) for i in range(freqs)])  4.27 us
    gather x2, local copies, waits for them, and re-layouts, _exchange_all(): return (table[src_index].T, rr)  3.63 us
    gather x2, local copies, waits for them, and re-layouts, _exchange(): return got[idx].T  3.63 us
  transfers between devices with their start and end apart: 5, of which 4 were waited for; matrix products, arithmetic and copies ran while one was open for 1% of the time, Pallas kernels for 24%

profile of v5, /device:TPU:8, one launch (start us, length us, event | category | flops | bytes accessed | tf_op | source)
XLA Modules:
  0.0 91.7 jit_solution(6722932036073402037)
XLA Ops:
  0.6 0.0 copy-start.3
  0.6 1.9 %prep.1 = (s32[1,1024]{1,0:T(1,128)}, f32[64,32]{1,0:T(8,128)}) custom-call(s32[1,1024]{1,0:T(1,128)} %bitcast.51, s32[1,1024]{1,0:T(1,128)} %bitcast.50), custom_call_target="tpu_custom_call" | custom-call | flops 134217728 | bytes 20480 | tf_op jit(solution)/shard_map/prep/pallas_call | solution.py:239
  2.5 5.0 %proj_pack.1 = f32[1088,128]{1,0:T(8,128)} custom-call(f32[2,4096]{1,0:T(2,128)} %bitcast.33, f32[1,4096]{1,0:T(1,128)} %c_ref.7, f32[2,16,4096]{2,1,0:T(8,128)} %bitcast.29, f32[64,32]{1,0:T(8,128)} %get-tuple-element.8.req_ref), custom_call_target="tpu_custom_call" | custom-call | flops 524288 | bytes 1138688 | tf_op jit(solution)/shard_map/proj_pack/pallas_call | solution.py:239
  7.5 12.1 %all-to-all-start = ((f32[64,1,2176]{2,1,0:T(1,128)}), f32[64,1,2176]{2,1,0:T(1,128)S(1)}, u32[]{:S(2)}, u32[]{:S(2)}) async-start(f32[64,1,2176]{2,1,0:T(1,128)} %bitcast.28), calls=%async_computation | async-start | bytes 1114112 | tf_op jit(solution)/shard_map/all_to_all | solution.py:257
  19.6 0.0 copy-done.3
  19.7 0.1 broadcast_in_dim.10
  19.8 0.7 reshape.68.nlc_ref
  20.5 0.0 copy-start.1
  20.5 0.0 copy-start
  20.5 10.9 %near.2.part_ref = f32[2,4096]{1,0:T(2,128)} custom-call(f32[2,4096]{1,0:T(2,128)} %bitcast.34, f32[1,4096]{1,0:T(1,128)} %c_ref.7, f32[2,192,4096]{2,1,0:T(8,128)} %bitcast.24, s32[3,4096]{1,0:T(4,128)} %reshape.68.nlc_ref, f32[2,4096]{1,0:T(2,128)} %bitcast.35), custom_call_target="tpu_custom_call" | custom-call | flops 6291456 | bytes 6455296 | tf_op jit(solution)/shard_map/near/pallas_call | solution.py:239
  31.3 0.0 copy-done.1
  31.4 0.0 copy-done
  31.4 5.6 %all-to-all-done = f32[64,1,2176]{2,1,0:T(1,128)S(1)} async-done(((f32[64,1,2176]{2,1,0:T(1,128)}), f32[64,1,2176]{2,1,0:T(1,128)S(1)}, u32[]{:S(2)}, u32[]{:S(2)}) %all-to-all-start) | async-done | bytes 557088 | tf_op jit(solution)/shard_map/all_to_all | solution.py:257
  37.0 1.3 %reduce = f32[64,2176]{1,0:T(8,128)S(1)} reduce(f32[64,1,2176]{2,1,0:T(1,128)S(1)} %all-to-all-done, f32[]{:T(128)} %constant.59), dimensions={1}, to_apply=%all_to_all.13.reduce_sub_computation | reduce | bytes 1114116 | tf_op jit(solution)/shard_map/all_to_all | solution.py:257
  38.3 0.1 reshape.71
  38.4 0.1 slice_reduce_fusion
  38.5 0.8 reshape_squeeze.3.rr_ref
  39.3 0.5 reshape.72
  39.8 2.8 %gather_fusion = f32[1024,32]{1,0:T(8,128)S(1)} fusion(f32[4096,32]{1,0:T(8,128)S(1)} %reshape.72, s32[1024]{0:T(1024)S(1)} %fusion), kind=kCustom, calls=%fused_computation | custom fusion | bytes 266240 | tf_op jit(solution)/shard_map/gather | solution.py:262
  42.6 0.8 copy.18
  43.4 0.0 copy-start.2
  43.4 8.9 %far_proj.1 = (f32[2,4096]{1,0:T(2,128)}, f32[512,128]{1,0:T(8,128)}) custom-call(f32[2,4096]{1,0:T(2,128)} %near.2.part_ref, f32[32,1024]{1,0:T(8,128)} %bitcast.37, f32[2,16,16,1024]{3,2,1,0:T(8,128)} %bitcast.26, f32[2,16,4096]{2,1,0:T(8,128)} %bitcast.31, f32[1,4096]{1,0:T(1,128)} %c_ref.7, f32[2,16,4096]{2,1,0:T(8,128)} %bitcast.30, ...), custom_call_target="tpu_custom_call" | custom-call | flops 4194304 | bytes 3629056 | tf_op jit(solution)/shard_map/far_proj/pallas_call | solution.py:239
  52.4 7.0 %all-to-all-start.1 = ((f32[64,1,1024]{2,1,0:T(1,128)}), f32[64,1,1024]{2,1,0:T(1,128)S(1)}, u32[]{:S(2)}, u32[]{:S(2)}) async-start(f32[64,1,1024]{2,1,0:T(1,128)} %bitcast.39), calls=%async_computation.1 | async-start | bytes 524288 | tf_op jit(solution)/shard_map/all_to_all | solution.py:250
  59.3 0.0 copy-done.2
  59.4 10.8 %near.3.part_ref = f32[2,4096]{1,0:T(2,128)} custom-call(f32[2,4096]{1,0:T(2,128)} %get-tuple-element.9.u_ref, f32[1,4096]{1,0:T(1,128)} %c_ref.7, f32[2,192,4096]{2,1,0:T(8,128)} %bitcast.25, s32[3,4096]{1,0:T(4,128)} %reshape.68.nlc_ref, f32[2,4096]{1,0:T(2,128)} %bitcast.36), custom_call_target="tpu_custom_call" | custom-call | flops 6291456 | bytes 6455296 | tf_op jit(solution)/shard_map/near/pallas_call | solution.py:239
  70.2 0.6 all-to-all-done.1
  70.9 0.6 reduce.2
  71.5 0.3 reshape.73
  71.8 2.8 %gather_fusion.1 = f32[1024,32]{1,0:T(8,128)S(1)} fusion(f32[2048,32]{1,0:T(8,128)S(1)} %reshape.73, s32[1024]{0:T(1024)S(1)} %broadcast_clamp_fusion), kind=kCustom, calls=%fused_computation.1 | custom fusion | bytes 266240 | tf_op jit(solution)/shard_map/gather | solution.py:252
  74.6 0.8 copy.20
  75.5 6.0 %far_grad.1 = (f32[2,4096]{1,0:T(2,128)}, f32[1,4096]{1,0:T(1,128)}) custom-call(f32[2,4096]{1,0:T(2,128)} %near.3.part_ref, f32[32,1024]{1,0:T(8,128)} %bitcast.38, f32[2,16,16,1024]{3,2,1,0:T(8,128)} %bitcast.27, f32[2,16,4096]{2,1,0:T(8,128)} %bitcast.32, f32[2,4096]{1,0:T(2,128)} %bitcast.40), custom_call_target="tpu_custom_call" | custom-call | flops 4194304 | bytes 2867200 | tf_op jit(solution)/shard_map/far_grad/pallas_call | solution.py:239
  81.5 2.8 %collective-permute-start.2 = (f32[4096]{0:T(1024)}, f32[4096]{0:T(1024)S(1)}, u32[]{:S(2)}, u32[]{:S(2)}) collective-permute-start(f32[4096]{0:T(1024)} %bitcast.44), channel_id=1, source_target_pairs={{0,3},{1,0},{2,1},{3,2},{4,7},{5,4},{6,5},{7,6},{8,11},{9,8},{10,9... | collective-permute-start | bytes 49160 | tf_op jit(solution)/shard_map/ppermute | solution.py:346
  84.3 0.8 collective-permute-start.1
  85.1 0.9 collective-permute-start
  85.9 0.0 collective-permute-done.2
  85.9 3.8 %collective-permute-done.1 = f32[4096]{0:T(1024)S(1)} collective-permute-done((f32[4096]{0:T(1024)}, f32[4096]{0:T(1024)S(1)}, u32[]{:S(2)}, u32[]{:S(2)}) %collective-permute-start.1) | collective-permute-done | bytes 16416 | tf_op jit(solution)/shard_map/ppermute | solution.py:346
  89.7 0.5 collective-permute-done
  90.2 0.8 pad_maximum_fusion
  91.0 0.7 dynamic-slice_add_fusion
  (6 shorter events, 0.1 us)
Async XLA Ops:
  0.6 19.0 %copy-start.3 = (s32[64,3]{0,1:T(4,128)S(1)}, s32[64,3]{0,1:T(4,128)}, u32[]{:S(2)}) copy-start(s32[64,3]{0,1:T(4,128)} %param.14) | copy-start | bytes 2308
  7.5 29.4 %all-to-all-start = ((f32[64,1,2176]{2,1,0:T(1,128)}), f32[64,1,2176]{2,1,0:T(1,128)S(1)}, u32[]{:S(2)}, u32[]{:S(2)}) async-start(f32[64,1,2176]{2,1,0:T(1,128)} %bitcast.28), calls=%async_computation | async-start | bytes 1114112 | tf_op jit(solution)/shard_map/all_to_all | solution.py:257
  20.5 10.9 %copy-start.1 = (s32[1024,1]{0,1:T(1,128)S(1)}, s32[1024,1]{0,1:T(1,128)}, u32[]{:S(2)}) copy-start(s32[1024,1]{0,1:T(1,128)} %param.18) | copy-start | bytes 12292
  20.5 10.9 %copy-start = (s32[1024]{0:T(1024)S(1)}, s32[1024]{0:T(1024)}, u32[]{:S(2)}) copy-start(s32[1024]{0:T(1024)} %param.19) | copy-start | bytes 12292
  43.4 15.9 %copy-start.2 = (s32[1,1024]{1,0:T(1,128)S(1)}, s32[1,1024]{1,0:T(1,128)}, u32[]{:S(2)}) copy-start(s32[1,1024]{1,0:T(1,128)} %get-tuple-element.11) | copy-start | bytes 12292
  52.4 18.5 %all-to-all-start.1 = ((f32[64,1,1024]{2,1,0:T(1,128)}), f32[64,1,1024]{2,1,0:T(1,128)S(1)}, u32[]{:S(2)}, u32[]{:S(2)}) async-start(f32[64,1,1024]{2,1,0:T(1,128)} %bitcast.39), calls=%async_computation.1 | async-start | bytes 524288 | tf_op jit(solution)/shard_map/all_to_all | solution.py:250
  81.5 4.5 %collective-permute-start.2 = (f32[4096]{0:T(1024)}, f32[4096]{0:T(1024)S(1)}, u32[]{:S(2)}, u32[]{:S(2)}) collective-permute-start(f32[4096]{0:T(1024)} %bitcast.44), channel_id=1, source_target_pairs={{0,3},{1,0},{2,1},{3,2},{4,7},{5,4},{6,5},{7,6},{8,11},{9,8},{10,9... | collective-permute-start | bytes 49160 | tf_op jit(solution)/shard_map/ppermute | solution.py:346
  84.3 5.5 %collective-permute-start.1 = (f32[4096]{0:T(1024)}, f32[4096]{0:T(1024)S(1)}, u32[]{:S(2)}, u32[]{:S(2)}) collective-permute-start(f32[4096]{0:T(1024)} %bitcast.45), channel_id=1, source_target_pairs={{0,2},{1,3},{2,0},{3,1},{4,6},{5,7},{6,4},{7,5},{8,10},{9,11},{10,... | collective-permute-start | bytes 49160 | tf_op jit(solution)/shard_map/ppermute | solution.py:346
  85.1 5.2 %collective-permute-start = (f32[4096]{0:T(1024)}, f32[4096]{0:T(1024)S(1)}, u32[]{:S(2)}, u32[]{:S(2)}) collective-permute-start(f32[4096]{0:T(1024)} %bitcast.46), channel_id=1, source_target_pairs={{0,1},{1,2},{2,3},{3,0},{4,5},{5,6},{6,7},{7,4},{8,9},{9,10},{10,1... | collective-permute-start | bytes 49160 | tf_op jit(solution)/shard_map/ppermute | solution.py:346

commit v6 on v5

--- a/solution.py
+++ b/solution.py
@@ -67,13 +67,28 @@
     return r[:, :n] + r[:, n : 2 * n] + r[:, 2 * n :]
 
 
-def _proj_pack_kernel(u_ref, c_ref, p_ref, req_ref, send_ref):
+def _prep(or_ref, sr_ref, idx_ref, devices, cap):
+    n = or_ref.shape[1]
+    oht = _iota((devices, n), 0) == or_ref[...]
+    upper = (_iota((n, n), 0) < _iota((n, n), 1)).astype(BF16)
+    counts = jnp.dot(oht.astype(BF16), upper, preferred_element_type=F32)
+    pos = jnp.sum(jnp.where(oht, counts, 0.0), axis=0, keepdims=True).astype(jnp.int32)
+    idx_ref[...] = or_ref[...] * cap + pos
+    pkt = (_iota((cap, n), 0) == pos).astype(BF16)
+    ohs = jnp.where(oht, sr_ref[...].astype(F32), 0.0).astype(BF16)
+    return lax.dot_general(ohs, pkt, (((1,), (1,)), ((), ())), preferred_element_type=F32)
+
+
+def _proj_pack_kernel(u_ref, c_ref, p_ref, or_ref, sr_ref, idx_ref, send_ref):
     cells = u_ref.shape[1]
     clusters = cells // 64
     rank2 = 2 * p_ref.shape[1]
-    devices, cap = req_ref.shape
-    groups = 4
-    lanes = groups * rank2
+    lanes = send_ref.shape[1]
+    nrow = rank2 * clusters // lanes
+    block = nrow + 1
+    devices = send_ref.shape[0] // block
+    cap = 32
+    req = _prep(or_ref, sr_ref, idx_ref, devices, cap)
 
     def body(ci, q):
         off = pl.multiple_of(ci * CHUNK, CHUNK)
@@ -82,29 +97,33 @@
         return q + _proj_chunk(pw, off, clusters, 64)
 
     q = lax.fori_loop(0, cells // CHUNK, body, jnp.zeros((rank2, clusters), F32))
-    nrow = clusters // groups
-    order = (_iota((nrow, groups), 0) * groups + _iota((nrow, groups), 1)).astype(F32)
-    flat = _pack(q, order)
+    per = lanes // clusters
+    hi = q.astype(BF16)
+    r1 = q - hi.astype(F32)
+    mid = r1.astype(BF16)
+    lo = (r1 - mid.astype(F32)).astype(BF16)
+    flat = jnp.zeros((nrow, lanes), F32)
+    for h in range(per):
+        sel = (_iota((nrow, rank2), 1) == _iota((nrow, rank2), 0) * per + h).astype(BF16)
+        part = sum(jnp.dot(sel, x, preferred_element_type=F32) for x in (hi, mid, lo))
+        place = (_iota((clusters, lanes), 1) == _iota((clusters, lanes), 0) + h * clusters)
+        flat = flat + _xdot(part, place.astype(BF16))
     place = (_iota((cap, lanes), 0) == _iota((cap, lanes), 1)).astype(BF16)
-    reqrow = jnp.dot(req_ref[...].astype(BF16), place, preferred_element_type=F32)
-    block = nrow + 1
+    reqrow = jnp.dot(req.astype(BF16), place, preferred_element_type=F32)
     for e in range(devices):
         send_ref[pl.ds(e * block, nrow), :] = flat
         send_ref[pl.ds(e * block + nrow, 1), :] = reqrow[e : e + 1]
 
 
-def _proj_kernel(u_ref, c_ref, p_ref, q_ref):
-    cells = u_ref.shape[1]
-    clusters = cells // 64
-    rank2 = 2 * p_ref.shape[1]
-
-    def body(ci, q):
-        off = pl.multiple_of(ci * CHUNK, CHUNK)
-        sl = pl.ds(off, CHUNK)
-        pw = _weighted_proj(u_ref[:, sl], c_ref[:, sl], p_ref[0, :, sl], p_ref[1, :, sl])
-        return q + _proj_chunk(pw, off, clusters, 64)
-
-    q_ref[...] = lax.fori_loop(0, cells // CHUNK, body, jnp.zeros((rank2, clusters), F32))
+def _rr_groups(rr, groups):
+    devices, cap = rr.shape
+    per = cap // groups
+    rows = devices * per
+    rep = ((_iota((rows, devices), 0) // per) == _iota((rows, devices), 1)).astype(BF16)
+    wide = jnp.dot(rep, rr.astype(BF16), preferred_element_type=F32)
+    keep = (_iota((rows, cap), 1) // groups) == (_iota((rows, cap), 0) % per)
+    fold = ((_iota((cap, groups), 0) % groups) == _iota((cap, groups), 1)).astype(BF16)
+    return jnp.dot(jnp.where(keep, wide, 0.0).astype(BF16), fold, preferred_element_type=F32)
 
 
 def _near_kernel(u_ref, c_ref, nb_ref, nlc_ref, base_ref, out_ref):
@@ -201,7 +220,7 @@
 
     body = _far_common(part_ref, qs_ref, cpl_ref, e_ref, u_ref, tail)
     q = lax.fori_loop(0, cells // CHUNK, body, jnp.zeros((rank2, clusters), F32))
-    send_ref[...] = _pack(q, rr_ref[...])
+    send_ref[...] = _pack(q, _rr_groups(rr_ref[...], send_ref.shape[1] // rank2))
 
 
 def _far_grad_kernel(part_ref, qs_ref, cpl_ref, e_ref, bg_ref, u_ref, t_ref):
@@ -214,21 +233,6 @@
 
     body = _far_common(part_ref, qs_ref, cpl_ref, e_ref, u_ref, tail)
     lax.fori_loop(0, cells // CHUNK, body, 0)
-
-
-def _prep_kernel(or_ref, sr_ref, idx_ref, req_ref):
-    n = or_ref.shape[1]
-    devices, cap = req_ref.shape
-    oht = _iota((devices, n), 0) == or_ref[...]
-    upper = (_iota((n, n), 0) < _iota((n, n), 1)).astype(BF16)
-    counts = jnp.dot(oht.astype(BF16), upper, preferred_element_type=F32)
-    pos = jnp.sum(jnp.where(oht, counts, 0.0), axis=0, keepdims=True).astype(jnp.int32)
-    idx_ref[...] = or_ref[...] * cap + pos
-    pkt = (_iota((cap, n), 0) == pos).astype(BF16)
-    ohs = jnp.where(oht, sr_ref[...].astype(F32), 0.0).astype(BF16)
-    req_ref[...] = lax.dot_general(
-        ohs, pkt, (((1,), (1,)), ((), ())), preferred_element_type=F32
-    )
 
 
 def _call(kernel, outs, args, flops, name):
@@ -257,9 +261,9 @@
     got = lax.all_to_all(send.reshape(devices, total // devices), "cells", 0, 0)
     lanes = send.shape[1]
     got = got.reshape(devices, total // (devices * lanes), lanes)
-    rr = got[:, -1, :cap].reshape(devices * cap // groups, groups)
-    table = got[:, :-1, :].reshape(devices * clusters, rank2)
-    return table[src_index].T, rr
+    rr = got[:, -1, :cap]
+    table = got[:, :-1, :].reshape(devices, rank2, clusters).transpose(1, 0, 2)
+    return table.reshape(rank2, devices * clusters)[:, src_index], rr
 
 
 def per_device(
@@ -293,18 +297,7 @@
     local_list = near_list - me * clusters
     nlc = jnp.repeat(local_list.T, width, axis=1)
 
-    idx, req = _call(
-        _prep_kernel,
-        (
-            jax.ShapeDtypeStruct((1, npairs), jnp.int32),
-            jax.ShapeDtypeStruct((devices, cap), F32),
-        ),
-        (far_owner.reshape(1, npairs), far_slot.reshape(1, npairs)),
-        2 * devices * npairs * npairs,
-        "prep",
-    )
     groups = 4
-    idx = idx.reshape(npairs)
     src_index = far_owner[:, 0] * clusters + far_slot
 
     nsend = devices * cap
@@ -313,7 +306,14 @@
     field_shape = jax.ShapeDtypeStruct((2, cells), F32)
 
     first_shape = jax.ShapeDtypeStruct((devices * (clusters // groups + 1), groups * rank2), F32)
-    send = _call(_proj_pack_kernel, first_shape, (src, cst, pb, req), 4 * rank2 * cells, "proj_pack")
+    idx, send = _call(
+        _proj_pack_kernel,
+        (jax.ShapeDtypeStruct((1, npairs), jnp.int32), first_shape),
+        (src, cst, pb, far_owner.reshape(1, npairs), far_slot.reshape(1, npairs)),
+        4 * rank2 * cells + 2 * devices * npairs * npairs,
+        "proj_pack",
+    )
+    idx = idx.reshape(npairs)
     send_shape = jax.ShapeDtypeStruct((devices * cap // groups, groups * rank2), F32)
     field = src
     for step in range(ITERS):

time: 92.1 us -> 91.2 us (level)
  Pallas kernels: 43.6 us -> 42.6 us
    pallas_call x6 -> x5, Pallas kernels: 43.6 us -> 42.6 us  [_call(): pl.pallas_call(kernel, out_shape=outs, compiler_params=pltpu.CompilerPara...]
  transfers between devices with their start and end apart: 5 -> 5, of which waited for: 4 -> 4; matrix products, arithmetic and copies ran while one was open for 1% -> 2% of each run, Pallas kernels for 24% -> 24%
where the time goes in v6:
time: 91.2 us; the launch traced here: 90.8 us
  Pallas kernels  42.6 us (47%)
  starting transfers between devices  23.5 us (26%)
  local copies, waits for them, and re-layouts  10 us (11%)
  waiting for transfers between devices  9.85 us (11%)
  other arithmetic  4.09 us (4%)
    pallas_call x5, Pallas kernels, _call(): pl.pallas_call(kernel, out_shape=outs, compiler_params=pltpu.CompilerPara...  42.6 us
    all_to_all x1, starting transfers between devices, _exchange_all(): got = lax.all_to_all(send.reshape(devices, total // devices), 'cells', 0, 0)  12.1 us
    all_to_all x1, starting transfers between devices, _exchange(): got = lax.all_to_all(send.reshape(devices, total // devices), 'cells', 0, 0)  6.96 us
    all_to_all x1, waiting for transfers between devices, _exchange_all(): got = lax.all_to_all(send.reshape(devices, total // devices), 'cells', 0, 0)  4.91 us
    ppermute x3, starting transfers between devices, per_device(): lax.ppermute(mine, 'freq', [(i, (i + k) % freqs) for i in range(freqs)])  4.43 us
    ppermute x3, waiting for transfers between devices, per_device(): lax.ppermute(mine, 'freq', [(i, (i + k) % freqs) for i in range(freqs)])  4.28 us
    gather x2, local copies, waits for them, and re-layouts, _exchange(): return got[idx].T  3.64 us
    gather x2, local copies, waits for them, and re-layouts, _exchange_all(): return (table.reshape(rank2, devices * clusters)[:, src_index], rr)  3.64 us
  transfers between devices with their start and end apart: 5, of which 4 were waited for; matrix products, arithmetic and copies ran while one was open for 2% of the time, Pallas kernels for 24%

profile of v6, /device:TPU:8, one launch (start us, length us, event | category | flops | bytes accessed | tf_op | source)
XLA Modules:
  0.0 90.8 jit_solution(9982749551468352990)
XLA Ops:
  0.6 5.5 %proj_pack.1 = (s32[1,1024]{1,0:T(1,128)}, f32[1088,128]{1,0:T(8,128)}) custom-call(f32[2,4096]{1,0:T(2,128)} %bitcast.40, f32[1,4096]{1,0:T(1,128)} %c_ref.7, f32[2,16,4096]{2,1,0:T(8,128)} %bitcast.35, s32[1,1024]{1,0:T(1,128)} %bitcast.50, s32[1,1024]{1,0:T(1,128)} %bitcast.49), custom_call_target="tpu_custom_call" | custom-call | flops 134742016 | bytes 1142784 | tf_op jit(solution)/shard_map/proj_pack/pallas_call | solution.py:243
  6.2 12.1 %all-to-all-start = ((f32[64,1,2176]{2,1,0:T(1,128)}), f32[64,1,2176]{2,1,0:T(1,128)S(1)}, u32[]{:S(2)}, u32[]{:S(2)}) async-start(f32[64,1,2176]{2,1,0:T(1,128)} %bitcast.39), calls=%async_computation | async-start | bytes 1114112 | tf_op jit(solution)/shard_map/all_to_all | solution.py:261
  18.3 0.7 subtract_bitcast_fusion
  19.0 0.1 broadcast_in_dim.10
  19.1 0.7 reshape.71.nlc_ref
  19.8 0.0 copy-start.1
  19.8 0.0 copy-start
  19.8 10.9 %near.2.part_ref = f32[2,4096]{1,0:T(2,128)} custom-call(f32[2,4096]{1,0:T(2,128)} %bitcast.41, f32[1,4096]{1,0:T(1,128)} %c_ref.7, f32[2,192,4096]{2,1,0:T(8,128)} %bitcast.29, s32[3,4096]{1,0:T(4,128)} %reshape.71.nlc_ref, f32[2,4096]{1,0:T(2,128)} %bitcast.42), custom_call_target="tpu_custom_call" | custom-call | flops 6291456 | bytes 6455296 | tf_op jit(solution)/shard_map/near/pallas_call | solution.py:243
  30.6 0.0 copy-done.1
  30.7 0.0 copy-done
  30.7 4.9 %all-to-all-done = f32[64,1,2176]{2,1,0:T(1,128)S(1)} async-done(((f32[64,1,2176]{2,1,0:T(1,128)}), f32[64,1,2176]{2,1,0:T(1,128)S(1)}, u32[]{:S(2)}, u32[]{:S(2)}) %all-to-all-start) | async-done | bytes 557088 | tf_op jit(solution)/shard_map/all_to_all | solution.py:261
  35.6 1.3 %reduce = f32[64,2176]{1,0:T(8,128)S(1)} reduce(f32[64,1,2176]{2,1,0:T(1,128)S(1)} %all-to-all-done, f32[]{:T(128)} %constant.59), dimensions={1}, to_apply=%all_to_all.13.reduce_sub_computation | reduce | bytes 1114116 | tf_op jit(solution)/shard_map/all_to_all | solution.py:261
  36.9 0.1 reshape.74
  37.0 0.6 slice.13
  37.7 0.2 reshape.75
  37.9 0.6 copy.19
  38.5 2.8 %gather_fusion = f32[1024,32]{1,0:T(8,128)S(1)} fusion(f32[32,4096]{0,1:T(8,128)S(1)} %bitcast.33, s32[1024]{0:T(1024)S(1)} %fusion), kind=kCustom, calls=%fused_computation | custom fusion | bytes 266240 | tf_op jit(solution)/shard_map/gather | solution.py:266
  41.3 0.8 copy.20
  42.2 0.0 copy-start.2
  42.2 9.3 %far_proj.1 = (f32[2,4096]{1,0:T(2,128)}, f32[512,128]{1,0:T(8,128)}) custom-call(f32[2,4096]{1,0:T(2,128)} %near.2.part_ref, f32[32,1024]{1,0:T(8,128)} %bitcast.44, f32[2,16,16,1024]{3,2,1,0:T(8,128)} %bitcast.31, f32[2,16,4096]{2,1,0:T(8,128)} %bitcast.37, f32[1,4096]{1,0:T(1,128)} %c_ref.7, f32[2,16,4096]{2,1,0:T(8,128)} %bitcast.36, f32[64,32]{1,0:T(8,128)} %bitcast.47), custom_call_target="tpu_custom_call" | custom-call | flops 4194304 | bytes 3629056 | tf_op jit(solution)/shard_map/far_proj/pallas_call | solution.py:243
  51.5 7.0 %all-to-all-start.1 = ((f32[64,1,1024]{2,1,0:T(1,128)}), f32[64,1,1024]{2,1,0:T(1,128)S(1)}, u32[]{:S(2)}, u32[]{:S(2)}) async-start(f32[64,1,1024]{2,1,0:T(1,128)} %bitcast.46), calls=%async_computation.1 | async-start | bytes 524288 | tf_op jit(solution)/shard_map/all_to_all | solution.py:254
  58.4 0.0 copy-done.2
  58.5 10.8 %near.3.part_ref = f32[2,4096]{1,0:T(2,128)} custom-call(f32[2,4096]{1,0:T(2,128)} %get-tuple-element.9.u_ref, f32[1,4096]{1,0:T(1,128)} %c_ref.7, f32[2,192,4096]{2,1,0:T(8,128)} %bitcast.30, s32[3,4096]{1,0:T(4,128)} %reshape.71.nlc_ref, f32[2,4096]{1,0:T(2,128)} %bitcast.43), custom_call_target="tpu_custom_call" | custom-call | flops 6291456 | bytes 6455296 | tf_op jit(solution)/shard_map/near/pallas_call | solution.py:243
  69.3 0.7 all-to-all-done.1
  70.0 0.6 reduce.1
  70.6 0.3 reshape.77
  70.9 2.8 %gather_fusion.1 = f32[1024,32]{1,0:T(8,128)S(1)} fusion(f32[2048,32]{1,0:T(8,128)S(1)} %reshape.77, s32[1024]{0:T(1024)S(1)} %broadcast_clamp_fusion), kind=kCustom, calls=%fused_computation.1 | custom fusion | bytes 266240 | tf_op jit(solution)/shard_map/gather | solution.py:256
  73.7 0.8 copy.23
  74.6 6.0 %far_grad.1 = (f32[2,4096]{1,0:T(2,128)}, f32[1,4096]{1,0:T(1,128)}) custom-call(f32[2,4096]{1,0:T(2,128)} %near.3.part_ref, f32[32,1024]{1,0:T(8,128)} %bitcast.45, f32[2,16,16,1024]{3,2,1,0:T(8,128)} %bitcast.32, f32[2,16,4096]{2,1,0:T(8,128)} %bitcast.38, f32[2,4096]{1,0:T(2,128)} %bitcast.48), custom_call_target="tpu_custom_call" | custom-call | flops 4194304 | bytes 2867200 | tf_op jit(solution)/shard_map/far_grad/pallas_call | solution.py:243
  80.6 2.8 %collective-permute-start.2 = (f32[4096]{0:T(1024)}, f32[4096]{0:T(1024)S(1)}, u32[]{:S(2)}, u32[]{:S(2)}) collective-permute-start(f32[4096]{0:T(1024)} %bitcast.54), channel_id=1, source_target_pairs={{0,3},{1,0},{2,1},{3,2},{4,7},{5,4},{6,5},{7,6},{8,11},{9,8},{10,9... | collective-permute-start | bytes 49160 | tf_op jit(solution)/shard_map/ppermute | solution.py:346
  83.4 0.8 collective-permute-start.1
  84.2 0.9 collective-permute-start
  85.0 0.0 collective-permute-done.2
  85.0 3.8 %collective-permute-done.1 = f32[4096]{0:T(1024)S(1)} collective-permute-done((f32[4096]{0:T(1024)}, f32[4096]{0:T(1024)S(1)}, u32[]{:S(2)}, u32[]{:S(2)}) %collective-permute-start.1) | collective-permute-done | bytes 16416 | tf_op jit(solution)/shard_map/ppermute | solution.py:346
  88.8 0.5 collective-permute-done
  89.3 0.8 pad_maximum_fusion
  90.1 0.7 dynamic-slice_add_fusion
  (5 shorter events, 0.1 us)
Async XLA Ops:
  6.2 29.4 %all-to-all-start = ((f32[64,1,2176]{2,1,0:T(1,128)}), f32[64,1,2176]{2,1,0:T(1,128)S(1)}, u32[]{:S(2)}, u32[]{:S(2)}) async-start(f32[64,1,2176]{2,1,0:T(1,128)} %bitcast.39), calls=%async_computation | async-start | bytes 1114112 | tf_op jit(solution)/shard_map/all_to_all | solution.py:261
  19.8 10.9 %copy-start.1 = (s32[1024,1]{0,1:T(1,128)S(1)}, s32[1024,1]{0,1:T(1,128)}, u32[]{:S(2)}) copy-start(s32[1024,1]{0,1:T(1,128)} %param.18) | copy-start | bytes 12292
  19.8 10.9 %copy-start = (s32[1024]{0:T(1024)S(1)}, s32[1024]{0:T(1024)}, u32[]{:S(2)}) copy-start(s32[1024]{0:T(1024)} %param.19) | copy-start | bytes 12292
  42.2 16.3 %copy-start.2 = (s32[1,1024]{1,0:T(1,128)S(1)}, s32[1,1024]{1,0:T(1,128)}, u32[]{:S(2)}) copy-start(s32[1,1024]{1,0:T(1,128)} %get-tuple-element.11) | copy-start | bytes 12292
  51.5 18.5 %all-to-all-start.1 = ((f32[64,1,1024]{2,1,0:T(1,128)}), f32[64,1,1024]{2,1,0:T(1,128)S(1)}, u32[]{:S(2)}, u32[]{:S(2)}) async-start(f32[64,1,1024]{2,1,0:T(1,128)} %bitcast.46), calls=%async_computation.1 | async-start | bytes 524288 | tf_op jit(solution)/shard_map/all_to_all | solution.py:254
  80.6 4.4 %collective-permute-start.2 = (f32[4096]{0:T(1024)}, f32[4096]{0:T(1024)S(1)}, u32[]{:S(2)}, u32[]{:S(2)}) collective-permute-start(f32[4096]{0:T(1024)} %bitcast.54), channel_id=1, source_target_pairs={{0,3},{1,0},{2,1},{3,2},{4,7},{5,4},{6,5},{7,6},{8,11},{9,8},{10,9... | collective-permute-start | bytes 49160 | tf_op jit(solution)/shard_map/ppermute | solution.py:346
  83.4 5.5 %collective-permute-start.1 = (f32[4096]{0:T(1024)}, f32[4096]{0:T(1024)S(1)}, u32[]{:S(2)}, u32[]{:S(2)}) collective-permute-start(f32[4096]{0:T(1024)} %bitcast.55), channel_id=1, source_target_pairs={{0,2},{1,3},{2,0},{3,1},{4,6},{5,7},{6,4},{7,5},{8,10},{9,11},{10,... | collective-permute-start | bytes 49160 | tf_op jit(solution)/shard_map/ppermute | solution.py:346
  84.2 5.2 %collective-permute-start = (f32[4096]{0:T(1024)}, f32[4096]{0:T(1024)S(1)}, u32[]{:S(2)}, u32[]{:S(2)}) collective-permute-start(f32[4096]{0:T(1024)} %bitcast.56), channel_id=1, source_target_pairs={{0,1},{1,2},{2,3},{3,0},{4,5},{5,6},{6,7},{7,4},{8,9},{9,10},{10,1... | collective-permute-start | bytes 49160 | tf_op jit(solution)/shard_map/ppermute | solution.py:346

commit v7 on v6

--- a/solution.py
+++ b/solution.py
@@ -179,12 +179,15 @@
         off = pl.multiple_of(pj * PAIR_CHUNK, PAIR_CHUNK)
         sl = pl.ds(off, PAIR_CHUNK)
         qs = qs_ref[:, sl]
-        qre = qs[:rank][None]
-        qim = qs[rank:][None]
-        cre = cpl_ref[0, :, :, sl]
-        cim = cpl_ref[1, :, :, sl]
-        zre = jnp.sum(cre * qre - cim * qim, axis=1)
-        zim = jnp.sum(cre * qim + cim * qre, axis=1)
+        zre = jnp.zeros((rank, PAIR_CHUNK), F32)
+        zim = jnp.zeros((rank, PAIR_CHUNK), F32)
+        for i in range(rank):
+            cre = cpl_ref[0, i, :, sl]
+            cim = cpl_ref[1, i, :, sl]
+            qre = qs[i : i + 1]
+            qim = qs[rank + i : rank + i + 1]
+            zre = zre + (cre * qre - cim * qim)
+            zim = zim + (cre * qim + cim * qre)
         seg = ((_iota((PAIR_CHUNK, clusters), 0) + off) // far) == _iota((PAIR_CHUNK, clusters), 1)
         return z + _xdot(jnp.concatenate([zre, zim], axis=0), seg.astype(BF16))
 
@@ -290,7 +293,7 @@
     nb = near_blocks[0]
     pb = proj_basis[0]
     eb = expand_basis[0]
-    cp = coupling[0]
+    cp = jnp.transpose(coupling[0], (0, 2, 1, 3))
     bg = background[0]
 
     me = lax.axis_index("cells")

time: 91.2 us -> 93.3 us (1.023)
  local copies, waits for them, and re-layouts: 10 us -> 14.2 us
  waiting for transfers between devices: 9.85 us -> 5.66 us
  starting transfers between devices: 23.5 us -> 26.2 us
    all_to_all x1, waiting for transfers between devices: 4.91 us -> 0.74 us  [_exchange_all(): got = lax.all_to_all(send.reshape(devices, total // devices), 'cells', 0, 0)]
    unnamed x6 -> x7, local copies, waits for them, and re-layouts: 0.01 us -> 4.17 us
    all_to_all x1, starting transfers between devices: 6.96 us -> 9.6 us  [_exchange(): got = lax.all_to_all(send.reshape(devices, total // devices), 'cells', 0, 0)]
  transfers between devices with their start and end apart: 5 -> 5, of which waited for: 4 -> 4; matrix products, arithmetic and copies ran while one was open for 2% -> 6% of each run, Pallas kernels for 24% -> 23%
where the time goes in v7:
time: 93.3 us; the launch traced here: 92.9 us
  Pallas kernels  42.1 us (45%)
  starting transfers between devices  26.2 us (28%)
  local copies, waits for them, and re-layouts  14.2 us (15%)
  waiting for transfers between devices  5.66 us (6%)
  other arithmetic  4.09 us (4%)
    pallas_call x5, Pallas kernels, _call(): pl.pallas_call(kernel, out_shape=outs, compiler_params=pltpu.CompilerPara...  42.1 us
    all_to_all x1, starting transfers between devices, _exchange_all(): got = lax.all_to_all(send.reshape(devices, total // devices), 'cells', 0, 0)  12.1 us
    all_to_all x1, starting transfers between devices, _exchange(): got = lax.all_to_all(send.reshape(devices, total // devices), 'cells', 0, 0)  9.6 us
    ppermute x3, starting transfers between devices, per_device(): lax.ppermute(mine, 'freq', [(i, (i + k) % freqs) for i in range(freqs)])  4.45 us
    ppermute x3, waiting for transfers between devices, per_device(): lax.ppermute(mine, 'freq', [(i, (i + k) % freqs) for i in range(freqs)])  4.26 us
    unnamed x7, local copies, waits for them, and re-layouts  4.17 us
    gather x2, local copies, waits for them, and re-layouts, _exchange_all(): return (table.reshape(rank2, devices * clusters)[:, src_index], rr)  3.64 us
    gather x2, local copies, waits for them, and re-layouts, _exchange(): return got[idx].T  3.63 us
  transfers between devices with their start and end apart: 5, of which 4 were waited for; matrix products, arithmetic and copies ran while one was open for 6% of the time, Pallas kernels for 23%

profile of v7, /device:TPU:8, one launch (start us, length us, event | category | flops | bytes accessed | tf_op | source)
XLA Modules:
  0.0 92.9 jit_solution(2188259624241008342)
XLA Ops:
  0.6 5.5 %proj_pack.1 = (s32[1,1024]{1,0:T(1,128)}, f32[1088,128]{1,0:T(8,128)}) custom-call(f32[2,4096]{1,0:T(2,128)} %bitcast.44, f32[1,4096]{1,0:T(1,128)} %c_ref.7, f32[2,16,4096]{2,1,0:T(8,128)} %bitcast.39, s32[1,1024]{1,0:T(1,128)} %bitcast.54, s32[1,1024]{1,0:T(1,128)} %bitcast.53), custom_call_target="tpu_custom_call" | custom-call | flops 134742016 | bytes 1142784 | tf_op jit(solution)/shard_map/proj_pack/pallas_call | solution.py:246
  6.2 12.1 %all-to-all-start = ((f32[64,1,2176]{2,1,0:T(1,128)}), f32[64,1,2176]{2,1,0:T(1,128)S(1)}, u32[]{:S(2)}, u32[]{:S(2)}) async-start(f32[64,1,2176]{2,1,0:T(1,128)} %bitcast.43), calls=%async_computation | async-start | bytes 1114112 | tf_op jit(solution)/shard_map/all_to_all | solution.py:264
  18.3 0.7 subtract_bitcast_fusion
  19.0 0.1 broadcast_in_dim.10
  19.1 0.7 reshape.71.nlc_ref
  19.8 4.2 %copy.29 = f32[1,2,16,16,1024]{4,2,3,1,0:T(8,128)} copy(f32[1,2,16,16,1024]{4,3,2,1,0:T(8,128)} %param.17) | data formatting | bytes 4194304 | tf_op args[7]
  23.9 0.0 copy-start.1
  23.9 0.0 copy-start
  24.0 10.9 %near.2.part_ref = f32[2,4096]{1,0:T(2,128)} custom-call(f32[2,4096]{1,0:T(2,128)} %bitcast.45, f32[1,4096]{1,0:T(1,128)} %c_ref.7, f32[2,192,4096]{2,1,0:T(8,128)} %bitcast.33, s32[3,4096]{1,0:T(4,128)} %reshape.71.nlc_ref, f32[2,4096]{1,0:T(2,128)} %bitcast.46), custom_call_target="tpu_custom_call" | custom-call | flops 6291456 | bytes 6455296 | tf_op jit(solution)/shard_map/near/pallas_call | solution.py:246
  34.8 0.0 copy-done.1
  34.8 0.0 copy-done
  34.9 0.7 all-to-all-done
  35.6 1.3 %reduce = f32[64,2176]{1,0:T(8,128)S(1)} reduce(f32[64,1,2176]{2,1,0:T(1,128)S(1)} %all-to-all-done, f32[]{:T(128)} %constant.59), dimensions={1}, to_apply=%all_to_all.13.reduce_sub_computation | reduce | bytes 1114116 | tf_op jit(solution)/shard_map/all_to_all | solution.py:264
  36.9 0.1 reshape.74
  37.0 0.6 slice.13
  37.7 0.2 reshape.75
  37.9 0.6 copy.21
  38.5 2.8 %gather_fusion = f32[1024,32]{1,0:T(8,128)S(1)} fusion(f32[32,4096]{0,1:T(8,128)S(1)} %bitcast.37, s32[1024]{0:T(1024)S(1)} %fusion), kind=kCustom, calls=%fused_computation | custom fusion | bytes 266240 | tf_op jit(solution)/shard_map/gather | solution.py:269
  41.3 0.8 copy.22
  42.2 0.0 copy-start.2
  42.2 9.1 %far_proj.1 = (f32[2,4096]{1,0:T(2,128)}, f32[512,128]{1,0:T(8,128)}) custom-call(f32[2,4096]{1,0:T(2,128)} %near.2.part_ref, f32[32,1024]{1,0:T(8,128)} %bitcast.48, f32[2,16,16,1024]{3,2,1,0:T(8,128)} %bitcast.35, f32[2,16,4096]{2,1,0:T(8,128)} %bitcast.41, f32[1,4096]{1,0:T(1,128)} %c_ref.7, f32[2,16,4096]{2,1,0:T(8,128)} %bitcast.40, f32[64,32]{1,0:T(8,128)} %bitcast.51), custom_call_target="tpu_custom_call" | custom-call | flops 4194304 | bytes 3629056 | tf_op jit(solution)/shard_map/far_proj/pallas_call | solution.py:246
  51.2 9.6 %all-to-all-start.1 = ((f32[64,1,1024]{2,1,0:T(1,128)}), f32[64,1,1024]{2,1,0:T(1,128)S(1)}, u32[]{:S(2)}, u32[]{:S(2)}) async-start(f32[64,1,1024]{2,1,0:T(1,128)} %bitcast.50), calls=%async_computation.1 | async-start | bytes 524288 | tf_op jit(solution)/shard_map/all_to_all | solution.py:257
  60.8 0.0 copy-done.2
  60.9 10.8 %near.3.part_ref = f32[2,4096]{1,0:T(2,128)} custom-call(f32[2,4096]{1,0:T(2,128)} %get-tuple-element.9.u_ref, f32[1,4096]{1,0:T(1,128)} %c_ref.7, f32[2,192,4096]{2,1,0:T(8,128)} %bitcast.34, s32[3,4096]{1,0:T(4,128)} %reshape.71.nlc_ref, f32[2,4096]{1,0:T(2,128)} %bitcast.47), custom_call_target="tpu_custom_call" | custom-call | flops 6291456 | bytes 6455296 | tf_op jit(solution)/shard_map/near/pallas_call | solution.py:246
  71.7 0.7 all-to-all-done.1
  72.4 0.6 reduce.1
  73.0 0.3 reshape.77
  73.3 2.8 %gather_fusion.1 = f32[1024,32]{1,0:T(8,128)S(1)} fusion(f32[2048,32]{1,0:T(8,128)S(1)} %reshape.77, s32[1024]{0:T(1024)S(1)} %broadcast_clamp_fusion), kind=kCustom, calls=%fused_computation.1 | custom fusion | bytes 266240 | tf_op jit(solution)/shard_map/gather | solution.py:259
  76.1 0.8 copy.26
  77.0 5.8 %far_grad.1 = (f32[2,4096]{1,0:T(2,128)}, f32[1,4096]{1,0:T(1,128)}) custom-call(f32[2,4096]{1,0:T(2,128)} %near.3.part_ref, f32[32,1024]{1,0:T(8,128)} %bitcast.49, f32[2,16,16,1024]{3,2,1,0:T(8,128)} %bitcast.36, f32[2,16,4096]{2,1,0:T(8,128)} %bitcast.42, f32[2,4096]{1,0:T(2,128)} %bitcast.52), custom_call_target="tpu_custom_call" | custom-call | flops 4194304 | bytes 2867200 | tf_op jit(solution)/shard_map/far_grad/pallas_call | solution.py:246
  82.7 2.8 %collective-permute-start.2 = (f32[4096]{0:T(1024)}, f32[4096]{0:T(1024)S(1)}, u32[]{:S(2)}, u32[]{:S(2)}) collective-permute-start(f32[4096]{0:T(1024)} %bitcast.58), channel_id=1, source_target_pairs={{0,3},{1,0},{2,1},{3,2},{4,7},{5,4},{6,5},{7,6},{8,11},{9,8},{10,9... | collective-permute-start | bytes 49160 | tf_op jit(solution)/shard_map/ppermute | solution.py:349
  85.5 0.8 collective-permute-start.1
  86.3 0.9 collective-permute-start
  87.2 0.0 collective-permute-done.2
  87.2 3.8 %collective-permute-done.1 = f32[4096]{0:T(1024)S(1)} collective-permute-done((f32[4096]{0:T(1024)}, f32[4096]{0:T(1024)S(1)}, u32[]{:S(2)}, u32[]{:S(2)}) %collective-permute-start.1) | collective-permute-done | bytes 16416 | tf_op jit(solution)/shard_map/ppermute | solution.py:349
  90.9 0.5 collective-permute-done
  91.5 0.8 pad_maximum_fusion
  92.2 0.7 dynamic-slice_add_fusion
  (5 shorter events, 0.1 us)
Async XLA Ops:
  6.2 29.4 %all-to-all-start = ((f32[64,1,2176]{2,1,0:T(1,128)}), f32[64,1,2176]{2,1,0:T(1,128)S(1)}, u32[]{:S(2)}, u32[]{:S(2)}) async-start(f32[64,1,2176]{2,1,0:T(1,128)} %bitcast.43), calls=%async_computation | async-start | bytes 1114112 | tf_op jit(solution)/shard_map/all_to_all | solution.py:264
  23.9 10.9 %copy-start.1 = (s32[1024,1]{0,1:T(1,128)S(1)}, s32[1024,1]{0,1:T(1,128)}, u32[]{:S(2)}) copy-start(s32[1024,1]{0,1:T(1,128)} %param.18) | copy-start | bytes 12292
  23.9 10.9 %copy-start = (s32[1024]{0:T(1024)S(1)}, s32[1024]{0:T(1024)}, u32[]{:S(2)}) copy-start(s32[1024]{0:T(1024)} %param.19) | copy-start | bytes 12292
  42.2 18.7 %copy-start.2 = (s32[1,1024]{1,0:T(1,128)S(1)}, s32[1,1024]{1,0:T(1,128)}, u32[]{:S(2)}) copy-start(s32[1,1024]{1,0:T(1,128)} %get-tuple-element.11) | copy-start | bytes 12292
  51.2 21.1 %all-to-all-start.1 = ((f32[64,1,1024]{2,1,0:T(1,128)}), f32[64,1,1024]{2,1,0:T(1,128)S(1)}, u32[]{:S(2)}, u32[]{:S(2)}) async-start(f32[64,1,1024]{2,1,0:T(1,128)} %bitcast.50), calls=%async_computation.1 | async-start | bytes 524288 | tf_op jit(solution)/shard_map/all_to_all | solution.py:257
  82.7 4.5 %collective-permute-start.2 = (f32[4096]{0:T(1024)}, f32[4096]{0:T(1024)S(1)}, u32[]{:S(2)}, u32[]{:S(2)}) collective-permute-start(f32[4096]{0:T(1024)} %bitcast.58), channel_id=1, source_target_pairs={{0,3},{1,0},{2,1},{3,2},{4,7},{5,4},{6,5},{7,6},{8,11},{9,8},{10,9... | collective-permute-start | bytes 49160 | tf_op jit(solution)/shard_map/ppermute | solution.py:349
  85.5 5.5 %collective-permute-start.1 = (f32[4096]{0:T(1024)}, f32[4096]{0:T(1024)S(1)}, u32[]{:S(2)}, u32[]{:S(2)}) collective-permute-start(f32[4096]{0:T(1024)} %bitcast.59), channel_id=1, source_target_pairs={{0,2},{1,3},{2,0},{3,1},{4,6},{5,7},{6,4},{7,5},{8,10},{9,11},{10,... | collective-permute-start | bytes 49160 | tf_op jit(solution)/shard_map/ppermute | solution.py:349
  86.3 5.2 %collective-permute-start = (f32[4096]{0:T(1024)}, f32[4096]{0:T(1024)S(1)}, u32[]{:S(2)}, u32[]{:S(2)}) collective-permute-start(f32[4096]{0:T(1024)} %bitcast.60), channel_id=1, source_target_pairs={{0,1},{1,2},{2,3},{3,0},{4,5},{5,6},{6,7},{7,4},{8,9},{9,10},{10,1... | collective-permute-start | bytes 49160 | tf_op jit(solution)/shard_map/ppermute | solution.py:349

commit v8 on v6

--- a/solution.py
+++ b/solution.py
@@ -235,15 +235,21 @@
     lax.fori_loop(0, cells // CHUNK, body, 0)
 
 
-def _call(kernel, outs, args, flops, name):
+def _call(kernel, outs, args, flops, name, resident=False):
     leaves = outs if isinstance(outs, tuple) else (outs,)
     nbytes = sum(a.size * a.dtype.itemsize for a in args) + sum(
         o.size * jnp.dtype(o.dtype).itemsize for o in leaves
     )
+    extra = {}
+    limit = VMEM_LIMIT
+    if resident:
+        extra["in_specs"] = [pl.BlockSpec(memory_space=pltpu.VMEM)] * len(args)
+        limit = 24 * 1024 * 1024
     return pl.pallas_call(
         kernel,
         out_shape=outs,
-        compiler_params=pltpu.CompilerParams(vmem_limit_bytes=VMEM_LIMIT),
+        **extra,
+        compiler_params=pltpu.CompilerParams(vmem_limit_bytes=limit),
         cost_estimate=pl.CostEstimate(flops=flops, bytes_accessed=nbytes, transcendentals=0),
         name=name,
     )(*args)
@@ -331,6 +337,7 @@
                 (part, qs, cp, eb, cst, pb, rr),
                 8 * cp.size,
                 "far_proj",
+                resident=True,
             )
         else:
             field, terms = _call(
@@ -339,6 +346,7 @@
                 (part, qs, cp, eb, bg),
                 8 * cp.size,
                 "far_grad",
+                resident=True,
             )
     freqs = lax.axis_size("freq")
     mine = terms[0]

time: 91.2 us -> 94.8 us (1.039)
  local copies, waits for them, and re-layouts: 10 us -> 18.5 us
  Pallas kernels: 42.6 us -> 38.7 us
    pallas_call x5, Pallas kernels: 42.6 us -> 38.7 us  [_call(): pl.pallas_call(kernel, out_shape=outs, **extra, compiler_params=pltpu.Com...]
    gather x2, local copies, waits for them, and re-layouts: 3.64 us -> 6.79 us  [_exchange_all(): return (table.reshape(rank2, devices * clusters)[:, src_index], rr)]
    transpose x1, local copies, waits for them, and re-layouts: 0.62 us -> 3.34 us  [_exchange_all(): table = got[:, :-1, :].reshape(devices, rank2, clusters).transpose(1, 0, 2)]
    reshape x1, local copies, waits for them, and re-layouts: 0.34 us -> 1.33 us  [_exchange(): got = got.reshape(devices * cap, total // (devices * cap))]
    reshape x1, local copies, waits for them, and re-layouts: 0.21 us -> 1.18 us  [_exchange_all(): table = got[:, :-1, :].reshape(devices, rank2, clusters).transpose(1, 0, 2)]
  transfers between devices with their start and end apart: 5 -> 5, of which waited for: 4 -> 4; matrix products, arithmetic and copies ran while one was open for 2% -> 2% of each run, Pallas kernels for 24% -> 23%
where the time goes in v8:
time: 94.8 us; the launch traced here: 94.5 us
  Pallas kernels  38.7 us (41%)
  starting transfers between devices  23.5 us (25%)
  local copies, waits for them, and re-layouts  18.5 us (20%)
  waiting for transfers between devices  9.6 us (10%)
  other arithmetic  3.37 us (4%)
    pallas_call x5, Pallas kernels, _call(): pl.pallas_call(kernel, out_shape=outs, **extra, compiler_params=pltpu.Com...  38.7 us
    all_to_all x1, starting transfers between devices, _exchange_all(): got = lax.all_to_all(send.reshape(devices, total // devices), 'cells', 0, 0)  12.1 us
    all_to_all x1, starting transfers between devices, _exchange(): got = lax.all_to_all(send.reshape(devices, total // devices), 'cells', 0, 0)  6.95 us
    gather x2, local copies, waits for them, and re-layouts, _exchange_all(): return (table.reshape(rank2, devices * clusters)[:, src_index], rr)  6.79 us
    all_to_all x1, waiting for transfers between devices, _exchange_all(): got = lax.all_to_all(send.reshape(devices, total // devices), 'cells', 0, 0)  4.89 us
    ppermute x3, starting transfers between devices, per_device(): lax.ppermute(mine, 'freq', [(i, (i + k) % freqs) for i in range(freqs)])  4.45 us
    gather x2, local copies, waits for them, and re-layouts, _exchange(): return got[idx].T  4.2 us
    ppermute x3, waiting for transfers between devices, per_device(): lax.ppermute(mine, 'freq', [(i, (i + k) % freqs) for i in range(freqs)])  4.05 us
  transfers between devices with their start and end apart: 5, of which 4 were waited for; matrix products, arithmetic and copies ran while one was open for 2% of the time, Pallas kernels for 23%

profile of v8, /device:TPU:8, one launch (start us, length us, event | category | flops | bytes accessed | tf_op | source)
XLA Modules:
  0.0 94.5 jit_solution(7583452428072702918)
XLA Ops:
  0.6 5.5 %proj_pack.1 = (s32[1,1024]{1,0:T(1,128)}, f32[1088,128]{1,0:T(8,128)}) custom-call(f32[2,4096]{1,0:T(2,128)} %bitcast.47, f32[1,4096]{1,0:T(1,128)} %c_ref.7, f32[2,16,4096]{2,1,0:T(8,128)} %bitcast.31, s32[1,1024]{1,0:T(1,128)} %bitcast.52, s32[1,1024]{1,0:T(1,128)} %bitcast.51), custom_call_target="tpu_custom_call" | custom-call | flops 134742016 | bytes 1142784 | tf_op jit(solution)/shard_map/proj_pack/pallas_call | solution.py:248
  6.1 12.1 %all-to-all-start = ((f32[64,1,2176]{2,1,0:T(1,128)}), f32[64,1,2176]{2,1,0:T(1,128)S(1)}, u32[]{:S(2)}, u32[]{:S(2)}) async-start(f32[64,1,2176]{2,1,0:T(1,128)} %bitcast.46), calls=%async_computation | async-start | bytes 1114112 | tf_op jit(solution)/shard_map/all_to_all | solution.py:267
  18.3 0.7 subtract_bitcast_fusion
  19.0 0.1 broadcast_in_dim.10
  19.0 0.7 reshape.71.nlc_ref
  19.8 0.0 copy-start.9
  19.8 0.0 copy-start.8
  19.8 10.9 %near.2.part_ref = f32[2,4096]{1,0:T(2,128)} custom-call(f32[2,4096]{1,0:T(2,128)} %bitcast.48, f32[1,4096]{1,0:T(1,128)} %c_ref.7, f32[2,192,4096]{2,1,0:T(8,128)} %bitcast.42, s32[3,4096]{1,0:T(4,128)} %reshape.71.nlc_ref, f32[2,4096]{1,0:T(2,128)} %bitcast.49), custom_call_target="tpu_custom_call" | custom-call | flops 6291456 | bytes 6455296 | tf_op jit(solution)/shard_map/near/pallas_call | solution.py:248
  30.7 0.0 copy-done.9
  30.7 0.0 copy-done.8
  30.7 4.9 %all-to-all-done = f32[64,1,2176]{2,1,0:T(1,128)S(1)} async-done(((f32[64,1,2176]{2,1,0:T(1,128)}), f32[64,1,2176]{2,1,0:T(1,128)S(1)}, u32[]{:S(2)}, u32[]{:S(2)}) %all-to-all-start) | async-done | bytes 557088 | tf_op jit(solution)/shard_map/all_to_all | solution.py:267
  35.6 1.3 %reduce = f32[64,2176]{1,0:T(8,128)S(1)} reduce(f32[64,1,2176]{2,1,0:T(1,128)S(1)} %all-to-all-done, f32[]{:T(128)} %constant.59), dimensions={1}, to_apply=%all_to_all.13.reduce_sub_computation | reduce | bytes 1114116 | tf_op jit(solution)/shard_map/all_to_all | solution.py:267
  36.9 0.1 reshape.74
  37.1 1.2 %reshape.75 = f32[64,32,64]{2,1,0:T(8,128)} reshape(f32[64,16,128]{2,1,0:T(8,128)S(1)} %slice.12) | data formatting | bytes 1048576 | tf_op jit(solution)/shard_map/reshape | solution.py:271
  38.2 0.0 copy-start
  38.2 0.0 copy-start.1
  38.2 0.0 copy-start.2
  38.3 0.0 copy-start.3
  38.3 0.0 copy-start.4
  38.3 3.3 %copy.19 = f32[32,64,64]{0,2,1:T(8,128)} copy(f32[32,64,64]{2,0,1:T(8,128)} %bitcast.45) | data formatting | bytes 1048576 | tf_op jit(solution)/shard_map/transpose | solution.py:271
  41.6 5.6 %gather_fusion = f32[1024,32]{1,0:T(8,128)} fusion(f32[32,4096]{0,1:T(8,128)} %bitcast.44, s32[1024]{0:T(1024)S(1)} %fusion), kind=kCustom, calls=%fused_computation | custom fusion | bytes 266240 | tf_op jit(solution)/shard_map/gather | solution.py:272
  47.2 1.2 %copy.20 = f32[1024,32]{0,1:T(8,128)S(1)} copy(f32[1024,32]{1,0:T(8,128)} %gather_fusion) | data formatting | bytes 262144 | tf_op jit(solution)/shard_map/gather | solution.py:272
  48.4 0.0 copy-start.10
  48.4 0.0 copy-done
  48.4 0.0 copy-done.1
  48.4 0.0 copy-done.2
  48.4 0.0 copy-done.3
  48.4 0.0 copy-done.4
  48.5 7.3 %far_proj.1 = (f32[2,4096]{1,0:T(2,128)S(1)}, f32[512,128]{1,0:T(8,128)}) custom-call(f32[2,4096]{1,0:T(2,128)S(1)} %copy-done.4, f32[32,1024]{1,0:T(8,128)S(1)} %bitcast.35, f32[2,16,16,1024]{3,2,1,0:T(8,128)S(1)} %bitcast.29, f32[2,16,4096]{2,1,0:T(8,128)S(1)} %bitcast.33, f32[1,4096]{1,0:T(1,128)S(1)} %copy-done.3, f32[2,16,4096]{2,1,0:T(8,128)S(1)} %bitcast.32, ...), custom_call_target="tpu_custom_call" | custom-call | flops 4194304 | bytes 3629056 | tf_op jit(solution)/shard_map/far_proj/pallas_call | solution.py:248
  55.8 0.0 copy-start.7
  55.8 0.6 copy-done.7
  56.4 7.0 %all-to-all-start.1 = ((f32[64,1,1024]{2,1,0:T(1,128)}), f32[64,1,1024]{2,1,0:T(1,128)S(1)}, u32[]{:S(2)}, u32[]{:S(2)}) async-start(f32[64,1,1024]{2,1,0:T(1,128)} %bitcast.14), calls=%async_computation.1 | async-start | bytes 524288 | tf_op jit(solution)/shard_map/all_to_all | solution.py:260
  63.3 0.0 copy-done.10
  63.4 10.8 %near.3.part_ref = f32[2,4096]{1,0:T(2,128)} custom-call(f32[2,4096]{1,0:T(2,128)} %copy-done.7, f32[1,4096]{1,0:T(1,128)} %c_ref.7, f32[2,192,4096]{2,1,0:T(8,128)} %bitcast.43, s32[3,4096]{1,0:T(4,128)} %reshape.71.nlc_ref, f32[2,4096]{1,0:T(2,128)} %bitcast.50), custom_call_target="tpu_custom_call" | custom-call | flops 6291456 | bytes 6455296 | tf_op jit(solution)/shard_map/near/pallas_call | solution.py:248
  74.2 0.7 all-to-all-done.1
  74.9 0.6 reduce.1
  75.5 1.3 %reshape.77 = f32[2048,32]{1,0:T(8,128)} reshape(f32[64,1024]{1,0:T(8,128)S(1)} %reduce.1) | data formatting | bytes 524288 | tf_op jit(solution)/shard_map/reshape | solution.py:261
  76.8 0.0 copy-start.5
  76.8 0.0 copy-start.6
  76.8 4.0 %gather_fusion.1 = f32[1024,32]{1,0:T(8,128)S(1)} fusion(f32[2048,32]{1,0:T(8,128)} %reshape.77, s32[1024]{0:T(1024)S(1)} %broadcast_clamp_fusion), kind=kCustom, calls=%fused_computation.1 | custom fusion | bytes 266240 | tf_op jit(solution)/shard_map/gather | solution.py:262
  80.9 0.2 copy.23
  81.0 0.0 copy-done.5
  81.0 0.0 copy-done.6
  81.0 4.2 %far_grad.1 = (f32[2,4096]{1,0:T(2,128)}, f32[1,4096]{1,0:T(1,128)S(1)}) custom-call(f32[2,4096]{1,0:T(2,128)S(1)} %copy-done.5, f32[32,1024]{1,0:T(8,128)S(1)} %bitcast.36, f32[2,16,16,1024]{3,2,1,0:T(8,128)S(1)} %bitcast.30, f32[2,16,4096]{2,1,0:T(8,128)S(1)} %bitcast.34, f32[2,4096]{1,0:T(2,128)S(1)} %bitcast.38), custom_call_target="tpu_custom_call" | custom-call | flops 4194304 | bytes 2867200 | tf_op jit(solution)/shard_map/far_grad/pallas_call | solution.py:248
  85.2 2.8 %collective-permute-start.2 = (f32[4096]{0:T(1024)S(1)}, f32[4096]{0:T(1024)S(1)}, u32[]{:S(2)}, u32[]{:S(2)}) collective-permute-start(f32[4096]{0:T(1024)S(1)} %bitcast.39), channel_id=1, source_target_pairs={{0,3},{1,0},{2,1},{3,2},{4,7},{5,4},{6,5},{7,6},{8,11},{9,8},{10,9... | collective-permute-start | bytes 49160 | tf_op jit(solution)/shard_map/ppermute | solution.py:354
  88.0 0.8 collective-permute-start.1
  88.8 0.9 collective-permute-start
  89.7 0.0 collective-permute-done.2
  89.7 3.5 %collective-permute-done.1 = f32[4096]{0:T(1024)S(1)} collective-permute-done((f32[4096]{0:T(1024)S(1)}, f32[4096]{0:T(1024)S(1)}, u32[]{:S(2)}, u32[]{:S(2)}) %collective-permute-start.1) | collective-permute-done | bytes 16416 | tf_op jit(solution)/shard_map/ppermute | solution.py:354
  93.2 0.5 collective-permute-done
  93.7 0.1 pad_maximum_fusion
  93.8 0.7 dynamic-slice_add_fusion
  (6 shorter events, 0.1 us)
Async XLA Ops:
  6.1 29.4 %all-to-all-start = ((f32[64,1,2176]{2,1,0:T(1,128)}), f32[64,1,2176]{2,1,0:T(1,128)S(1)}, u32[]{:S(2)}, u32[]{:S(2)}) async-start(f32[64,1,2176]{2,1,0:T(1,128)} %bitcast.46), calls=%async_computation | async-start | bytes 1114112 | tf_op jit(solution)/shard_map/all_to_all | solution.py:267
  19.8 10.9 %copy-start.9 = (s32[1024,1]{0,1:T(1,128)S(1)}, s32[1024,1]{0,1:T(1,128)}, u32[]{:S(2)}) copy-start(s32[1024,1]{0,1:T(1,128)} %param.18) | copy-start | bytes 12292
  19.8 10.9 %copy-start.8 = (s32[1024]{0:T(1024)S(1)}, s32[1024]{0:T(1024)}, u32[]{:S(2)}) copy-start(s32[1024]{0:T(1024)} %param.19) | copy-start | bytes 12292
  38.2 10.2 %copy-start = (f32[1,2,16,16,1024]{4,3,2,1,0:T(8,128)S(1)}, f32[1,2,16,16,1024]{4,3,2,1,0:T(8,128)}, u32[]{:S(2)}) copy-start(f32[1,2,16,16,1024]{4,3,2,1,0:T(8,128)} %param.17) | copy-start | bytes 6291460
  38.2 10.2 %copy-start.1 = (f32[1,2,16,4096]{3,2,1,0:T(8,128)S(1)}, f32[1,2,16,4096]{3,2,1,0:T(8,128)}, u32[]{:S(2)}) copy-start(f32[1,2,16,4096]{3,2,1,0:T(8,128)} %param.15) | copy-start | bytes 1572868
  38.2 10.2 %copy-start.2 = (f32[1,2,16,4096]{3,2,1,0:T(8,128)S(1)}, f32[1,2,16,4096]{3,2,1,0:T(8,128)}, u32[]{:S(2)}) copy-start(f32[1,2,16,4096]{3,2,1,0:T(8,128)} %param.16) | copy-start | bytes 1572868
  38.3 10.2 %copy-start.3 = (f32[1,4096]{1,0:T(1,128)S(1)}, f32[1,4096]{1,0:T(1,128)}, u32[]{:S(2)}) copy-start(f32[1,4096]{1,0:T(1,128)} %c_ref.7) | copy-start | bytes 49156
  38.3 10.2 %copy-start.4 = (f32[2,4096]{1,0:T(2,128)S(1)}, f32[2,4096]{1,0:T(2,128)}, u32[]{:S(2)}) copy-start(f32[2,4096]{1,0:T(2,128)} %near.2.part_ref) | copy-start | bytes 98308
  48.4 14.9 %copy-start.10 = (s32[1,1024]{1,0:T(1,128)S(1)}, s32[1,1024]{1,0:T(1,128)}, u32[]{:S(2)}) copy-start(s32[1,1024]{1,0:T(1,128)} %get-tuple-element.11) | copy-start | bytes 12292
  55.8 0.6 copy-start.7
  56.4 18.5 %all-to-all-start.1 = ((f32[64,1,1024]{2,1,0:T(1,128)}), f32[64,1,1024]{2,1,0:T(1,128)S(1)}, u32[]{:S(2)}, u32[]{:S(2)}) async-start(f32[64,1,1024]{2,1,0:T(1,128)} %bitcast.14), calls=%async_computation.1 | async-start | bytes 524288 | tf_op jit(solution)/shard_map/all_to_all | solution.py:260
  76.8 4.2 %copy-start.5 = (f32[2,4096]{1,0:T(2,128)S(1)}, f32[2,4096]{1,0:T(2,128)}, u32[]{:S(2)}) copy-start(f32[2,4096]{1,0:T(2,128)} %near.3.part_ref) | copy-start | bytes 98308
  76.8 4.2 %copy-start.6 = (f32[1,2,4096]{2,1,0:T(2,128)S(1)}, f32[1,2,4096]{2,1,0:T(2,128)}, u32[]{:S(2)}) copy-start(f32[1,2,4096]{2,1,0:T(2,128)} %param.12) | copy-start | bytes 98308
  85.2 4.5 %collective-permute-start.2 = (f32[4096]{0:T(1024)S(1)}, f32[4096]{0:T(1024)S(1)}, u32[]{:S(2)}, u32[]{:S(2)}) collective-permute-start(f32[4096]{0:T(1024)S(1)} %bitcast.39), channel_id=1, source_target_pairs={{0,3},{1,0},{2,1},{3,2},{4,7},{5,4},{6,5},{7,6},{8,11},{9,8},{10,9... | collective-permute-start | bytes 49160 | tf_op jit(solution)/shard_map/ppermute | solution.py:354
  88.0 5.2 %collective-permute-start.1 = (f32[4096]{0:T(1024)S(1)}, f32[4096]{0:T(1024)S(1)}, u32[]{:S(2)}, u32[]{:S(2)}) collective-permute-start(f32[4096]{0:T(1024)S(1)} %bitcast.40), channel_id=1, source_target_pairs={{0,2},{1,3},{2,0},{3,1},{4,6},{5,7},{6,4},{7,5},{8,10},{9,11},{10,... | collective-permute-start | bytes 49160 | tf_op jit(solution)/shard_map/ppermute | solution.py:354
  88.8 4.9 %collective-permute-start = (f32[4096]{0:T(1024)S(1)}, f32[4096]{0:T(1024)S(1)}, u32[]{:S(2)}, u32[]{:S(2)}) collective-permute-start(f32[4096]{0:T(1024)S(1)} %bitcast.41), channel_id=1, source_target_pairs={{0,1},{1,2},{2,3},{3,0},{4,5},{5,6},{6,7},{7,4},{8,9},{9,10},{10,1... | collective-permute-start | bytes 49160 | tf_op jit(solution)/shard_map/ppermute | solution.py:354

commit v9 on v6

--- a/solution.py
+++ b/solution.py
@@ -35,6 +35,14 @@
     return lax.broadcasted_iota(jnp.int32, shape, dim)
 
 
+def _div(x, d):
+    return x >> (d.bit_length() - 1) if d & (d - 1) == 0 else x // d
+
+
+def _mod(x, d):
+    return x & (d - 1) if d & (d - 1) == 0 else x % d
+
+
 def _weighted_proj(u, c, pre, pim):
     wre = u[0:1] * c
     wim = u[1:2] * c
@@ -43,7 +51,7 @@
 
 def _proj_chunk(pw, off, clusters, width):
     n = pw.shape[1]
-    seg = ((_iota((n, clusters), 0) + off) // width) == _iota((n, clusters), 1)
+    seg = _div(_iota((n, clusters), 0) + off, width) == _iota((n, clusters), 1)
     return _xdot(pw, seg.astype(BF16))
 
 
@@ -52,15 +60,15 @@
     rows, groups = rr.shape
     wide = groups * clusters
     lane = _iota((rows, wide), 1)
-    grp = lane // clusters
+    grp = _div(lane, clusters)
     want = rr[:, 0:1]
     for g in range(1, groups):
         want = jnp.where(grp == g, rr[:, g : g + 1], want)
-    oh = ((lane % clusters).astype(F32) == want).astype(BF16)
-    tile = (_iota((clusters, wide), 0) == _iota((clusters, wide), 1) % clusters).astype(BF16)
+    oh = (_mod(lane, clusters).astype(F32) == want).astype(BF16)
+    tile = (_iota((clusters, wide), 0) == _mod(_iota((clusters, wide), 1), clusters)).astype(BF16)
     qw = _xdot(q, tile)
     qw = jnp.concatenate([qw] * groups, axis=0)
-    keep = (_iota((groups * rank2, wide), 0) // rank2) == (_iota((groups * rank2, wide), 1) // clusters)
+    keep = _div(_iota((groups * rank2, wide), 0), rank2) == _div(_iota((groups * rank2, wide), 1), clusters)
     qw = jnp.where(keep, qw, 0.0)
     r = lax.dot_general(oh, _split3(qw), (((1,), (1,)), ((), ())), preferred_element_type=F32)
     n = groups * rank2
@@ -119,10 +127,10 @@
     devices, cap = rr.shape
     per = cap // groups
     rows = devices * per
-    rep = ((_iota((rows, devices), 0) // per) == _iota((rows, devices), 1)).astype(BF16)
+    rep = (_div(_iota((rows, devices), 0), per) == _iota((rows, devices), 1)).astype(BF16)
     wide = jnp.dot(rep, rr.astype(BF16), preferred_element_type=F32)
-    keep = (_iota((rows, cap), 1) // groups) == (_iota((rows, cap), 0) % per)
-    fold = ((_iota((cap, groups), 0) % groups) == _iota((cap, groups), 1)).astype(BF16)
+    keep = _div(_iota((rows, cap), 1), groups) == _mod(_iota((rows, cap), 0), per)
+    fold = (_mod(_iota((cap, groups), 0), groups) == _iota((cap, groups), 1)).astype(BF16)
     return jnp.dot(jnp.where(keep, wide, 0.0).astype(BF16), fold, preferred_element_type=F32)
 
 
@@ -136,11 +144,11 @@
         off = pl.multiple_of(ci * CHUNK, CHUNK)
         sl = pl.ds(off, CHUNK)
         w = u_ref[:, sl] * c_ref[:, sl]
-        sel = _iota((width, CHUNK), 0) == ((_iota((width, CHUNK), 1) + off) % width)
+        sel = _iota((width, CHUNK), 0) == _mod(_iota((width, CHUNK), 1) + off, width)
         wm = jnp.concatenate(
             [jnp.where(sel, w[0:1], 0.0), jnp.where(sel, w[1:2], 0.0)], axis=0
         )
-        seg = ((_iota((CHUNK, clusters), 0) + off) // width) == _iota((CHUNK, clusters), 1)
+        seg = _div(_iota((CHUNK, clusters), 0) + off, width) == _iota((CHUNK, clusters), 1)
         return acc + _xdot(wm, seg.astype(BF16))
 
     wt = lax.fori_loop(0, cells // CHUNK, wt_body, jnp.zeros((2 * width, clusters), F32))
@@ -185,7 +193,7 @@
         cim = cpl_ref[1, :, :, sl]
         zre = jnp.sum(cre * qre - cim * qim, axis=1)
         zim = jnp.sum(cre * qim + cim * qre, axis=1)
-        seg = ((_iota((PAIR_CHUNK, clusters), 0) + off) // far) == _iota((PAIR_CHUNK, clusters), 1)
+        seg = _div(_iota((PAIR_CHUNK, clusters), 0) + off, far) == _iota((PAIR_CHUNK, clusters), 1)
         return z + _xdot(jnp.concatenate([zre, zim], axis=0), seg.astype(BF16))
 
     z = lax.fori_loop(0, npairs // PAIR_CHUNK, pair_body, jnp.zeros((2 * rank, clusters), F32))
@@ -194,7 +202,7 @@
     def cell_body(ci, acc):
         off = pl.multiple_of(ci * CHUNK, CHUNK)
         sl = pl.ds(off, CHUNK)
-        spread = _iota((clusters, CHUNK), 0) == ((_iota((clusters, CHUNK), 1) + off) // width)
+        spread = _iota((clusters, CHUNK), 0) == _div(_iota((clusters, CHUNK), 1) + off, width)
         zz = _sdot(z_split, spread.astype(BF16))
         zre = zz[:rank]
         zim = zz[rank:]

time: 91.2 us -> 88.5 us (0.970)
  Pallas kernels: 42.6 us -> 37.5 us
  waiting for transfers between devices: 9.85 us -> 12.3 us
    pallas_call x5, Pallas kernels: 42.6 us -> 37.5 us  [_call(): pl.pallas_call(kernel, out_shape=outs, compiler_params=pltpu.CompilerPara...]
    all_to_all x1, waiting for transfers between devices: 4.91 us -> 6.12 us  [_exchange_all(): got = lax.all_to_all(send.reshape(devices, total // devices), 'cells', 0, 0)]
    all_to_all x1, waiting for transfers between devices: 0.67 us -> 1.87 us  [_exchange(): got = lax.all_to_all(send.reshape(devices, total // devices), 'cells', 0, 0)]
  transfers between devices with their start and end apart: 5 -> 5, of which waited for: 4 -> 4; matrix products, arithmetic and copies ran while one was open for 2% -> 2% of each run, Pallas kernels for 24% -> 22%
where the time goes in v9:
time: 88.5 us; the launch traced here: 88.2 us
  Pallas kernels  37.5 us (42%)
  starting transfers between devices  23.5 us (27%)
  waiting for transfers between devices  12.3 us (14%)
  local copies, waits for them, and re-layouts  10 us (11%)
  other arithmetic  4.09 us (5%)
    pallas_call x5, Pallas kernels, _call(): pl.pallas_call(kernel, out_shape=outs, compiler_params=pltpu.CompilerPara...  37.5 us
    all_to_all x1, starting transfers between devices, _exchange_all(): got = lax.all_to_all(send.reshape(devices, total // devices), 'cells', 0, 0)  12.1 us
    all_to_all x1, starting transfers between devices, _exchange(): got = lax.all_to_all(send.reshape(devices, total // devices), 'cells', 0, 0)  6.95 us
    all_to_all x1, waiting for transfers between devices, _exchange_all(): got = lax.all_to_all(send.reshape(devices, total // devices), 'cells', 0, 0)  6.12 us
    ppermute x3, starting transfers between devices, per_device(): lax.ppermute(mine, 'freq', [(i, (i + k) % freqs) for i in range(freqs)])  4.45 us
    ppermute x3, waiting for transfers between devices, per_device(): lax.ppermute(mine, 'freq', [(i, (i + k) % freqs) for i in range(freqs)])  4.27 us
    gather x2, local copies, waits for them, and re-layouts, _exchange_all(): return (table.reshape(rank2, devices * clusters)[:, src_index], rr)  3.64 us
    gather x2, local copies, waits for them, and re-layouts, _exchange(): return got[idx].T  3.64 us
  transfers between devices with their start and end apart: 5, of which 4 were waited for; matrix products, arithmetic and copies ran while one was open for 2% of the time, Pallas kernels for 22%

profile of v9, /device:TPU:8, one launch (start us, length us, event | category | flops | bytes accessed | tf_op | source)
XLA Modules:
  0.0 88.2 jit_solution(5999619894037253977)
XLA Ops:
  0.6 4.4 %proj_pack.1 = (s32[1,1024]{1,0:T(1,128)}, f32[1088,128]{1,0:T(8,128)}) custom-call(f32[2,4096]{1,0:T(2,128)} %bitcast.40, f32[1,4096]{1,0:T(1,128)} %c_ref.7, f32[2,16,4096]{2,1,0:T(8,128)} %bitcast.35, s32[1,1024]{1,0:T(1,128)} %bitcast.50, s32[1,1024]{1,0:T(1,128)} %bitcast.49), custom_call_target="tpu_custom_call" | custom-call | flops 134742016 | bytes 1142784 | tf_op jit(solution)/shard_map/proj_pack/pallas_call | solution.py:251
  5.0 12.1 %all-to-all-start = ((f32[64,1,2176]{2,1,0:T(1,128)}), f32[64,1,2176]{2,1,0:T(1,128)S(1)}, u32[]{:S(2)}, u32[]{:S(2)}) async-start(f32[64,1,2176]{2,1,0:T(1,128)} %bitcast.39), calls=%async_computation | async-start | bytes 1114112 | tf_op jit(solution)/shard_map/all_to_all | solution.py:269
  17.1 0.7 subtract_bitcast_fusion
  17.8 0.1 broadcast_in_dim.10
  17.9 0.7 reshape.71.nlc_ref
  18.6 0.0 copy-start.1
  18.6 0.0 copy-start
  18.6 9.6 %near.2.part_ref = f32[2,4096]{1,0:T(2,128)} custom-call(f32[2,4096]{1,0:T(2,128)} %bitcast.41, f32[1,4096]{1,0:T(1,128)} %c_ref.7, f32[2,192,4096]{2,1,0:T(8,128)} %bitcast.29, s32[3,4096]{1,0:T(4,128)} %reshape.71.nlc_ref, f32[2,4096]{1,0:T(2,128)} %bitcast.42), custom_call_target="tpu_custom_call" | custom-call | flops 6291456 | bytes 6455296 | tf_op jit(solution)/shard_map/near/pallas_call | solution.py:251
  28.3 0.0 copy-done.1
  28.3 0.0 copy-done
  28.3 6.1 %all-to-all-done = f32[64,1,2176]{2,1,0:T(1,128)S(1)} async-done(((f32[64,1,2176]{2,1,0:T(1,128)}), f32[64,1,2176]{2,1,0:T(1,128)S(1)}, u32[]{:S(2)}, u32[]{:S(2)}) %all-to-all-start) | async-done | bytes 557088 | tf_op jit(solution)/shard_map/all_to_all | solution.py:269
  34.4 1.3 %reduce = f32[64,2176]{1,0:T(8,128)S(1)} reduce(f32[64,1,2176]{2,1,0:T(1,128)S(1)} %all-to-all-done, f32[]{:T(128)} %constant.59), dimensions={1}, to_apply=%all_to_all.13.reduce_sub_computation | reduce | bytes 1114116 | tf_op jit(solution)/shard_map/all_to_all | solution.py:269
  35.8 0.1 reshape.74
  35.8 0.6 slice.13
  36.5 0.2 reshape.75
  36.7 0.6 copy.19
  37.4 2.8 %gather_fusion = f32[1024,32]{1,0:T(8,128)S(1)} fusion(f32[32,4096]{0,1:T(8,128)S(1)} %bitcast.33, s32[1024]{0:T(1024)S(1)} %fusion), kind=kCustom, calls=%fused_computation | custom fusion | bytes 266240 | tf_op jit(solution)/shard_map/gather | solution.py:274
  40.2 0.8 copy.20
  41.0 0.0 copy-start.2
  41.0 8.2 %far_proj.1 = (f32[2,4096]{1,0:T(2,128)}, f32[512,128]{1,0:T(8,128)}) custom-call(f32[2,4096]{1,0:T(2,128)} %near.2.part_ref, f32[32,1024]{1,0:T(8,128)} %bitcast.44, f32[2,16,16,1024]{3,2,1,0:T(8,128)} %bitcast.31, f32[2,16,4096]{2,1,0:T(8,128)} %bitcast.37, f32[1,4096]{1,0:T(1,128)} %c_ref.7, f32[2,16,4096]{2,1,0:T(8,128)} %bitcast.36, f32[64,32]{1,0:T(8,128)} %bitcast.47), custom_call_target="tpu_custom_call" | custom-call | flops 4194304 | bytes 3629056 | tf_op jit(solution)/shard_map/far_proj/pallas_call | solution.py:251
  49.2 6.9 %all-to-all-start.1 = ((f32[64,1,1024]{2,1,0:T(1,128)}), f32[64,1,1024]{2,1,0:T(1,128)S(1)}, u32[]{:S(2)}, u32[]{:S(2)}) async-start(f32[64,1,1024]{2,1,0:T(1,128)} %bitcast.46), calls=%async_computation.1 | async-start | bytes 524288 | tf_op jit(solution)/shard_map/all_to_all | solution.py:262
  56.1 0.0 copy-done.2
  56.2 9.6 %near.3.part_ref = f32[2,4096]{1,0:T(2,128)} custom-call(f32[2,4096]{1,0:T(2,128)} %get-tuple-element.9.u_ref, f32[1,4096]{1,0:T(1,128)} %c_ref.7, f32[2,192,4096]{2,1,0:T(8,128)} %bitcast.30, s32[3,4096]{1,0:T(4,128)} %reshape.71.nlc_ref, f32[2,4096]{1,0:T(2,128)} %bitcast.43), custom_call_target="tpu_custom_call" | custom-call | flops 6291456 | bytes 6455296 | tf_op jit(solution)/shard_map/near/pallas_call | solution.py:251
  65.8 1.9 %all-to-all-done.1 = f32[64,1,1024]{2,1,0:T(1,128)S(1)} async-done(((f32[64,1,1024]{2,1,0:T(1,128)}), f32[64,1,1024]{2,1,0:T(1,128)S(1)}, u32[]{:S(2)}, u32[]{:S(2)}) %all-to-all-start.1) | async-done | bytes 262176 | tf_op jit(solution)/shard_map/all_to_all | solution.py:262
  67.6 0.6 reduce.1
  68.3 0.3 reshape.77
  68.6 2.8 %gather_fusion.1 = f32[1024,32]{1,0:T(8,128)S(1)} fusion(f32[2048,32]{1,0:T(8,128)S(1)} %reshape.77, s32[1024]{0:T(1024)S(1)} %broadcast_clamp_fusion), kind=kCustom, calls=%fused_computation.1 | custom fusion | bytes 266240 | tf_op jit(solution)/shard_map/gather | solution.py:264
  71.4 0.8 copy.23
  72.2 5.7 %far_grad.1 = (f32[2,4096]{1,0:T(2,128)}, f32[1,4096]{1,0:T(1,128)}) custom-call(f32[2,4096]{1,0:T(2,128)} %near.3.part_ref, f32[32,1024]{1,0:T(8,128)} %bitcast.45, f32[2,16,16,1024]{3,2,1,0:T(8,128)} %bitcast.32, f32[2,16,4096]{2,1,0:T(8,128)} %bitcast.38, f32[2,4096]{1,0:T(2,128)} %bitcast.48), custom_call_target="tpu_custom_call" | custom-call | flops 4194304 | bytes 2867200 | tf_op jit(solution)/shard_map/far_grad/pallas_call | solution.py:251
  78.0 2.8 %collective-permute-start.2 = (f32[4096]{0:T(1024)}, f32[4096]{0:T(1024)S(1)}, u32[]{:S(2)}, u32[]{:S(2)}) collective-permute-start(f32[4096]{0:T(1024)} %bitcast.54), channel_id=1, source_target_pairs={{0,3},{1,0},{2,1},{3,2},{4,7},{5,4},{6,5},{7,6},{8,11},{9,8},{10,9... | collective-permute-start | bytes 49160 | tf_op jit(solution)/shard_map/ppermute | solution.py:354
  80.7 0.8 collective-permute-start.1
  81.5 0.9 %collective-permute-start = (f32[4096]{0:T(1024)}, f32[4096]{0:T(1024)S(1)}, u32[]{:S(2)}, u32[]{:S(2)}) collective-permute-start(f32[4096]{0:T(1024)} %bitcast.56), channel_id=1, source_target_pairs={{0,1},{1,2},{2,3},{3,0},{4,5},{5,6},{6,7},{7,4},{8,9},{9,10},{10,1... | collective-permute-start | bytes 49160 | tf_op jit(solution)/shard_map/ppermute | solution.py:354
  82.4 0.0 collective-permute-done.2
  82.4 3.8 %collective-permute-done.1 = f32[4096]{0:T(1024)S(1)} collective-permute-done((f32[4096]{0:T(1024)}, f32[4096]{0:T(1024)S(1)}, u32[]{:S(2)}, u32[]{:S(2)}) %collective-permute-start.1) | collective-permute-done | bytes 16416 | tf_op jit(solution)/shard_map/ppermute | solution.py:354
  86.2 0.5 collective-permute-done
  86.7 0.8 pad_maximum_fusion
  87.5 0.7 dynamic-slice_add_fusion
  (5 shorter events, 0.1 us)
Async XLA Ops:
  5.0 29.4 %all-to-all-start = ((f32[64,1,2176]{2,1,0:T(1,128)}), f32[64,1,2176]{2,1,0:T(1,128)S(1)}, u32[]{:S(2)}, u32[]{:S(2)}) async-start(f32[64,1,2176]{2,1,0:T(1,128)} %bitcast.39), calls=%async_computation | async-start | bytes 1114112 | tf_op jit(solution)/shard_map/all_to_all | solution.py:269
  18.6 9.7 %copy-start.1 = (s32[1024,1]{0,1:T(1,128)S(1)}, s32[1024,1]{0,1:T(1,128)}, u32[]{:S(2)}) copy-start(s32[1024,1]{0,1:T(1,128)} %param.18) | copy-start | bytes 12292
  18.6 9.7 %copy-start = (s32[1024]{0:T(1024)S(1)}, s32[1024]{0:T(1024)}, u32[]{:S(2)}) copy-start(s32[1024]{0:T(1024)} %param.19) | copy-start | bytes 12292
  41.0 15.1 %copy-start.2 = (s32[1,1024]{1,0:T(1,128)S(1)}, s32[1,1024]{1,0:T(1,128)}, u32[]{:S(2)}) copy-start(s32[1,1024]{1,0:T(1,128)} %get-tuple-element.11) | copy-start | bytes 12292
  49.2 18.5 %all-to-all-start.1 = ((f32[64,1,1024]{2,1,0:T(1,128)}), f32[64,1,1024]{2,1,0:T(1,128)S(1)}, u32[]{:S(2)}, u32[]{:S(2)}) async-start(f32[64,1,1024]{2,1,0:T(1,128)} %bitcast.46), calls=%async_computation.1 | async-start | bytes 524288 | tf_op jit(solution)/shard_map/all_to_all | solution.py:262
  78.0 4.5 %collective-permute-start.2 = (f32[4096]{0:T(1024)}, f32[4096]{0:T(1024)S(1)}, u32[]{:S(2)}, u32[]{:S(2)}) collective-permute-start(f32[4096]{0:T(1024)} %bitcast.54), channel_id=1, source_target_pairs={{0,3},{1,0},{2,1},{3,2},{4,7},{5,4},{6,5},{7,6},{8,11},{9,8},{10,9... | collective-permute-start | bytes 49160 | tf_op jit(solution)/shard_map/ppermute | solution.py:354
  80.7 5.5 %collective-permute-start.1 = (f32[4096]{0:T(1024)}, f32[4096]{0:T(1024)S(1)}, u32[]{:S(2)}, u32[]{:S(2)}) collective-permute-start(f32[4096]{0:T(1024)} %bitcast.55), channel_id=1, source_target_pairs={{0,2},{1,3},{2,0},{3,1},{4,6},{5,7},{6,4},{7,5},{8,10},{9,11},{10,... | collective-permute-start | bytes 49160 | tf_op jit(solution)/shard_map/ppermute | solution.py:354
  81.5 5.2 %collective-permute-start = (f32[4096]{0:T(1024)}, f32[4096]{0:T(1024)S(1)}, u32[]{:S(2)}, u32[]{:S(2)}) collective-permute-start(f32[4096]{0:T(1024)} %bitcast.56), channel_id=1, source_target_pairs={{0,1},{1,2},{2,3},{3,0},{4,5},{5,6},{6,7},{7,4},{8,9},{9,10},{10,1... | collective-permute-start | bytes 49160 | tf_op jit(solution)/shard_map/ppermute | solution.py:354

commit v10 on v9

--- a/solution.py
+++ b/solution.py
@@ -8,8 +8,8 @@
 ITERS = 2
 F32 = jnp.float32
 BF16 = jnp.bfloat16
-CHUNK = 512
-PAIR_CHUNK = 128
+CHUNK = 1024
+PAIR_CHUNK = 256
 VMEM_LIMIT = 56 * 1024 * 1024
 
 

time: 88.5 us -> 85.3 us (0.964)
  Pallas kernels: 37.5 us -> 31.8 us
  waiting for transfers between devices: 12.3 us -> 14.7 us
    pallas_call x5, Pallas kernels: 37.5 us -> 31.8 us  [_call(): pl.pallas_call(kernel, out_shape=outs, compiler_params=pltpu.CompilerPara...]
    all_to_all x1, waiting for transfers between devices: 6.12 us -> 7.32 us  [_exchange_all(): got = lax.all_to_all(send.reshape(devices, total // devices), 'cells', 0, 0)]
    all_to_all x1, waiting for transfers between devices: 1.87 us -> 3.07 us  [_exchange(): got = lax.all_to_all(send.reshape(devices, total // devices), 'cells', 0, 0)]
  transfers between devices with their start and end apart: 5 -> 5, of which waited for: 4 -> 4; matrix products, arithmetic and copies ran while one was open for 2% -> 2% of each run, Pallas kernels for 22% -> 20%
where the time goes in v10:
time: 85.3 us; the launch traced here: 84.9 us
  Pallas kernels  31.8 us (37%)
  starting transfers between devices  23.5 us (28%)
  waiting for transfers between devices  14.7 us (17%)
  local copies, waits for them, and re-layouts  10 us (12%)
  other arithmetic  4.09 us (5%)
    pallas_call x5, Pallas kernels, _call(): pl.pallas_call(kernel, out_shape=outs, compiler_params=pltpu.CompilerPara...  31.8 us
    all_to_all x1, starting transfers between devices, _exchange_all(): got = lax.all_to_all(send.reshape(devices, total // devices), 'cells', 0, 0)  12.1 us
    all_to_all x1, waiting for transfers between devices, _exchange_all(): got = lax.all_to_all(send.reshape(devices, total // devices), 'cells', 0, 0)  7.32 us
    all_to_all x1, starting transfers between devices, _exchange(): got = lax.all_to_all(send.reshape(devices, total // devices), 'cells', 0, 0)  6.96 us
    ppermute x3, starting transfers between devices, per_device(): lax.ppermute(mine, 'freq', [(i, (i + k) % freqs) for i in range(freqs)])  4.43 us
    ppermute x3, waiting for transfers between devices, per_device(): lax.ppermute(mine, 'freq', [(i, (i + k) % freqs) for i in range(freqs)])  4.27 us
    gather x2, local copies, waits for them, and re-layouts, _exchange_all(): return (table.reshape(rank2, devices * clusters)[:, src_index], rr)  3.64 us
    gather x2, local copies, waits for them, and re-layouts, _exchange(): return got[idx].T  3.64 us
  transfers between devices with their start and end apart: 5, of which 4 were waited for; matrix products, arithmetic and copies ran while one was open for 2% of the time, Pallas kernels for 20%

profile of v10, /device:TPU:8, one launch (start us, length us, event | category | flops | bytes accessed | tf_op | source)
XLA Modules:
  0.0 84.9 jit_solution(7976232633593764501)
XLA Ops:
  0.6 3.8 %proj_pack.1 = (s32[1,1024]{1,0:T(1,128)}, f32[1088,128]{1,0:T(8,128)}) custom-call(f32[2,4096]{1,0:T(2,128)} %bitcast.40, f32[1,4096]{1,0:T(1,128)} %c_ref.7, f32[2,16,4096]{2,1,0:T(8,128)} %bitcast.35, s32[1,1024]{1,0:T(1,128)} %bitcast.50, s32[1,1024]{1,0:T(1,128)} %bitcast.49), custom_call_target="tpu_custom_call" | custom-call | flops 134742016 | bytes 1142784 | tf_op jit(solution)/shard_map/proj_pack/pallas_call | solution.py:251
  4.5 12.1 %all-to-all-start = ((f32[64,1,2176]{2,1,0:T(1,128)}), f32[64,1,2176]{2,1,0:T(1,128)S(1)}, u32[]{:S(2)}, u32[]{:S(2)}) async-start(f32[64,1,2176]{2,1,0:T(1,128)} %bitcast.39), calls=%async_computation | async-start | bytes 1114112 | tf_op jit(solution)/shard_map/all_to_all | solution.py:269
  16.6 0.7 subtract_bitcast_fusion
  17.3 0.1 broadcast_in_dim.10
  17.4 0.7 reshape.71.nlc_ref
  18.1 0.0 copy-start.1
  18.1 0.0 copy-start
  18.1 8.4 %near.2.part_ref = f32[2,4096]{1,0:T(2,128)} custom-call(f32[2,4096]{1,0:T(2,128)} %bitcast.41, f32[1,4096]{1,0:T(1,128)} %c_ref.7, f32[2,192,4096]{2,1,0:T(8,128)} %bitcast.29, s32[3,4096]{1,0:T(4,128)} %reshape.71.nlc_ref, f32[2,4096]{1,0:T(2,128)} %bitcast.42), custom_call_target="tpu_custom_call" | custom-call | flops 6291456 | bytes 6455296 | tf_op jit(solution)/shard_map/near/pallas_call | solution.py:251
  26.5 0.0 copy-done.1
  26.5 0.0 copy-done
  26.6 7.3 %all-to-all-done = f32[64,1,2176]{2,1,0:T(1,128)S(1)} async-done(((f32[64,1,2176]{2,1,0:T(1,128)}), f32[64,1,2176]{2,1,0:T(1,128)S(1)}, u32[]{:S(2)}, u32[]{:S(2)}) %all-to-all-start) | async-done | bytes 557088 | tf_op jit(solution)/shard_map/all_to_all | solution.py:269
  33.9 1.3 %reduce = f32[64,2176]{1,0:T(8,128)S(1)} reduce(f32[64,1,2176]{2,1,0:T(1,128)S(1)} %all-to-all-done, f32[]{:T(128)} %constant.59), dimensions={1}, to_apply=%all_to_all.13.reduce_sub_computation | reduce | bytes 1114116 | tf_op jit(solution)/shard_map/all_to_all | solution.py:269
  35.2 0.1 reshape.74
  35.3 0.6 slice.13
  36.0 0.2 reshape.75
  36.2 0.6 copy.19
  36.8 2.8 %gather_fusion = f32[1024,32]{1,0:T(8,128)S(1)} fusion(f32[32,4096]{0,1:T(8,128)S(1)} %bitcast.33, s32[1024]{0:T(1024)S(1)} %fusion), kind=kCustom, calls=%fused_computation | custom fusion | bytes 266240 | tf_op jit(solution)/shard_map/gather | solution.py:274
  39.6 0.8 copy.20
  40.5 0.0 copy-start.2
  40.5 6.6 %far_proj.1 = (f32[2,4096]{1,0:T(2,128)}, f32[512,128]{1,0:T(8,128)}) custom-call(f32[2,4096]{1,0:T(2,128)} %near.2.part_ref, f32[32,1024]{1,0:T(8,128)} %bitcast.44, f32[2,16,16,1024]{3,2,1,0:T(8,128)} %bitcast.31, f32[2,16,4096]{2,1,0:T(8,128)} %bitcast.37, f32[1,4096]{1,0:T(1,128)} %c_ref.7, f32[2,16,4096]{2,1,0:T(8,128)} %bitcast.36, f32[64,32]{1,0:T(8,128)} %bitcast.47), custom_call_target="tpu_custom_call" | custom-call | flops 4194304 | bytes 3629056 | tf_op jit(solution)/shard_map/far_proj/pallas_call | solution.py:251
  47.0 7.0 %all-to-all-start.1 = ((f32[64,1,1024]{2,1,0:T(1,128)}), f32[64,1,1024]{2,1,0:T(1,128)S(1)}, u32[]{:S(2)}, u32[]{:S(2)}) async-start(f32[64,1,1024]{2,1,0:T(1,128)} %bitcast.46), calls=%async_computation.1 | async-start | bytes 524288 | tf_op jit(solution)/shard_map/all_to_all | solution.py:262
  54.0 0.0 copy-done.2
  54.1 8.4 %near.3.part_ref = f32[2,4096]{1,0:T(2,128)} custom-call(f32[2,4096]{1,0:T(2,128)} %get-tuple-element.9.u_ref, f32[1,4096]{1,0:T(1,128)} %c_ref.7, f32[2,192,4096]{2,1,0:T(8,128)} %bitcast.30, s32[3,4096]{1,0:T(4,128)} %reshape.71.nlc_ref, f32[2,4096]{1,0:T(2,128)} %bitcast.43), custom_call_target="tpu_custom_call" | custom-call | flops 6291456 | bytes 6455296 | tf_op jit(solution)/shard_map/near/pallas_call | solution.py:251
  62.5 3.1 %all-to-all-done.1 = f32[64,1,1024]{2,1,0:T(1,128)S(1)} async-done(((f32[64,1,1024]{2,1,0:T(1,128)}), f32[64,1,1024]{2,1,0:T(1,128)S(1)}, u32[]{:S(2)}, u32[]{:S(2)}) %all-to-all-start.1) | async-done | bytes 262176 | tf_op jit(solution)/shard_map/all_to_all | solution.py:262
  65.5 0.6 reduce.1
  66.2 0.3 reshape.77
  66.5 2.8 %gather_fusion.1 = f32[1024,32]{1,0:T(8,128)S(1)} fusion(f32[2048,32]{1,0:T(8,128)S(1)} %reshape.77, s32[1024]{0:T(1024)S(1)} %broadcast_clamp_fusion), kind=kCustom, calls=%fused_computation.1 | custom fusion | bytes 266240 | tf_op jit(solution)/shard_map/gather | solution.py:264
  69.3 0.8 copy.23
  70.1 4.6 %far_grad.1 = (f32[2,4096]{1,0:T(2,128)}, f32[1,4096]{1,0:T(1,128)}) custom-call(f32[2,4096]{1,0:T(2,128)} %near.3.part_ref, f32[32,1024]{1,0:T(8,128)} %bitcast.45, f32[2,16,16,1024]{3,2,1,0:T(8,128)} %bitcast.32, f32[2,16,4096]{2,1,0:T(8,128)} %bitcast.38, f32[2,4096]{1,0:T(2,128)} %bitcast.48), custom_call_target="tpu_custom_call" | custom-call | flops 4194304 | bytes 2867200 | tf_op jit(solution)/shard_map/far_grad/pallas_call | solution.py:251
  74.7 2.7 %collective-permute-start.2 = (f32[4096]{0:T(1024)}, f32[4096]{0:T(1024)S(1)}, u32[]{:S(2)}, u32[]{:S(2)}) collective-permute-start(f32[4096]{0:T(1024)} %bitcast.54), channel_id=1, source_target_pairs={{0,3},{1,0},{2,1},{3,2},{4,7},{5,4},{6,5},{7,6},{8,11},{9,8},{10,9... | collective-permute-start | bytes 49160 | tf_op jit(solution)/shard_map/ppermute | solution.py:354
  77.5 0.8 collective-permute-start.1
  78.3 0.9 %collective-permute-start = (f32[4096]{0:T(1024)}, f32[4096]{0:T(1024)S(1)}, u32[]{:S(2)}, u32[]{:S(2)}) collective-permute-start(f32[4096]{0:T(1024)} %bitcast.56), channel_id=1, source_target_pairs={{0,1},{1,2},{2,3},{3,0},{4,5},{5,6},{6,7},{7,4},{8,9},{9,10},{10,1... | collective-permute-start | bytes 49160 | tf_op jit(solution)/shard_map/ppermute | solution.py:354
  79.1 0.0 collective-permute-done.2
  79.1 3.8 %collective-permute-done.1 = f32[4096]{0:T(1024)S(1)} collective-permute-done((f32[4096]{0:T(1024)}, f32[4096]{0:T(1024)S(1)}, u32[]{:S(2)}, u32[]{:S(2)}) %collective-permute-start.1) | collective-permute-done | bytes 16416 | tf_op jit(solution)/shard_map/ppermute | solution.py:354
  82.9 0.5 collective-permute-done
  83.4 0.8 pad_maximum_fusion
  84.2 0.7 dynamic-slice_add_fusion
  (5 shorter events, 0.1 us)
Async XLA Ops:
  4.5 29.4 %all-to-all-start = ((f32[64,1,2176]{2,1,0:T(1,128)}), f32[64,1,2176]{2,1,0:T(1,128)S(1)}, u32[]{:S(2)}, u32[]{:S(2)}) async-start(f32[64,1,2176]{2,1,0:T(1,128)} %bitcast.39), calls=%async_computation | async-start | bytes 1114112 | tf_op jit(solution)/shard_map/all_to_all | solution.py:269
  18.1 8.4 %copy-start.1 = (s32[1024,1]{0,1:T(1,128)S(1)}, s32[1024,1]{0,1:T(1,128)}, u32[]{:S(2)}) copy-start(s32[1024,1]{0,1:T(1,128)} %param.18) | copy-start | bytes 12292
  18.1 8.5 %copy-start = (s32[1024]{0:T(1024)S(1)}, s32[1024]{0:T(1024)}, u32[]{:S(2)}) copy-start(s32[1024]{0:T(1024)} %param.19) | copy-start | bytes 12292
  40.5 13.6 %copy-start.2 = (s32[1,1024]{1,0:T(1,128)S(1)}, s32[1,1024]{1,0:T(1,128)}, u32[]{:S(2)}) copy-start(s32[1,1024]{1,0:T(1,128)} %get-tuple-element.11) | copy-start | bytes 12292
  47.0 18.5 %all-to-all-start.1 = ((f32[64,1,1024]{2,1,0:T(1,128)}), f32[64,1,1024]{2,1,0:T(1,128)S(1)}, u32[]{:S(2)}, u32[]{:S(2)}) async-start(f32[64,1,1024]{2,1,0:T(1,128)} %bitcast.46), calls=%async_computation.1 | async-start | bytes 524288 | tf_op jit(solution)/shard_map/all_to_all | solution.py:262
  74.7 4.4 %collective-permute-start.2 = (f32[4096]{0:T(1024)}, f32[4096]{0:T(1024)S(1)}, u32[]{:S(2)}, u32[]{:S(2)}) collective-permute-start(f32[4096]{0:T(1024)} %bitcast.54), channel_id=1, source_target_pairs={{0,3},{1,0},{2,1},{3,2},{4,7},{5,4},{6,5},{7,6},{8,11},{9,8},{10,9... | collective-permute-start | bytes 49160 | tf_op jit(solution)/shard_map/ppermute | solution.py:354
  77.5 5.5 %collective-permute-start.1 = (f32[4096]{0:T(1024)}, f32[4096]{0:T(1024)S(1)}, u32[]{:S(2)}, u32[]{:S(2)}) collective-permute-start(f32[4096]{0:T(1024)} %bitcast.55), channel_id=1, source_target_pairs={{0,2},{1,3},{2,0},{3,1},{4,6},{5,7},{6,4},{7,5},{8,10},{9,11},{10,... | collective-permute-start | bytes 49160 | tf_op jit(solution)/shard_map/ppermute | solution.py:354
  78.3 5.2 %collective-permute-start = (f32[4096]{0:T(1024)}, f32[4096]{0:T(1024)S(1)}, u32[]{:S(2)}, u32[]{:S(2)}) collective-permute-start(f32[4096]{0:T(1024)} %bitcast.56), channel_id=1, source_target_pairs={{0,1},{1,2},{2,3},{3,0},{4,5},{5,6},{6,7},{7,4},{8,9},{9,10},{10,1... | collective-permute-start | bytes 49160 | tf_op jit(solution)/shard_map/ppermute | solution.py:354

commit v11 on v10

--- a/solution.py
+++ b/solution.py
@@ -8,8 +8,8 @@
 ITERS = 2
 F32 = jnp.float32
 BF16 = jnp.bfloat16
-CHUNK = 1024
-PAIR_CHUNK = 256
+CHUNK = 2048
+PAIR_CHUNK = 512
 VMEM_LIMIT = 56 * 1024 * 1024
 
 

time: 85.3 us -> 83.8 us (0.982)
  Pallas kernels: 31.8 us -> 29.4 us
  waiting for transfers between devices: 14.7 us -> 15.7 us
    pallas_call x5, Pallas kernels: 31.8 us -> 29.4 us  [_call(): pl.pallas_call(kernel, out_shape=outs, compiler_params=pltpu.CompilerPara...]
  transfers between devices with their start and end apart: 5 -> 5, of which waited for: 4 -> 4; matrix products, arithmetic and copies ran while one was open for 2% -> 2% of each run, Pallas kernels for 20% -> 19%
where the time goes in v11:
time: 83.8 us; the launch traced here: 83.5 us
  Pallas kernels  29.4 us (35%)
  starting transfers between devices  23.5 us (28%)
  waiting for transfers between devices  15.7 us (19%)
  local copies, waits for them, and re-layouts  10 us (12%)
  other arithmetic  4.09 us (5%)
    pallas_call x5, Pallas kernels, _call(): pl.pallas_call(kernel, out_shape=outs, compiler_params=pltpu.CompilerPara...  29.4 us
    all_to_all x1, starting transfers between devices, _exchange_all(): got = lax.all_to_all(send.reshape(devices, total // devices), 'cells', 0, 0)  12.1 us
    all_to_all x1, waiting for transfers between devices, _exchange_all(): got = lax.all_to_all(send.reshape(devices, total // devices), 'cells', 0, 0)  7.82 us
    all_to_all x1, starting transfers between devices, _exchange(): got = lax.all_to_all(send.reshape(devices, total // devices), 'cells', 0, 0)  6.96 us
    ppermute x3, starting transfers between devices, per_device(): lax.ppermute(mine, 'freq', [(i, (i + k) % freqs) for i in range(freqs)])  4.44 us
    ppermute x3, waiting for transfers between devices, per_device(): lax.ppermute(mine, 'freq', [(i, (i + k) % freqs) for i in range(freqs)])  4.27 us
    gather x2, local copies, waits for them, and re-layouts, _exchange(): return got[idx].T  3.64 us
    gather x2, local copies, waits for them, and re-layouts, _exchange_all(): return (table.reshape(rank2, devices * clusters)[:, src_index], rr)  3.64 us
  transfers between devices with their start and end apart: 5, of which 4 were waited for; matrix products, arithmetic and copies ran while one was open for 2% of the time, Pallas kernels for 19%

profile of v11, /device:TPU:8, one launch (start us, length us, event | category | flops | bytes accessed | tf_op | source)
XLA Modules:
  0.0 83.5 jit_solution(8832370470955440641)
XLA Ops:
  0.6 3.5 %proj_pack.1 = (s32[1,1024]{1,0:T(1,128)}, f32[1088,128]{1,0:T(8,128)}) custom-call(f32[2,4096]{1,0:T(2,128)} %bitcast.40, f32[1,4096]{1,0:T(1,128)} %c_ref.7, f32[2,16,4096]{2,1,0:T(8,128)} %bitcast.35, s32[1,1024]{1,0:T(1,128)} %bitcast.50, s32[1,1024]{1,0:T(1,128)} %bitcast.49), custom_call_target="tpu_custom_call" | custom-call | flops 134742016 | bytes 1142784 | tf_op jit(solution)/shard_map/proj_pack/pallas_call | solution.py:251
  4.1 12.1 %all-to-all-start = ((f32[64,1,2176]{2,1,0:T(1,128)}), f32[64,1,2176]{2,1,0:T(1,128)S(1)}, u32[]{:S(2)}, u32[]{:S(2)}) async-start(f32[64,1,2176]{2,1,0:T(1,128)} %bitcast.39), calls=%async_computation | async-start | bytes 1114112 | tf_op jit(solution)/shard_map/all_to_all | solution.py:269
  16.3 0.7 subtract_bitcast_fusion
  17.0 0.1 broadcast_in_dim.10
  17.1 0.7 reshape.71.nlc_ref
  17.8 0.0 copy-start.1
  17.8 0.0 copy-start
  17.8 7.9 %near.2.part_ref = f32[2,4096]{1,0:T(2,128)} custom-call(f32[2,4096]{1,0:T(2,128)} %bitcast.41, f32[1,4096]{1,0:T(1,128)} %c_ref.7, f32[2,192,4096]{2,1,0:T(8,128)} %bitcast.29, s32[3,4096]{1,0:T(4,128)} %reshape.71.nlc_ref, f32[2,4096]{1,0:T(2,128)} %bitcast.42), custom_call_target="tpu_custom_call" | custom-call | flops 6291456 | bytes 6455296 | tf_op jit(solution)/shard_map/near/pallas_call | solution.py:251
  25.7 0.0 copy-done.1
  25.7 0.0 copy-done
  25.8 7.8 %all-to-all-done = f32[64,1,2176]{2,1,0:T(1,128)S(1)} async-done(((f32[64,1,2176]{2,1,0:T(1,128)}), f32[64,1,2176]{2,1,0:T(1,128)S(1)}, u32[]{:S(2)}, u32[]{:S(2)}) %all-to-all-start) | async-done | bytes 557088 | tf_op jit(solution)/shard_map/all_to_all | solution.py:269
  33.6 1.3 %reduce = f32[64,2176]{1,0:T(8,128)S(1)} reduce(f32[64,1,2176]{2,1,0:T(1,128)S(1)} %all-to-all-done, f32[]{:T(128)} %constant.59), dimensions={1}, to_apply=%all_to_all.13.reduce_sub_computation | reduce | bytes 1114116 | tf_op jit(solution)/shard_map/all_to_all | solution.py:269
  34.9 0.1 reshape.74
  35.0 0.6 slice.13
  35.7 0.2 reshape.75
  35.9 0.6 copy.19
  36.5 2.8 %gather_fusion = f32[1024,32]{1,0:T(8,128)S(1)} fusion(f32[32,4096]{0,1:T(8,128)S(1)} %bitcast.33, s32[1024]{0:T(1024)S(1)} %fusion), kind=kCustom, calls=%fused_computation | custom fusion | bytes 266240 | tf_op jit(solution)/shard_map/gather | solution.py:274
  39.3 0.8 copy.20
  40.2 0.0 copy-start.2
  40.2 5.9 %far_proj.1 = (f32[2,4096]{1,0:T(2,128)}, f32[512,128]{1,0:T(8,128)}) custom-call(f32[2,4096]{1,0:T(2,128)} %near.2.part_ref, f32[32,1024]{1,0:T(8,128)} %bitcast.44, f32[2,16,16,1024]{3,2,1,0:T(8,128)} %bitcast.31, f32[2,16,4096]{2,1,0:T(8,128)} %bitcast.37, f32[1,4096]{1,0:T(1,128)} %c_ref.7, f32[2,16,4096]{2,1,0:T(8,128)} %bitcast.36, f32[64,32]{1,0:T(8,128)} %bitcast.47), custom_call_target="tpu_custom_call" | custom-call | flops 4194304 | bytes 3629056 | tf_op jit(solution)/shard_map/far_proj/pallas_call | solution.py:251
  46.0 7.0 %all-to-all-start.1 = ((f32[64,1,1024]{2,1,0:T(1,128)}), f32[64,1,1024]{2,1,0:T(1,128)S(1)}, u32[]{:S(2)}, u32[]{:S(2)}) async-start(f32[64,1,1024]{2,1,0:T(1,128)} %bitcast.46), calls=%async_computation.1 | async-start | bytes 524288 | tf_op jit(solution)/shard_map/all_to_all | solution.py:262
  53.0 0.0 copy-done.2
  53.1 7.9 %near.3.part_ref = f32[2,4096]{1,0:T(2,128)} custom-call(f32[2,4096]{1,0:T(2,128)} %get-tuple-element.9.u_ref, f32[1,4096]{1,0:T(1,128)} %c_ref.7, f32[2,192,4096]{2,1,0:T(8,128)} %bitcast.30, s32[3,4096]{1,0:T(4,128)} %reshape.71.nlc_ref, f32[2,4096]{1,0:T(2,128)} %bitcast.43), custom_call_target="tpu_custom_call" | custom-call | flops 6291456 | bytes 6455296 | tf_op jit(solution)/shard_map/near/pallas_call | solution.py:251
  61.0 3.6 %all-to-all-done.1 = f32[64,1,1024]{2,1,0:T(1,128)S(1)} async-done(((f32[64,1,1024]{2,1,0:T(1,128)}), f32[64,1,1024]{2,1,0:T(1,128)S(1)}, u32[]{:S(2)}, u32[]{:S(2)}) %all-to-all-start.1) | async-done | bytes 262176 | tf_op jit(solution)/shard_map/all_to_all | solution.py:262
  64.5 0.6 reduce.1
  65.1 0.3 reshape.77
  65.5 2.8 %gather_fusion.1 = f32[1024,32]{1,0:T(8,128)S(1)} fusion(f32[2048,32]{1,0:T(8,128)S(1)} %reshape.77, s32[1024]{0:T(1024)S(1)} %broadcast_clamp_fusion), kind=kCustom, calls=%fused_computation.1 | custom fusion | bytes 266240 | tf_op jit(solution)/shard_map/gather | solution.py:264
  68.3 0.8 copy.23
  69.1 4.1 %far_grad.1 = (f32[2,4096]{1,0:T(2,128)}, f32[1,4096]{1,0:T(1,128)}) custom-call(f32[2,4096]{1,0:T(2,128)} %near.3.part_ref, f32[32,1024]{1,0:T(8,128)} %bitcast.45, f32[2,16,16,1024]{3,2,1,0:T(8,128)} %bitcast.32, f32[2,16,4096]{2,1,0:T(8,128)} %bitcast.38, f32[2,4096]{1,0:T(2,128)} %bitcast.48), custom_call_target="tpu_custom_call" | custom-call | flops 4194304 | bytes 2867200 | tf_op jit(solution)/shard_map/far_grad/pallas_call | solution.py:251
  73.3 2.8 %collective-permute-start.2 = (f32[4096]{0:T(1024)}, f32[4096]{0:T(1024)S(1)}, u32[]{:S(2)}, u32[]{:S(2)}) collective-permute-start(f32[4096]{0:T(1024)} %bitcast.54), channel_id=1, source_target_pairs={{0,3},{1,0},{2,1},{3,2},{4,7},{5,4},{6,5},{7,6},{8,11},{9,8},{10,9... | collective-permute-start | bytes 49160 | tf_op jit(solution)/shard_map/ppermute | solution.py:354
  76.0 0.8 collective-permute-start.1
  76.8 0.9 %collective-permute-start = (f32[4096]{0:T(1024)}, f32[4096]{0:T(1024)S(1)}, u32[]{:S(2)}, u32[]{:S(2)}) collective-permute-start(f32[4096]{0:T(1024)} %bitcast.56), channel_id=1, source_target_pairs={{0,1},{1,2},{2,3},{3,0},{4,5},{5,6},{6,7},{7,4},{8,9},{9,10},{10,1... | collective-permute-start | bytes 49160 | tf_op jit(solution)/shard_map/ppermute | solution.py:354
  77.7 0.0 collective-permute-done.2
  77.7 3.8 %collective-permute-done.1 = f32[4096]{0:T(1024)S(1)} collective-permute-done((f32[4096]{0:T(1024)}, f32[4096]{0:T(1024)S(1)}, u32[]{:S(2)}, u32[]{:S(2)}) %collective-permute-start.1) | collective-permute-done | bytes 16416 | tf_op jit(solution)/shard_map/ppermute | solution.py:354
  81.5 0.5 collective-permute-done
  82.0 0.8 pad_maximum_fusion
  82.8 0.7 dynamic-slice_add_fusion
  (5 shorter events, 0.1 us)
Async XLA Ops:
  4.1 29.4 %all-to-all-start = ((f32[64,1,2176]{2,1,0:T(1,128)}), f32[64,1,2176]{2,1,0:T(1,128)S(1)}, u32[]{:S(2)}, u32[]{:S(2)}) async-start(f32[64,1,2176]{2,1,0:T(1,128)} %bitcast.39), calls=%async_computation | async-start | bytes 1114112 | tf_op jit(solution)/shard_map/all_to_all | solution.py:269
  17.8 7.9 %copy-start.1 = (s32[1024,1]{0,1:T(1,128)S(1)}, s32[1024,1]{0,1:T(1,128)}, u32[]{:S(2)}) copy-start(s32[1024,1]{0,1:T(1,128)} %param.18) | copy-start | bytes 12292
  17.8 8.0 %copy-start = (s32[1024]{0:T(1024)S(1)}, s32[1024]{0:T(1024)}, u32[]{:S(2)}) copy-start(s32[1024]{0:T(1024)} %param.19) | copy-start | bytes 12292
  40.2 12.9 %copy-start.2 = (s32[1,1024]{1,0:T(1,128)S(1)}, s32[1,1024]{1,0:T(1,128)}, u32[]{:S(2)}) copy-start(s32[1,1024]{1,0:T(1,128)} %get-tuple-element.11) | copy-start | bytes 12292
  46.0 18.5 %all-to-all-start.1 = ((f32[64,1,1024]{2,1,0:T(1,128)}), f32[64,1,1024]{2,1,0:T(1,128)S(1)}, u32[]{:S(2)}, u32[]{:S(2)}) async-start(f32[64,1,1024]{2,1,0:T(1,128)} %bitcast.46), calls=%async_computation.1 | async-start | bytes 524288 | tf_op jit(solution)/shard_map/all_to_all | solution.py:262
  73.3 4.4 %collective-permute-start.2 = (f32[4096]{0:T(1024)}, f32[4096]{0:T(1024)S(1)}, u32[]{:S(2)}, u32[]{:S(2)}) collective-permute-start(f32[4096]{0:T(1024)} %bitcast.54), channel_id=1, source_target_pairs={{0,3},{1,0},{2,1},{3,2},{4,7},{5,4},{6,5},{7,6},{8,11},{9,8},{10,9... | collective-permute-start | bytes 49160 | tf_op jit(solution)/shard_map/ppermute | solution.py:354
  76.0 5.5 %collective-permute-start.1 = (f32[4096]{0:T(1024)}, f32[4096]{0:T(1024)S(1)}, u32[]{:S(2)}, u32[]{:S(2)}) collective-permute-start(f32[4096]{0:T(1024)} %bitcast.55), channel_id=1, source_target_pairs={{0,2},{1,3},{2,0},{3,1},{4,6},{5,7},{6,4},{7,5},{8,10},{9,11},{10,... | collective-permute-start | bytes 49160 | tf_op jit(solution)/shard_map/ppermute | solution.py:354
  76.8 5.2 %collective-permute-start = (f32[4096]{0:T(1024)}, f32[4096]{0:T(1024)S(1)}, u32[]{:S(2)}, u32[]{:S(2)}) collective-permute-start(f32[4096]{0:T(1024)} %bitcast.56), channel_id=1, source_target_pairs={{0,1},{1,2},{2,3},{3,0},{4,5},{5,6},{6,7},{7,4},{8,9},{9,10},{10,1... | collective-permute-start | bytes 49160 | tf_op jit(solution)/shard_map/ppermute | solution.py:354

commit v12 on v11

--- a/solution.py
+++ b/solution.py
@@ -8,8 +8,8 @@
 ITERS = 2
 F32 = jnp.float32
 BF16 = jnp.bfloat16
-CHUNK = 2048
-PAIR_CHUNK = 512
+CHUNK = 4096
+PAIR_CHUNK = 1024
 VMEM_LIMIT = 56 * 1024 * 1024
 
 

time: 83.8 us -> 82.6 us (0.986)
  waiting for transfers between devices: 15.7 us -> 14.1 us
  transfers between devices with their start and end apart: 5 -> 5, of which waited for: 4 -> 4; matrix products, arithmetic and copies ran while one was open for 2% -> 2% of each run, Pallas kernels for 19% -> 21%
where the time goes in v12:
time: 82.6 us; the launch traced here: 82.2 us
  Pallas kernels  29.7 us (36%)
  starting transfers between devices  23.5 us (28%)
  waiting for transfers between devices  14.1 us (17%)
  local copies, waits for them, and re-layouts  10 us (12%)
  other arithmetic  4.09 us (5%)
    pallas_call x5, Pallas kernels, _call(): pl.pallas_call(kernel, out_shape=outs, compiler_params=pltpu.CompilerPara...  29.7 us
    all_to_all x1, starting transfers between devices, _exchange_all(): got = lax.all_to_all(send.reshape(devices, total // devices), 'cells', 0, 0)  12.1 us
    all_to_all x1, waiting for transfers between devices, _exchange_all(): got = lax.all_to_all(send.reshape(devices, total // devices), 'cells', 0, 0)  7.03 us
    all_to_all x1, starting transfers between devices, _exchange(): got = lax.all_to_all(send.reshape(devices, total // devices), 'cells', 0, 0)  6.96 us
    ppermute x3, starting transfers between devices, per_device(): lax.ppermute(mine, 'freq', [(i, (i + k) % freqs) for i in range(freqs)])  4.44 us
    ppermute x3, waiting for transfers between devices, per_device(): lax.ppermute(mine, 'freq', [(i, (i + k) % freqs) for i in range(freqs)])  4.27 us
    gather x2, local copies, waits for them, and re-layouts, _exchange(): return got[idx].T  3.64 us
    gather x2, local copies, waits for them, and re-layouts, _exchange_all(): return (table.reshape(rank2, devices * clusters)[:, src_index], rr)  3.64 us
  transfers between devices with their start and end apart: 5, of which 4 were waited for; matrix products, arithmetic and copies ran while one was open for 2% of the time, Pallas kernels for 21%

profile of v12, /device:TPU:8, one launch (start us, length us, event | category | flops | bytes accessed | tf_op | source)
XLA Modules:
  0.0 82.2 jit_solution(16276050267233246741)
XLA Ops:
  0.6 3.1 %proj_pack.1 = (s32[1,1024]{1,0:T(1,128)}, f32[1088,128]{1,0:T(8,128)}) custom-call(f32[2,4096]{1,0:T(2,128)} %bitcast.40, f32[1,4096]{1,0:T(1,128)} %c_ref.7, f32[2,16,4096]{2,1,0:T(8,128)} %bitcast.35, s32[1,1024]{1,0:T(1,128)} %bitcast.50, s32[1,1024]{1,0:T(1,128)} %bitcast.49), custom_call_target="tpu_custom_call" | custom-call | flops 134742016 | bytes 1142784 | tf_op jit(solution)/shard_map/proj_pack/pallas_call | solution.py:251
  3.8 12.1 %all-to-all-start = ((f32[64,1,2176]{2,1,0:T(1,128)}), f32[64,1,2176]{2,1,0:T(1,128)S(1)}, u32[]{:S(2)}, u32[]{:S(2)}) async-start(f32[64,1,2176]{2,1,0:T(1,128)} %bitcast.39), calls=%async_computation | async-start | bytes 1114112 | tf_op jit(solution)/shard_map/all_to_all | solution.py:269
  15.9 0.7 subtract_bitcast_fusion
  16.6 0.1 broadcast_in_dim.10
  16.7 0.7 reshape.71.nlc_ref
  17.4 0.0 copy-start.1
  17.4 0.0 copy-start
  17.4 8.7 %near.2.part_ref = f32[2,4096]{1,0:T(2,128)} custom-call(f32[2,4096]{1,0:T(2,128)} %bitcast.41, f32[1,4096]{1,0:T(1,128)} %c_ref.7, f32[2,192,4096]{2,1,0:T(8,128)} %bitcast.29, s32[3,4096]{1,0:T(4,128)} %reshape.71.nlc_ref, f32[2,4096]{1,0:T(2,128)} %bitcast.42), custom_call_target="tpu_custom_call" | custom-call | flops 6291456 | bytes 6455296 | tf_op jit(solution)/shard_map/near/pallas_call | solution.py:251
  26.1 0.0 copy-done.1
  26.1 0.0 copy-done
  26.2 7.0 %all-to-all-done = f32[64,1,2176]{2,1,0:T(1,128)S(1)} async-done(((f32[64,1,2176]{2,1,0:T(1,128)}), f32[64,1,2176]{2,1,0:T(1,128)S(1)}, u32[]{:S(2)}, u32[]{:S(2)}) %all-to-all-start) | async-done | bytes 557088 | tf_op jit(solution)/shard_map/all_to_all | solution.py:269
  33.2 1.3 %reduce = f32[64,2176]{1,0:T(8,128)S(1)} reduce(f32[64,1,2176]{2,1,0:T(1,128)S(1)} %all-to-all-done, f32[]{:T(128)} %constant.59), dimensions={1}, to_apply=%all_to_all.13.reduce_sub_computation | reduce | bytes 1114116 | tf_op jit(solution)/shard_map/all_to_all | solution.py:269
  34.5 0.1 reshape.74
  34.6 0.6 slice.13
  35.3 0.2 reshape.75
  35.5 0.6 copy.19
  36.1 2.8 %gather_fusion = f32[1024,32]{1,0:T(8,128)S(1)} fusion(f32[32,4096]{0,1:T(8,128)S(1)} %bitcast.33, s32[1024]{0:T(1024)S(1)} %fusion), kind=kCustom, calls=%fused_computation | custom fusion | bytes 266240 | tf_op jit(solution)/shard_map/gather | solution.py:274
  38.9 0.8 %copy.20 = f32[1024,32]{0,1:T(8,128)} copy(f32[1024,32]{1,0:T(8,128)S(1)} %gather_fusion) | data formatting | bytes 262144 | tf_op jit(solution)/shard_map/gather | solution.py:274
  39.8 0.0 copy-start.2
  39.8 5.4 %far_proj.1 = (f32[2,4096]{1,0:T(2,128)}, f32[512,128]{1,0:T(8,128)}) custom-call(f32[2,4096]{1,0:T(2,128)} %near.2.part_ref, f32[32,1024]{1,0:T(8,128)} %bitcast.44, f32[2,16,16,1024]{3,2,1,0:T(8,128)} %bitcast.31, f32[2,16,4096]{2,1,0:T(8,128)} %bitcast.37, f32[1,4096]{1,0:T(1,128)} %c_ref.7, f32[2,16,4096]{2,1,0:T(8,128)} %bitcast.36, f32[64,32]{1,0:T(8,128)} %bitcast.47), custom_call_target="tpu_custom_call" | custom-call | flops 4194304 | bytes 3629056 | tf_op jit(solution)/shard_map/far_proj/pallas_call | solution.py:251
  45.1 7.0 %all-to-all-start.1 = ((f32[64,1,1024]{2,1,0:T(1,128)}), f32[64,1,1024]{2,1,0:T(1,128)S(1)}, u32[]{:S(2)}, u32[]{:S(2)}) async-start(f32[64,1,1024]{2,1,0:T(1,128)} %bitcast.46), calls=%async_computation.1 | async-start | bytes 524288 | tf_op jit(solution)/shard_map/all_to_all | solution.py:262
  52.1 0.0 copy-done.2
  52.1 8.7 %near.3.part_ref = f32[2,4096]{1,0:T(2,128)} custom-call(f32[2,4096]{1,0:T(2,128)} %get-tuple-element.9.u_ref, f32[1,4096]{1,0:T(1,128)} %c_ref.7, f32[2,192,4096]{2,1,0:T(8,128)} %bitcast.30, s32[3,4096]{1,0:T(4,128)} %reshape.71.nlc_ref, f32[2,4096]{1,0:T(2,128)} %bitcast.43), custom_call_target="tpu_custom_call" | custom-call | flops 6291456 | bytes 6455296 | tf_op jit(solution)/shard_map/near/pallas_call | solution.py:251
  60.8 2.8 %all-to-all-done.1 = f32[64,1,1024]{2,1,0:T(1,128)S(1)} async-done(((f32[64,1,1024]{2,1,0:T(1,128)}), f32[64,1,1024]{2,1,0:T(1,128)S(1)}, u32[]{:S(2)}, u32[]{:S(2)}) %all-to-all-start.1) | async-done | bytes 262176 | tf_op jit(solution)/shard_map/all_to_all | solution.py:262
  63.6 0.6 reduce.1
  64.2 0.3 reshape.77
  64.6 2.8 %gather_fusion.1 = f32[1024,32]{1,0:T(8,128)S(1)} fusion(f32[2048,32]{1,0:T(8,128)S(1)} %reshape.77, s32[1024]{0:T(1024)S(1)} %broadcast_clamp_fusion), kind=kCustom, calls=%fused_computation.1 | custom fusion | bytes 266240 | tf_op jit(solution)/shard_map/gather | solution.py:264
  67.4 0.8 %copy.23 = f32[1024,32]{0,1:T(8,128)} copy(f32[1024,32]{1,0:T(8,128)S(1)} %gather_fusion.1) | data formatting | bytes 262144 | tf_op jit(solution)/shard_map/gather | solution.py:264
  68.2 3.8 %far_grad.1 = (f32[2,4096]{1,0:T(2,128)}, f32[1,4096]{1,0:T(1,128)}) custom-call(f32[2,4096]{1,0:T(2,128)} %near.3.part_ref, f32[32,1024]{1,0:T(8,128)} %bitcast.45, f32[2,16,16,1024]{3,2,1,0:T(8,128)} %bitcast.32, f32[2,16,4096]{2,1,0:T(8,128)} %bitcast.38, f32[2,4096]{1,0:T(2,128)} %bitcast.48), custom_call_target="tpu_custom_call" | custom-call | flops 4194304 | bytes 2867200 | tf_op jit(solution)/shard_map/far_grad/pallas_call | solution.py:251
  72.0 2.8 %collective-permute-start.2 = (f32[4096]{0:T(1024)}, f32[4096]{0:T(1024)S(1)}, u32[]{:S(2)}, u32[]{:S(2)}) collective-permute-start(f32[4096]{0:T(1024)} %bitcast.54), channel_id=1, source_target_pairs={{0,3},{1,0},{2,1},{3,2},{4,7},{5,4},{6,5},{7,6},{8,11},{9,8},{10,9... | collective-permute-start | bytes 49160 | tf_op jit(solution)/shard_map/ppermute | solution.py:354
  74.8 0.8 collective-permute-start.1
  75.6 0.9 %collective-permute-start = (f32[4096]{0:T(1024)}, f32[4096]{0:T(1024)S(1)}, u32[]{:S(2)}, u32[]{:S(2)}) collective-permute-start(f32[4096]{0:T(1024)} %bitcast.56), channel_id=1, source_target_pairs={{0,1},{1,2},{2,3},{3,0},{4,5},{5,6},{6,7},{7,4},{8,9},{9,10},{10,1... | collective-permute-start | bytes 49160 | tf_op jit(solution)/shard_map/ppermute | solution.py:354
  76.4 0.0 collective-permute-done.2
  76.4 3.8 %collective-permute-done.1 = f32[4096]{0:T(1024)S(1)} collective-permute-done((f32[4096]{0:T(1024)}, f32[4096]{0:T(1024)S(1)}, u32[]{:S(2)}, u32[]{:S(2)}) %collective-permute-start.1) | collective-permute-done | bytes 16416 | tf_op jit(solution)/shard_map/ppermute | solution.py:354
  80.2 0.5 collective-permute-done
  80.7 0.8 pad_maximum_fusion
  81.5 0.7 dynamic-slice_add_fusion
  (5 shorter events, 0.1 us)
Async XLA Ops:
  3.8 29.4 %all-to-all-start = ((f32[64,1,2176]{2,1,0:T(1,128)}), f32[64,1,2176]{2,1,0:T(1,128)S(1)}, u32[]{:S(2)}, u32[]{:S(2)}) async-start(f32[64,1,2176]{2,1,0:T(1,128)} %bitcast.39), calls=%async_computation | async-start | bytes 1114112 | tf_op jit(solution)/shard_map/all_to_all | solution.py:269
  17.4 8.7 %copy-start.1 = (s32[1024,1]{0,1:T(1,128)S(1)}, s32[1024,1]{0,1:T(1,128)}, u32[]{:S(2)}) copy-start(s32[1024,1]{0,1:T(1,128)} %param.18) | copy-start | bytes 12292
  17.4 8.7 %copy-start = (s32[1024]{0:T(1024)S(1)}, s32[1024]{0:T(1024)}, u32[]{:S(2)}) copy-start(s32[1024]{0:T(1024)} %param.19) | copy-start | bytes 12292
  39.8 12.3 %copy-start.2 = (s32[1,1024]{1,0:T(1,128)S(1)}, s32[1,1024]{1,0:T(1,128)}, u32[]{:S(2)}) copy-start(s32[1,1024]{1,0:T(1,128)} %get-tuple-element.11) | copy-start | bytes 12292
  45.1 18.5 %all-to-all-start.1 = ((f32[64,1,1024]{2,1,0:T(1,128)}), f32[64,1,1024]{2,1,0:T(1,128)S(1)}, u32[]{:S(2)}, u32[]{:S(2)}) async-start(f32[64,1,1024]{2,1,0:T(1,128)} %bitcast.46), calls=%async_computation.1 | async-start | bytes 524288 | tf_op jit(solution)/shard_map/all_to_all | solution.py:262
  72.0 4.4 %collective-permute-start.2 = (f32[4096]{0:T(1024)}, f32[4096]{0:T(1024)S(1)}, u32[]{:S(2)}, u32[]{:S(2)}) collective-permute-start(f32[4096]{0:T(1024)} %bitcast.54), channel_id=1, source_target_pairs={{0,3},{1,0},{2,1},{3,2},{4,7},{5,4},{6,5},{7,6},{8,11},{9,8},{10,9... | collective-permute-start | bytes 49160 | tf_op jit(solution)/shard_map/ppermute | solution.py:354
  74.8 5.5 %collective-permute-start.1 = (f32[4096]{0:T(1024)}, f32[4096]{0:T(1024)S(1)}, u32[]{:S(2)}, u32[]{:S(2)}) collective-permute-start(f32[4096]{0:T(1024)} %bitcast.55), channel_id=1, source_target_pairs={{0,2},{1,3},{2,0},{3,1},{4,6},{5,7},{6,4},{7,5},{8,10},{9,11},{10,... | collective-permute-start | bytes 49160 | tf_op jit(solution)/shard_map/ppermute | solution.py:354
  75.6 5.2 %collective-permute-start = (f32[4096]{0:T(1024)}, f32[4096]{0:T(1024)S(1)}, u32[]{:S(2)}, u32[]{:S(2)}) collective-permute-start(f32[4096]{0:T(1024)} %bitcast.56), channel_id=1, source_target_pairs={{0,1},{1,2},{2,3},{3,0},{4,5},{5,6},{6,7},{7,4},{8,9},{9,10},{10,1... | collective-permute-start | bytes 49160 | tf_op jit(solution)/shard_map/ppermute | solution.py:354

commit v13 on v12

--- a/solution.py
+++ b/solution.py
@@ -180,13 +180,13 @@
     width = 64
     clusters = cells // width
     rank = cpl_ref.shape[1]
-    npairs = qs_ref.shape[1]
+    npairs = qs_ref.shape[0]
     far = npairs // clusters
 
     def pair_body(pj, z):
         off = pl.multiple_of(pj * PAIR_CHUNK, PAIR_CHUNK)
         sl = pl.ds(off, PAIR_CHUNK)
-        qs = qs_ref[:, sl]
+        qs = qs_ref[sl, :].T
         qre = qs[:rank][None]
         qim = qs[rank:][None]
         cre = cpl_ref[0, :, :, sl]
@@ -261,7 +261,7 @@
     total = send.size
     got = lax.all_to_all(send.reshape(devices, total // devices), "cells", 0, 0)
     got = got.reshape(devices * cap, total // (devices * cap))
-    return got[idx].T
+    return got[idx]
 
 
 def _exchange_all(send, devices, clusters, rank2, cap, groups, src_index):
@@ -271,7 +271,7 @@
     got = got.reshape(devices, total // (devices * lanes), lanes)
     rr = got[:, -1, :cap]
     table = got[:, :-1, :].reshape(devices, rank2, clusters).transpose(1, 0, 2)
-    return table.reshape(rank2, devices * clusters)[:, src_index], rr
+    return table.reshape(rank2, devices * clusters)[:, src_index].T, rr
 
 
 def per_device(

time: 82.6 us -> 83.5 us (1.011)
    gather x4 -> x2, local copies, waits for them, and re-layouts: 7.28 us -> 8 us  [the longest x1 4 us: _exchange_all(): return (table.reshape(rank2, devices * clusters)[:, src_index].T, rr)]
where the time goes in v13:
time: 83.5 us; the launch traced here: 83.1 us
  Pallas kernels  29.9 us (36%)
  starting transfers between devices  23.5 us (28%)
  waiting for transfers between devices  14.1 us (17%)
  local copies, waits for them, and re-layouts  10.7 us (13%)
  other arithmetic  4.09 us (5%)
    pallas_call x5, Pallas kernels, _call(): pl.pallas_call(kernel, out_shape=outs, compiler_params=pltpu.CompilerPara...  29.9 us
    all_to_all x1, starting transfers between devices, _exchange_all(): got = lax.all_to_all(send.reshape(devices, total // devices), 'cells', 0, 0)  12.1 us
    all_to_all x1, waiting for transfers between devices, _exchange_all(): got = lax.all_to_all(send.reshape(devices, total // devices), 'cells', 0, 0)  7.04 us
    all_to_all x1, starting transfers between devices, _exchange(): got = lax.all_to_all(send.reshape(devices, total // devices), 'cells', 0, 0)  6.95 us
    ppermute x3, starting transfers between devices, per_device(): lax.ppermute(mine, 'freq', [(i, (i + k) % freqs) for i in range(freqs)])  4.44 us
    ppermute x3, waiting for transfers between devices, per_device(): lax.ppermute(mine, 'freq', [(i, (i + k) % freqs) for i in range(freqs)])  4.27 us
    gather x1, local copies, waits for them, and re-layouts, _exchange_all(): return (table.reshape(rank2, devices * clusters)[:, src_index].T, rr)  4 us
    gather x1, local copies, waits for them, and re-layouts, _exchange(): return got[idx]  4 us
  transfers between devices with their start and end apart: 5, of which 4 were waited for; matrix products, arithmetic and copies ran while one was open for 2% of the time, Pallas kernels for 21%

profile of v13, /device:TPU:8, one launch (start us, length us, event | category | flops | bytes accessed | tf_op | source)
XLA Modules:
  0.0 83.1 jit_solution(7894378982863523056)
XLA Ops:
  0.6 3.1 %proj_pack.1 = (s32[1,1024]{1,0:T(1,128)}, f32[1088,128]{1,0:T(8,128)}) custom-call(f32[2,4096]{1,0:T(2,128)} %bitcast.38, f32[1,4096]{1,0:T(1,128)} %c_ref.7, f32[2,16,4096]{2,1,0:T(8,128)} %bitcast.35, s32[1,1024]{1,0:T(1,128)} %bitcast.46, s32[1,1024]{1,0:T(1,128)} %bitcast.45), custom_call_target="tpu_custom_call" | custom-call | flops 134742016 | bytes 1142784 | tf_op jit(solution)/shard_map/proj_pack/pallas_call | solution.py:251
  3.8 12.1 %all-to-all-start = ((f32[64,1,2176]{2,1,0:T(1,128)}), f32[64,1,2176]{2,1,0:T(1,128)S(1)}, u32[]{:S(2)}, u32[]{:S(2)}) async-start(f32[64,1,2176]{2,1,0:T(1,128)} %bitcast.37), calls=%async_computation | async-start | bytes 1114112 | tf_op jit(solution)/shard_map/all_to_all | solution.py:269
  15.9 0.7 subtract_bitcast_fusion
  16.6 0.1 broadcast_in_dim.10
  16.7 0.7 reshape.71.nlc_ref
  17.4 0.0 copy-start.1
  17.4 0.0 copy-start
  17.4 8.7 %near.2.part_ref = f32[2,4096]{1,0:T(2,128)} custom-call(f32[2,4096]{1,0:T(2,128)} %bitcast.39, f32[1,4096]{1,0:T(1,128)} %c_ref.7, f32[2,192,4096]{2,1,0:T(8,128)} %bitcast.27, s32[3,4096]{1,0:T(4,128)} %reshape.71.nlc_ref, f32[2,4096]{1,0:T(2,128)} %bitcast.40), custom_call_target="tpu_custom_call" | custom-call | flops 6291456 | bytes 6455296 | tf_op jit(solution)/shard_map/near/pallas_call | solution.py:251
  26.1 0.0 copy-done.1
  26.1 0.0 copy-done
  26.2 7.0 %all-to-all-done = f32[64,1,2176]{2,1,0:T(1,128)S(1)} async-done(((f32[64,1,2176]{2,1,0:T(1,128)}), f32[64,1,2176]{2,1,0:T(1,128)S(1)}, u32[]{:S(2)}, u32[]{:S(2)}) %all-to-all-start) | async-done | bytes 557088 | tf_op jit(solution)/shard_map/all_to_all | solution.py:269
  33.2 1.3 %reduce = f32[64,2176]{1,0:T(8,128)S(1)} reduce(f32[64,1,2176]{2,1,0:T(1,128)S(1)} %all-to-all-done, f32[]{:T(128)} %constant.59), dimensions={1}, to_apply=%all_to_all.13.reduce_sub_computation | reduce | bytes 1114116 | tf_op jit(solution)/shard_map/all_to_all | solution.py:269
  34.5 0.1 reshape.74
  34.6 0.6 slice.13
  35.3 0.2 reshape.75
  35.5 0.6 copy.15
  36.1 4.0 %gather_fusion = f32[1024,32]{1,0:T(8,128)} fusion(f32[32,4096]{0,1:T(8,128)S(1)} %bitcast.31, s32[1024]{0:T(1024)S(1)} %fusion), kind=kCustom, calls=%fused_computation | custom fusion | bytes 266240 | tf_op jit(solution)/shard_map/gather | solution.py:274
  40.1 0.0 copy-start.2
  40.1 5.5 %far_proj.1 = (f32[2,4096]{1,0:T(2,128)}, f32[512,128]{1,0:T(8,128)}) custom-call(f32[2,4096]{1,0:T(2,128)} %near.2.part_ref, f32[1024,32]{1,0:T(8,128)} %gather_fusion, f32[2,16,16,1024]{3,2,1,0:T(8,128)} %bitcast.29, f32[2,16,4096]{2,1,0:T(8,128)} %bitcast.33, f32[1,4096]{1,0:T(1,128)} %c_ref.7, f32[2,16,4096]{2,1,0:T(8,128)} %bitcast.36, f32[64,32]{1,0:T(8,128)} %bitcast.43), custom_call_target="tpu_custom_call" | custom-call | flops 4194304 | bytes 3629056 | tf_op jit(solution)/shard_map/far_proj/pallas_call | solution.py:251
  45.6 7.0 %all-to-all-start.1 = ((f32[64,1,1024]{2,1,0:T(1,128)}), f32[64,1,1024]{2,1,0:T(1,128)S(1)}, u32[]{:S(2)}, u32[]{:S(2)}) async-start(f32[64,1,1024]{2,1,0:T(1,128)} %bitcast.42), calls=%async_computation.1 | async-start | bytes 524288 | tf_op jit(solution)/shard_map/all_to_all | solution.py:262
  52.6 0.0 copy-done.2
  52.6 8.7 %near.3.part_ref = f32[2,4096]{1,0:T(2,128)} custom-call(f32[2,4096]{1,0:T(2,128)} %get-tuple-element.9.u_ref, f32[1,4096]{1,0:T(1,128)} %c_ref.7, f32[2,192,4096]{2,1,0:T(8,128)} %bitcast.28, s32[3,4096]{1,0:T(4,128)} %reshape.71.nlc_ref, f32[2,4096]{1,0:T(2,128)} %bitcast.41), custom_call_target="tpu_custom_call" | custom-call | flops 6291456 | bytes 6455296 | tf_op jit(solution)/shard_map/near/pallas_call | solution.py:251
  61.3 2.8 %all-to-all-done.1 = f32[64,1,1024]{2,1,0:T(1,128)S(1)} async-done(((f32[64,1,1024]{2,1,0:T(1,128)}), f32[64,1,1024]{2,1,0:T(1,128)S(1)}, u32[]{:S(2)}, u32[]{:S(2)}) %all-to-all-start.1) | async-done | bytes 262176 | tf_op jit(solution)/shard_map/all_to_all | solution.py:262
  64.1 0.6 reduce.1
  64.7 0.3 reshape.77
  65.1 4.0 %gather_fusion.1 = f32[1024,32]{1,0:T(8,128)} fusion(f32[2048,32]{1,0:T(8,128)S(1)} %reshape.77, s32[1024]{0:T(1024)S(1)} %broadcast_clamp_fusion), kind=kCustom, calls=%fused_computation.1 | custom fusion | bytes 266240 | tf_op jit(solution)/shard_map/gather | solution.py:264
  69.1 3.9 %far_grad.1 = (f32[2,4096]{1,0:T(2,128)}, f32[1,4096]{1,0:T(1,128)}) custom-call(f32[2,4096]{1,0:T(2,128)} %near.3.part_ref, f32[1024,32]{1,0:T(8,128)} %gather_fusion.1, f32[2,16,16,1024]{3,2,1,0:T(8,128)} %bitcast.30, f32[2,16,4096]{2,1,0:T(8,128)} %bitcast.34, f32[2,4096]{1,0:T(2,128)} %bitcast.44), custom_call_target="tpu_custom_call" | custom-call | flops 4194304 | bytes 2867200 | tf_op jit(solution)/shard_map/far_grad/pallas_call | solution.py:251
  72.9 2.8 %collective-permute-start.2 = (f32[4096]{0:T(1024)}, f32[4096]{0:T(1024)S(1)}, u32[]{:S(2)}, u32[]{:S(2)}) collective-permute-start(f32[4096]{0:T(1024)} %bitcast.50), channel_id=1, source_target_pairs={{0,3},{1,0},{2,1},{3,2},{4,7},{5,4},{6,5},{7,6},{8,11},{9,8},{10,9... | collective-permute-start | bytes 49160 | tf_op jit(solution)/shard_map/ppermute | solution.py:354
  75.7 0.8 collective-permute-start.1
  76.5 0.9 %collective-permute-start = (f32[4096]{0:T(1024)}, f32[4096]{0:T(1024)S(1)}, u32[]{:S(2)}, u32[]{:S(2)}) collective-permute-start(f32[4096]{0:T(1024)} %bitcast.52), channel_id=1, source_target_pairs={{0,1},{1,2},{2,3},{3,0},{4,5},{5,6},{6,7},{7,4},{8,9},{9,10},{10,1... | collective-permute-start | bytes 49160 | tf_op jit(solution)/shard_map/ppermute | solution.py:354
  77.4 0.0 collective-permute-done.2
  77.4 3.8 %collective-permute-done.1 = f32[4096]{0:T(1024)S(1)} collective-permute-done((f32[4096]{0:T(1024)}, f32[4096]{0:T(1024)S(1)}, u32[]{:S(2)}, u32[]{:S(2)}) %collective-permute-start.1) | collective-permute-done | bytes 16416 | tf_op jit(solution)/shard_map/ppermute | solution.py:354
  81.2 0.5 collective-permute-done
  81.7 0.8 pad_maximum_fusion
  82.4 0.7 dynamic-slice_add_fusion
  (5 shorter events, 0.1 us)
Async XLA Ops:
  3.8 29.4 %all-to-all-start = ((f32[64,1,2176]{2,1,0:T(1,128)}), f32[64,1,2176]{2,1,0:T(1,128)S(1)}, u32[]{:S(2)}, u32[]{:S(2)}) async-start(f32[64,1,2176]{2,1,0:T(1,128)} %bitcast.37), calls=%async_computation | async-start | bytes 1114112 | tf_op jit(solution)/shard_map/all_to_all | solution.py:269
  17.4 8.7 %copy-start.1 = (s32[1024,1]{0,1:T(1,128)S(1)}, s32[1024,1]{0,1:T(1,128)}, u32[]{:S(2)}) copy-start(s32[1024,1]{0,1:T(1,128)} %param.18) | copy-start | bytes 12292
  17.4 8.7 %copy-start = (s32[1024]{0:T(1024)S(1)}, s32[1024]{0:T(1024)}, u32[]{:S(2)}) copy-start(s32[1024]{0:T(1024)} %param.19) | copy-start | bytes 12292
  40.1 12.5 %copy-start.2 = (s32[1,1024]{1,0:T(1,128)S(1)}, s32[1,1024]{1,0:T(1,128)}, u32[]{:S(2)}) copy-start(s32[1,1024]{1,0:T(1,128)} %get-tuple-element.11) | copy-start | bytes 12292
  45.6 18.5 %all-to-all-start.1 = ((f32[64,1,1024]{2,1,0:T(1,128)}), f32[64,1,1024]{2,1,0:T(1,128)S(1)}, u32[]{:S(2)}, u32[]{:S(2)}) async-start(f32[64,1,1024]{2,1,0:T(1,128)} %bitcast.42), calls=%async_computation.1 | async-start | bytes 524288 | tf_op jit(solution)/shard_map/all_to_all | solution.py:262
  72.9 4.4 %collective-permute-start.2 = (f32[4096]{0:T(1024)}, f32[4096]{0:T(1024)S(1)}, u32[]{:S(2)}, u32[]{:S(2)}) collective-permute-start(f32[4096]{0:T(1024)} %bitcast.50), channel_id=1, source_target_pairs={{0,3},{1,0},{2,1},{3,2},{4,7},{5,4},{6,5},{7,6},{8,11},{9,8},{10,9... | collective-permute-start | bytes 49160 | tf_op jit(solution)/shard_map/ppermute | solution.py:354
  75.7 5.5 %collective-permute-start.1 = (f32[4096]{0:T(1024)}, f32[4096]{0:T(1024)S(1)}, u32[]{:S(2)}, u32[]{:S(2)}) collective-permute-start(f32[4096]{0:T(1024)} %bitcast.51), channel_id=1, source_target_pairs={{0,2},{1,3},{2,0},{3,1},{4,6},{5,7},{6,4},{7,5},{8,10},{9,11},{10,... | collective-permute-start | bytes 49160 | tf_op jit(solution)/shard_map/ppermute | solution.py:354
  76.5 5.2 %collective-permute-start = (f32[4096]{0:T(1024)}, f32[4096]{0:T(1024)S(1)}, u32[]{:S(2)}, u32[]{:S(2)}) collective-permute-start(f32[4096]{0:T(1024)} %bitcast.52), channel_id=1, source_target_pairs={{0,1},{1,2},{2,3},{3,0},{4,5},{5,6},{6,7},{7,4},{8,9},{9,10},{10,1... | collective-permute-start | bytes 49160 | tf_op jit(solution)/shard_map/ppermute | solution.py:354

commit v14 on v12

--- a/solution.py
+++ b/solution.py
@@ -187,12 +187,15 @@
         off = pl.multiple_of(pj * PAIR_CHUNK, PAIR_CHUNK)
         sl = pl.ds(off, PAIR_CHUNK)
         qs = qs_ref[:, sl]
-        qre = qs[:rank][None]
-        qim = qs[rank:][None]
-        cre = cpl_ref[0, :, :, sl]
-        cim = cpl_ref[1, :, :, sl]
-        zre = jnp.sum(cre * qre - cim * qim, axis=1)
-        zim = jnp.sum(cre * qim + cim * qre, axis=1)
+        zre = jnp.zeros((rank, PAIR_CHUNK), F32)
+        zim = jnp.zeros((rank, PAIR_CHUNK), F32)
+        for i in range(rank):
+            cre = cpl_ref[0, i, :, sl]
+            cim = cpl_ref[1, i, :, sl]
+            qre = qs[i : i + 1]
+            qim = qs[rank + i : rank + i + 1]
+            zre = zre + (cre * qre - cim * qim)
+            zim = zim + (cre * qim + cim * qre)
         seg = _div(_iota((PAIR_CHUNK, clusters), 0) + off, far) == _iota((PAIR_CHUNK, clusters), 1)
         return z + _xdot(jnp.concatenate([zre, zim], axis=0), seg.astype(BF16))
 
@@ -298,7 +301,7 @@
     nb = near_blocks[0]
     pb = proj_basis[0]
     eb = expand_basis[0]
-    cp = coupling[0]
+    cp = jnp.transpose(coupling[0], (0, 2, 1, 3))
     bg = background[0]
 
     me = lax.axis_index("cells")

time: 82.6 us -> 82.6 us (level)
  local copies, waits for them, and re-layouts: 10 us -> 14.2 us
  waiting for transfers between devices: 14.1 us -> 9.95 us
    unnamed x6 -> x7, local copies, waits for them, and re-layouts: 0.01 us -> 4.17 us
    all_to_all x1, waiting for transfers between devices: 7.03 us -> 2.88 us  [_exchange_all(): got = lax.all_to_all(send.reshape(devices, total // devices), 'cells', 0, 0)]
  transfers between devices with their start and end apart: 5 -> 5, of which waited for: 4 -> 4; matrix products, arithmetic and copies ran while one was open for 2% -> 7% of each run, Pallas kernels for 21% -> 21%
where the time goes in v14:
time: 82.6 us; the launch traced here: 82.2 us
  Pallas kernels  29.2 us (35%)
  starting transfers between devices  24 us (29%)
  local copies, waits for them, and re-layouts  14.2 us (17%)
  waiting for transfers between devices  9.95 us (12%)
  other arithmetic  4.09 us (5%)
    pallas_call x5, Pallas kernels, _call(): pl.pallas_call(kernel, out_shape=outs, compiler_params=pltpu.CompilerPara...  29.2 us
    all_to_all x1, starting transfers between devices, _exchange_all(): got = lax.all_to_all(send.reshape(devices, total // devices), 'cells', 0, 0)  12.1 us
    all_to_all x1, starting transfers between devices, _exchange(): got = lax.all_to_all(send.reshape(devices, total // devices), 'cells', 0, 0)  7.46 us
    ppermute x3, starting transfers between devices, per_device(): lax.ppermute(mine, 'freq', [(i, (i + k) % freqs) for i in range(freqs)])  4.44 us
    ppermute x3, waiting for transfers between devices, per_device(): lax.ppermute(mine, 'freq', [(i, (i + k) % freqs) for i in range(freqs)])  4.27 us
    unnamed x7, local copies, waits for them, and re-layouts  4.17 us
    gather x2, local copies, waits for them, and re-layouts, _exchange_all(): return (table.reshape(rank2, devices * clusters)[:, src_index], rr)  3.64 us
    gather x2, local copies, waits for them, and re-layouts, _exchange(): return got[idx].T  3.63 us
  transfers between devices with their start and end apart: 5, of which 4 were waited for; matrix products, arithmetic and copies ran while one was open for 7% of the time, Pallas kernels for 21%

profile of v14, /device:TPU:8, one launch (start us, length us, event | category | flops | bytes accessed | tf_op | source)
XLA Modules:
  0.0 82.2 jit_solution(6043177664862425600)
XLA Ops:
  0.6 3.1 %proj_pack.1 = (s32[1,1024]{1,0:T(1,128)}, f32[1088,128]{1,0:T(8,128)}) custom-call(f32[2,4096]{1,0:T(2,128)} %bitcast.44, f32[1,4096]{1,0:T(1,128)} %c_ref.7, f32[2,16,4096]{2,1,0:T(8,128)} %bitcast.39, s32[1,1024]{1,0:T(1,128)} %bitcast.54, s32[1,1024]{1,0:T(1,128)} %bitcast.53), custom_call_target="tpu_custom_call" | custom-call | flops 134742016 | bytes 1142784 | tf_op jit(solution)/shard_map/proj_pack/pallas_call | solution.py:254
  3.8 12.1 %all-to-all-start = ((f32[64,1,2176]{2,1,0:T(1,128)}), f32[64,1,2176]{2,1,0:T(1,128)S(1)}, u32[]{:S(2)}, u32[]{:S(2)}) async-start(f32[64,1,2176]{2,1,0:T(1,128)} %bitcast.43), calls=%async_computation | async-start | bytes 1114112 | tf_op jit(solution)/shard_map/all_to_all | solution.py:272
  15.9 0.7 subtract_bitcast_fusion
  16.6 0.1 broadcast_in_dim.10
  16.7 0.7 reshape.71.nlc_ref
  17.4 4.2 %copy.29 = f32[1,2,16,16,1024]{4,2,3,1,0:T(8,128)} copy(f32[1,2,16,16,1024]{4,3,2,1,0:T(8,128)} %param.17) | data formatting | bytes 4194304 | tf_op args[7]
  21.6 0.0 copy-start.1
  21.6 0.0 copy-start
  21.6 8.7 %near.2.part_ref = f32[2,4096]{1,0:T(2,128)} custom-call(f32[2,4096]{1,0:T(2,128)} %bitcast.45, f32[1,4096]{1,0:T(1,128)} %c_ref.7, f32[2,192,4096]{2,1,0:T(8,128)} %bitcast.33, s32[3,4096]{1,0:T(4,128)} %reshape.71.nlc_ref, f32[2,4096]{1,0:T(2,128)} %bitcast.46), custom_call_target="tpu_custom_call" | custom-call | flops 6291456 | bytes 6455296 | tf_op jit(solution)/shard_map/near/pallas_call | solution.py:254
  30.3 0.0 copy-done.1
  30.3 0.0 copy-done
  30.3 2.9 %all-to-all-done = f32[64,1,2176]{2,1,0:T(1,128)S(1)} async-done(((f32[64,1,2176]{2,1,0:T(1,128)}), f32[64,1,2176]{2,1,0:T(1,128)S(1)}, u32[]{:S(2)}, u32[]{:S(2)}) %all-to-all-start) | async-done | bytes 557088 | tf_op jit(solution)/shard_map/all_to_all | solution.py:272
  33.2 1.3 %reduce = f32[64,2176]{1,0:T(8,128)S(1)} reduce(f32[64,1,2176]{2,1,0:T(1,128)S(1)} %all-to-all-done, f32[]{:T(128)} %constant.59), dimensions={1}, to_apply=%all_to_all.13.reduce_sub_computation | reduce | bytes 1114116 | tf_op jit(solution)/shard_map/all_to_all | solution.py:272
  34.5 0.1 reshape.74
  34.6 0.6 slice.13
  35.3 0.2 reshape.75
  35.5 0.6 copy.21
  36.1 2.8 %gather_fusion = f32[1024,32]{1,0:T(8,128)S(1)} fusion(f32[32,4096]{0,1:T(8,128)S(1)} %bitcast.37, s32[1024]{0:T(1024)S(1)} %fusion), kind=kCustom, calls=%fused_computation | custom fusion | bytes 266240 | tf_op jit(solution)/shard_map/gather | solution.py:277
  38.9 0.8 %copy.22 = f32[1024,32]{0,1:T(8,128)} copy(f32[1024,32]{1,0:T(8,128)S(1)} %gather_fusion) | data formatting | bytes 262144 | tf_op jit(solution)/shard_map/gather | solution.py:277
  39.8 0.0 copy-start.2
  39.8 5.1 %far_proj.1 = (f32[2,4096]{1,0:T(2,128)}, f32[512,128]{1,0:T(8,128)}) custom-call(f32[2,4096]{1,0:T(2,128)} %near.2.part_ref, f32[32,1024]{1,0:T(8,128)} %bitcast.48, f32[2,16,16,1024]{3,2,1,0:T(8,128)} %bitcast.35, f32[2,16,4096]{2,1,0:T(8,128)} %bitcast.41, f32[1,4096]{1,0:T(1,128)} %c_ref.7, f32[2,16,4096]{2,1,0:T(8,128)} %bitcast.40, f32[64,32]{1,0:T(8,128)} %bitcast.51), custom_call_target="tpu_custom_call" | custom-call | flops 4194304 | bytes 3629056 | tf_op jit(solution)/shard_map/far_proj/pallas_call | solution.py:254
  44.9 7.5 %all-to-all-start.1 = ((f32[64,1,1024]{2,1,0:T(1,128)}), f32[64,1,1024]{2,1,0:T(1,128)S(1)}, u32[]{:S(2)}, u32[]{:S(2)}) async-start(f32[64,1,1024]{2,1,0:T(1,128)} %bitcast.50), calls=%async_computation.1 | async-start | bytes 524288 | tf_op jit(solution)/shard_map/all_to_all | solution.py:265
  52.3 0.0 copy-done.2
  52.4 8.7 %near.3.part_ref = f32[2,4096]{1,0:T(2,128)} custom-call(f32[2,4096]{1,0:T(2,128)} %get-tuple-element.9.u_ref, f32[1,4096]{1,0:T(1,128)} %c_ref.7, f32[2,192,4096]{2,1,0:T(8,128)} %bitcast.34, s32[3,4096]{1,0:T(4,128)} %reshape.71.nlc_ref, f32[2,4096]{1,0:T(2,128)} %bitcast.47), custom_call_target="tpu_custom_call" | custom-call | flops 6291456 | bytes 6455296 | tf_op jit(solution)/shard_map/near/pallas_call | solution.py:254
  61.1 2.8 %all-to-all-done.1 = f32[64,1,1024]{2,1,0:T(1,128)S(1)} async-done(((f32[64,1,1024]{2,1,0:T(1,128)}), f32[64,1,1024]{2,1,0:T(1,128)S(1)}, u32[]{:S(2)}, u32[]{:S(2)}) %all-to-all-start.1) | async-done | bytes 262176 | tf_op jit(solution)/shard_map/all_to_all | solution.py:265
  63.8 0.6 reduce.1
  64.5 0.3 reshape.77
  64.8 2.8 %gather_fusion.1 = f32[1024,32]{1,0:T(8,128)S(1)} fusion(f32[2048,32]{1,0:T(8,128)S(1)} %reshape.77, s32[1024]{0:T(1024)S(1)} %broadcast_clamp_fusion), kind=kCustom, calls=%fused_computation.1 | custom fusion | bytes 266240 | tf_op jit(solution)/shard_map/gather | solution.py:267
  67.6 0.8 %copy.26 = f32[1024,32]{0,1:T(8,128)} copy(f32[1024,32]{1,0:T(8,128)S(1)} %gather_fusion.1) | data formatting | bytes 262144 | tf_op jit(solution)/shard_map/gather | solution.py:267
  68.5 3.6 %far_grad.1 = (f32[2,4096]{1,0:T(2,128)}, f32[1,4096]{1,0:T(1,128)}) custom-call(f32[2,4096]{1,0:T(2,128)} %near.3.part_ref, f32[32,1024]{1,0:T(8,128)} %bitcast.49, f32[2,16,16,1024]{3,2,1,0:T(8,128)} %bitcast.36, f32[2,16,4096]{2,1,0:T(8,128)} %bitcast.42, f32[2,4096]{1,0:T(2,128)} %bitcast.52), custom_call_target="tpu_custom_call" | custom-call | flops 4194304 | bytes 2867200 | tf_op jit(solution)/shard_map/far_grad/pallas_call | solution.py:254
  72.0 2.8 %collective-permute-start.2 = (f32[4096]{0:T(1024)}, f32[4096]{0:T(1024)S(1)}, u32[]{:S(2)}, u32[]{:S(2)}) collective-permute-start(f32[4096]{0:T(1024)} %bitcast.58), channel_id=1, source_target_pairs={{0,3},{1,0},{2,1},{3,2},{4,7},{5,4},{6,5},{7,6},{8,11},{9,8},{10,9... | collective-permute-start | bytes 49160 | tf_op jit(solution)/shard_map/ppermute | solution.py:357
  74.8 0.8 collective-permute-start.1
  75.6 0.9 %collective-permute-start = (f32[4096]{0:T(1024)}, f32[4096]{0:T(1024)S(1)}, u32[]{:S(2)}, u32[]{:S(2)}) collective-permute-start(f32[4096]{0:T(1024)} %bitcast.60), channel_id=1, source_target_pairs={{0,1},{1,2},{2,3},{3,0},{4,5},{5,6},{6,7},{7,4},{8,9},{9,10},{10,1... | collective-permute-start | bytes 49160 | tf_op jit(solution)/shard_map/ppermute | solution.py:357
  76.5 0.0 collective-permute-done.2
  76.5 3.8 %collective-permute-done.1 = f32[4096]{0:T(1024)S(1)} collective-permute-done((f32[4096]{0:T(1024)}, f32[4096]{0:T(1024)S(1)}, u32[]{:S(2)}, u32[]{:S(2)}) %collective-permute-start.1) | collective-permute-done | bytes 16416 | tf_op jit(solution)/shard_map/ppermute | solution.py:357
  80.2 0.5 collective-permute-done
  80.7 0.8 pad_maximum_fusion
  81.5 0.7 dynamic-slice_add_fusion
  (5 shorter events, 0.1 us)
Async XLA Ops:
  3.8 29.4 %all-to-all-start = ((f32[64,1,2176]{2,1,0:T(1,128)}), f32[64,1,2176]{2,1,0:T(1,128)S(1)}, u32[]{:S(2)}, u32[]{:S(2)}) async-start(f32[64,1,2176]{2,1,0:T(1,128)} %bitcast.43), calls=%async_computation | async-start | bytes 1114112 | tf_op jit(solution)/shard_map/all_to_all | solution.py:272
  21.6 8.7 %copy-start.1 = (s32[1024,1]{0,1:T(1,128)S(1)}, s32[1024,1]{0,1:T(1,128)}, u32[]{:S(2)}) copy-start(s32[1024,1]{0,1:T(1,128)} %param.18) | copy-start | bytes 12292
  21.6 8.7 %copy-start = (s32[1024]{0:T(1024)S(1)}, s32[1024]{0:T(1024)}, u32[]{:S(2)}) copy-start(s32[1024]{0:T(1024)} %param.19) | copy-start | bytes 12292
  39.8 12.6 %copy-start.2 = (s32[1,1024]{1,0:T(1,128)S(1)}, s32[1,1024]{1,0:T(1,128)}, u32[]{:S(2)}) copy-start(s32[1,1024]{1,0:T(1,128)} %get-tuple-element.11) | copy-start | bytes 12292
  44.9 19.0 %all-to-all-start.1 = ((f32[64,1,1024]{2,1,0:T(1,128)}), f32[64,1,1024]{2,1,0:T(1,128)S(1)}, u32[]{:S(2)}, u32[]{:S(2)}) async-start(f32[64,1,1024]{2,1,0:T(1,128)} %bitcast.50), calls=%async_computation.1 | async-start | bytes 524288 | tf_op jit(solution)/shard_map/all_to_all | solution.py:265
  72.0 4.4 %collective-permute-start.2 = (f32[4096]{0:T(1024)}, f32[4096]{0:T(1024)S(1)}, u32[]{:S(2)}, u32[]{:S(2)}) collective-permute-start(f32[4096]{0:T(1024)} %bitcast.58), channel_id=1, source_target_pairs={{0,3},{1,0},{2,1},{3,2},{4,7},{5,4},{6,5},{7,6},{8,11},{9,8},{10,9... | collective-permute-start | bytes 49160 | tf_op jit(solution)/shard_map/ppermute | solution.py:357
  74.8 5.5 %collective-permute-start.1 = (f32[4096]{0:T(1024)}, f32[4096]{0:T(1024)S(1)}, u32[]{:S(2)}, u32[]{:S(2)}) collective-permute-start(f32[4096]{0:T(1024)} %bitcast.59), channel_id=1, source_target_pairs={{0,2},{1,3},{2,0},{3,1},{4,6},{5,7},{6,4},{7,5},{8,10},{9,11},{10,... | collective-permute-start | bytes 49160 | tf_op jit(solution)/shard_map/ppermute | solution.py:357
  75.6 5.2 %collective-permute-start = (f32[4096]{0:T(1024)}, f32[4096]{0:T(1024)S(1)}, u32[]{:S(2)}, u32[]{:S(2)}) collective-permute-start(f32[4096]{0:T(1024)} %bitcast.60), channel_id=1, source_target_pairs={{0,1},{1,2},{2,3},{3,0},{4,5},{5,6},{6,7},{7,4},{8,9},{9,10},{10,1... | collective-permute-start | bytes 49160 | tf_op jit(solution)/shard_map/ppermute | solution.py:357

commit v15 on v12

--- a/solution.py
+++ b/solution.py
@@ -350,15 +350,8 @@
             )
     freqs = lax.axis_size("freq")
     mine = terms[0]
-    got = [mine] + [
-        lax.ppermute(mine, "freq", [(i, (i + k) % freqs) for i in range(freqs)])
-        for k in range(1, freqs)
-    ]
-    stacked = jnp.stack(got)
-    f = lax.axis_index("freq")
-    total = stacked[(f - 0) % freqs]
-    for src in range(1, freqs):
-        total = total + stacked[(f - src) % freqs]
+    got = [lax.ppermute(mine, "freq", [(i, i ^ k) for i in range(freqs)]) for k in range(1, freqs)]
+    total = (mine + got[0]) + (got[1] + got[2])
     return (field[None], total)
 
 

time: 82.6 us -> 82 us (level)
  no operation moved by 1% of the time
where the time goes in v15:
time: 82 us; the launch traced here: 81.5 us
  Pallas kernels  29.7 us (36%)
  starting transfers between devices  23.2 us (28%)
  waiting for transfers between devices  13.9 us (17%)
  local copies, waits for them, and re-layouts  10 us (12%)
  other arithmetic  3.97 us (5%)
    pallas_call x5, Pallas kernels, _call(): pl.pallas_call(kernel, out_shape=outs, compiler_params=pltpu.CompilerPara...  29.7 us
    all_to_all x1, starting transfers between devices, _exchange_all(): got = lax.all_to_all(send.reshape(devices, total // devices), 'cells', 0, 0)  12.1 us
    all_to_all x1, waiting for transfers between devices, _exchange_all(): got = lax.all_to_all(send.reshape(devices, total // devices), 'cells', 0, 0)  7.04 us
    all_to_all x1, starting transfers between devices, _exchange(): got = lax.all_to_all(send.reshape(devices, total // devices), 'cells', 0, 0)  6.96 us
    ppermute x3, waiting for transfers between devices, per_device(): lax.ppermute(mine, 'freq', [(i, i ^ k) for i in range(freqs)])  4.12 us
    ppermute x3, starting transfers between devices, per_device(): lax.ppermute(mine, 'freq', [(i, i ^ k) for i in range(freqs)])  4.09 us
    gather x2, local copies, waits for them, and re-layouts, _exchange(): return got[idx].T  3.64 us
    gather x2, local copies, waits for them, and re-layouts, _exchange_all(): return (table.reshape(rank2, devices * clusters)[:, src_index], rr)  3.64 us
  transfers between devices with their start and end apart: 5, of which 4 were waited for; matrix products, arithmetic and copies ran while one was open for 2% of the time, Pallas kernels for 21%

profile of v15, /device:TPU:8, one launch (start us, length us, event | category | flops | bytes accessed | tf_op | source)
XLA Modules:
  0.0 81.5 jit_solution(11637682737737633393)
XLA Ops:
  0.6 3.1 %proj_pack.1 = (s32[1,1024]{1,0:T(1,128)}, f32[1088,128]{1,0:T(8,128)}) custom-call(f32[2,4096]{1,0:T(2,128)} %bitcast.36, f32[1,4096]{1,0:T(1,128)} %c_ref.7, f32[2,16,4096]{2,1,0:T(8,128)} %bitcast.31, s32[1,1024]{1,0:T(1,128)} %bitcast.46, s32[1,1024]{1,0:T(1,128)} %bitcast.45), custom_call_target="tpu_custom_call" | custom-call | flops 134742016 | bytes 1142784 | tf_op jit(solution)/shard_map/proj_pack/pallas_call | solution.py:251
  3.8 12.1 %all-to-all-start = ((f32[64,1,2176]{2,1,0:T(1,128)}), f32[64,1,2176]{2,1,0:T(1,128)S(1)}, u32[]{:S(2)}, u32[]{:S(2)}) async-start(f32[64,1,2176]{2,1,0:T(1,128)} %bitcast.35), calls=%async_computation | async-start | bytes 1114112 | tf_op jit(solution)/shard_map/all_to_all | solution.py:269
  15.9 0.7 subtract_bitcast_fusion
  16.6 0.1 broadcast_in_dim.10
  16.7 0.7 reshape.68.nlc_ref
  17.4 0.0 copy-start.1
  17.4 0.0 copy-start
  17.4 8.7 %near.2.part_ref = f32[2,4096]{1,0:T(2,128)} custom-call(f32[2,4096]{1,0:T(2,128)} %bitcast.37, f32[1,4096]{1,0:T(1,128)} %c_ref.7, f32[2,192,4096]{2,1,0:T(8,128)} %bitcast.25, s32[3,4096]{1,0:T(4,128)} %reshape.68.nlc_ref, f32[2,4096]{1,0:T(2,128)} %bitcast.38), custom_call_target="tpu_custom_call" | custom-call | flops 6291456 | bytes 6455296 | tf_op jit(solution)/shard_map/near/pallas_call | solution.py:251
  26.1 0.0 copy-done.1
  26.1 0.0 copy-done
  26.2 7.0 %all-to-all-done = f32[64,1,2176]{2,1,0:T(1,128)S(1)} async-done(((f32[64,1,2176]{2,1,0:T(1,128)}), f32[64,1,2176]{2,1,0:T(1,128)S(1)}, u32[]{:S(2)}, u32[]{:S(2)}) %all-to-all-start) | async-done | bytes 557088 | tf_op jit(solution)/shard_map/all_to_all | solution.py:269
  33.2 1.3 %reduce = f32[64,2176]{1,0:T(8,128)S(1)} reduce(f32[64,1,2176]{2,1,0:T(1,128)S(1)} %all-to-all-done, f32[]{:T(128)} %constant.22), dimensions={1}, to_apply=%all_to_all.13.reduce_sub_computation | reduce | bytes 1114116 | tf_op jit(solution)/shard_map/all_to_all | solution.py:269
  34.5 0.1 reshape.71
  34.6 0.6 slice.13
  35.3 0.2 reshape.72
  35.5 0.6 copy.19
  36.1 2.8 %gather_fusion = f32[1024,32]{1,0:T(8,128)S(1)} fusion(f32[32,4096]{0,1:T(8,128)S(1)} %bitcast.29, s32[1024]{0:T(1024)S(1)} %fusion), kind=kCustom, calls=%fused_computation | custom fusion | bytes 266240 | tf_op jit(solution)/shard_map/gather | solution.py:274
  38.9 0.8 %copy.20 = f32[1024,32]{0,1:T(8,128)} copy(f32[1024,32]{1,0:T(8,128)S(1)} %gather_fusion) | data formatting | bytes 262144 | tf_op jit(solution)/shard_map/gather | solution.py:274
  39.8 0.0 copy-start.2
  39.8 5.3 %far_proj.1 = (f32[2,4096]{1,0:T(2,128)}, f32[512,128]{1,0:T(8,128)}) custom-call(f32[2,4096]{1,0:T(2,128)} %near.2.part_ref, f32[32,1024]{1,0:T(8,128)} %bitcast.40, f32[2,16,16,1024]{3,2,1,0:T(8,128)} %bitcast.27, f32[2,16,4096]{2,1,0:T(8,128)} %bitcast.33, f32[1,4096]{1,0:T(1,128)} %c_ref.7, f32[2,16,4096]{2,1,0:T(8,128)} %bitcast.32, f32[64,32]{1,0:T(8,128)} %bitcast.43), custom_call_target="tpu_custom_call" | custom-call | flops 4194304 | bytes 3629056 | tf_op jit(solution)/shard_map/far_proj/pallas_call | solution.py:251
  45.1 7.0 %all-to-all-start.1 = ((f32[64,1,1024]{2,1,0:T(1,128)}), f32[64,1,1024]{2,1,0:T(1,128)S(1)}, u32[]{:S(2)}, u32[]{:S(2)}) async-start(f32[64,1,1024]{2,1,0:T(1,128)} %bitcast.42), calls=%async_computation.1 | async-start | bytes 524288 | tf_op jit(solution)/shard_map/all_to_all | solution.py:262
  52.1 0.0 copy-done.2
  52.1 8.7 %near.3.part_ref = f32[2,4096]{1,0:T(2,128)} custom-call(f32[2,4096]{1,0:T(2,128)} %get-tuple-element.9.u_ref, f32[1,4096]{1,0:T(1,128)} %c_ref.7, f32[2,192,4096]{2,1,0:T(8,128)} %bitcast.26, s32[3,4096]{1,0:T(4,128)} %reshape.68.nlc_ref, f32[2,4096]{1,0:T(2,128)} %bitcast.39), custom_call_target="tpu_custom_call" | custom-call | flops 6291456 | bytes 6455296 | tf_op jit(solution)/shard_map/near/pallas_call | solution.py:251
  60.8 2.8 %all-to-all-done.1 = f32[64,1,1024]{2,1,0:T(1,128)S(1)} async-done(((f32[64,1,1024]{2,1,0:T(1,128)}), f32[64,1,1024]{2,1,0:T(1,128)S(1)}, u32[]{:S(2)}, u32[]{:S(2)}) %all-to-all-start.1) | async-done | bytes 262176 | tf_op jit(solution)/shard_map/all_to_all | solution.py:262
  63.6 0.6 reduce.1
  64.2 0.3 reshape.74
  64.6 2.8 %gather_fusion.1 = f32[1024,32]{1,0:T(8,128)S(1)} fusion(f32[2048,32]{1,0:T(8,128)S(1)} %reshape.74, s32[1024]{0:T(1024)S(1)} %broadcast_clamp_fusion), kind=kCustom, calls=%fused_computation.1 | custom fusion | bytes 266240 | tf_op jit(solution)/shard_map/gather | solution.py:264
  67.4 0.8 %copy.23 = f32[1024,32]{0,1:T(8,128)} copy(f32[1024,32]{1,0:T(8,128)S(1)} %gather_fusion.1) | data formatting | bytes 262144 | tf_op jit(solution)/shard_map/gather | solution.py:264
  68.2 3.8 %far_grad.1 = (f32[2,4096]{1,0:T(2,128)}, f32[1,4096]{1,0:T(1,128)}) custom-call(f32[2,4096]{1,0:T(2,128)} %near.3.part_ref, f32[32,1024]{1,0:T(8,128)} %bitcast.41, f32[2,16,16,1024]{3,2,1,0:T(8,128)} %bitcast.28, f32[2,16,4096]{2,1,0:T(8,128)} %bitcast.34, f32[2,4096]{1,0:T(2,128)} %bitcast.44), custom_call_target="tpu_custom_call" | custom-call | flops 4194304 | bytes 2867200 | tf_op jit(solution)/shard_map/far_grad/pallas_call | solution.py:251
  72.0 2.8 %collective-permute-start.2 = (f32[4096]{0:T(1024)}, f32[4096]{0:T(1024)S(1)}, u32[]{:S(2)}, u32[]{:S(2)}) collective-permute-start(f32[4096]{0:T(1024)} %bitcast.47), channel_id=1, source_target_pairs={{0,3},{1,2},{2,1},{3,0},{4,7},{5,6},{6,5},{7,4},{8,11},{9,10},{10,... | collective-permute-start | bytes 49160 | tf_op jit(solution)/shard_map/ppermute | solution.py:353
  74.8 0.8 collective-permute-start.1
  75.5 0.5 collective-permute-start
  76.1 1.1 %collective-permute-done.2 = f32[4096]{0:T(1024)S(1)} collective-permute-done((f32[4096]{0:T(1024)}, f32[4096]{0:T(1024)S(1)}, u32[]{:S(2)}, u32[]{:S(2)}) %collective-permute-start.2) | collective-permute-done | bytes 16416 | tf_op jit(solution)/shard_map/ppermute | solution.py:353
  77.2 3.1 %collective-permute-done.1 = f32[4096]{0:T(1024)S(1)} collective-permute-done((f32[4096]{0:T(1024)}, f32[4096]{0:T(1024)S(1)}, u32[]{:S(2)}, u32[]{:S(2)}) %collective-permute-start.1) | collective-permute-done | bytes 16416 | tf_op jit(solution)/shard_map/ppermute | solution.py:353
  80.2 0.0 collective-permute-done
  80.2 1.3 %add_add_fusion = f32[4096]{0:T(1024)} fusion(f32[4096]{0:T(1024)S(1)} %collective-permute-done.1, f32[4096]{0:T(1024)S(1)} %collective-permute-done.2, f32[4096]{0:T(1024)} %bitcast.50, f32[4096]{0:T(1024)S(1)} %collective-permute-done), kind=kLoop, calls=%fused_computation.3 | loop fusion | flops 12288 | bytes 81920 | tf_op jit(solution)/shard_map/add | solution.py:354
  (5 shorter events, 0.1 us)
Async XLA Ops:
  3.8 29.4 %all-to-all-start = ((f32[64,1,2176]{2,1,0:T(1,128)}), f32[64,1,2176]{2,1,0:T(1,128)S(1)}, u32[]{:S(2)}, u32[]{:S(2)}) async-start(f32[64,1,2176]{2,1,0:T(1,128)} %bitcast.35), calls=%async_computation | async-start | bytes 1114112 | tf_op jit(solution)/shard_map/all_to_all | solution.py:269
  17.4 8.7 %copy-start.1 = (s32[1024,1]{0,1:T(1,128)S(1)}, s32[1024,1]{0,1:T(1,128)}, u32[]{:S(2)}) copy-start(s32[1024,1]{0,1:T(1,128)} %param.18) | copy-start | bytes 12292
  17.4 8.7 %copy-start = (s32[1024]{0:T(1024)S(1)}, s32[1024]{0:T(1024)}, u32[]{:S(2)}) copy-start(s32[1024]{0:T(1024)} %param.19) | copy-start | bytes 12292
  39.8 12.3 %copy-start.2 = (s32[1,1024]{1,0:T(1,128)S(1)}, s32[1,1024]{1,0:T(1,128)}, u32[]{:S(2)}) copy-start(s32[1,1024]{1,0:T(1,128)} %get-tuple-element.11) | copy-start | bytes 12292
  45.1 18.5 %all-to-all-start.1 = ((f32[64,1,1024]{2,1,0:T(1,128)}), f32[64,1,1024]{2,1,0:T(1,128)S(1)}, u32[]{:S(2)}, u32[]{:S(2)}) async-start(f32[64,1,1024]{2,1,0:T(1,128)} %bitcast.42), calls=%async_computation.1 | async-start | bytes 524288 | tf_op jit(solution)/shard_map/all_to_all | solution.py:262
  72.0 5.2 %collective-permute-start.2 = (f32[4096]{0:T(1024)}, f32[4096]{0:T(1024)S(1)}, u32[]{:S(2)}, u32[]{:S(2)}) collective-permute-start(f32[4096]{0:T(1024)} %bitcast.47), channel_id=1, source_target_pairs={{0,3},{1,2},{2,1},{3,0},{4,7},{5,6},{6,5},{7,4},{8,11},{9,10},{10,... | collective-permute-start | bytes 49160 | tf_op jit(solution)/shard_map/ppermute | solution.py:353
  74.8 5.5 %collective-permute-start.1 = (f32[4096]{0:T(1024)}, f32[4096]{0:T(1024)S(1)}, u32[]{:S(2)}, u32[]{:S(2)}) collective-permute-start(f32[4096]{0:T(1024)} %bitcast.48), channel_id=1, source_target_pairs={{0,2},{1,3},{2,0},{3,1},{4,6},{5,7},{6,4},{7,5},{8,10},{9,11},{10,... | collective-permute-start | bytes 49160 | tf_op jit(solution)/shard_map/ppermute | solution.py:353
  75.5 4.7 %collective-permute-start = (f32[4096]{0:T(1024)}, f32[4096]{0:T(1024)S(1)}, u32[]{:S(2)}, u32[]{:S(2)}) collective-permute-start(f32[4096]{0:T(1024)} %bitcast.49), channel_id=1, source_target_pairs={{0,1},{1,0},{2,3},{3,2},{4,5},{5,4},{6,7},{7,6},{8,9},{9,8},{10,11... | collective-permute-start | bytes 49160 | tf_op jit(solution)/shard_map/ppermute | solution.py:353
